TPU v7x, 32 devices: a whole 2x2x4 slice. The times are simulated.
32 devices in a mesh: grp: 4 (over y, x), dev: 8 (over z, core).
Axes of the slice: x: 2, y: 2, z: 4, core: 2. Of those that a mesh axis runs over, the one named last changes fastest.
Arguments:
- load_vector: bfloat16 [4, 8, 2, 48, 2304], P('grp', 'dev'), may hold values from -6 to 6
- transform: float32 [4, 8, 2, 48, 48], P('grp', 'dev'), may hold values from -0.875 to 0.875
- diagonal: float32 [4, 8, 2, 48], P('grp', 'dev'), may hold values from 0.05 to 4
- scaling: float32 [4, 8, 2, 3], P('grp', 'dev'), may hold values from 0.5 to 2
- live_count: int32 [4, 8], replicated, may hold values from 1 to 2
- coarse_inverse: float32 [4, 8, 6, 48], P('grp', 'dev'), may hold values from -48 to 48, as said below
Outputs:
- multiplier: float32 [4, 8, 2, 3, 2304], P('grp', 'dev')
- residual: float32 [4, 8, 2, 3, 2304], P('grp', 'dev')
Inputs may be any that keep to these rules, and one draw needn't show every extreme that they name: Read as 4 matrices of order 48, coarse_inverse is symmetric and positive definite in every group.
All inputs are finite; a program needn't handle non-finite values.
Results may differ from a plain program's by a relative error of at most 0.00055.
Values sent between devices are 32-bit elements; how exact they have to be, the bound alone decides.
No kernel may reach another device: no remote copies, remote signals or barrier semaphores. Data moves between devices by JAX's collectives and lax.ppermute only.
A program may use at most 64 MiB of HBM per device.

v0:
```python
import jax
import jax.numpy as jnp
from jax import lax
from jax.sharding import PartitionSpec as P

PRECISE = lax.Precision.HIGHEST


def shifted(block, axis, distance):
    devices = range(lax.axis_size(axis))
    route = [((i - distance) % len(devices), i) for i in devices]
    return lax.ppermute(block, axis, route)


def inverse_diagonal(diagonal):
    return 1.0 / (diagonal[:, None, None] + diagonal[None, :, None] + diagonal[None, None, :])


def spectral(patch_load, transform):
    points = transform.shape[0]
    spatial = patch_load.astype(jnp.float32).reshape(points, points, points)
    moved = jnp.einsum("ai,abc->ibc", transform, spatial, precision=PRECISE)
    moved = jnp.einsum("bj,ibc->ijc", transform, moved, precision=PRECISE)
    return jnp.einsum("ck,ijc->ijk", transform, moved, precision=PRECISE)


def face_spectrum(transform, low_side, high_side):
    points = transform.shape[0]
    planes = jnp.stack([low_side, high_side]).reshape(2, 3, points, points)
    hats = jnp.einsum("bj,edbc,ck->edjk", transform, planes, transform, precision=PRECISE)
    low_row = transform[0]
    high_row = transform[points - 1]
    result = low_row[:, None, None] * hats[0, 0][None] + high_row[:, None, None] * hats[1, 0][None]
    result = (
        result
        + low_row[None, :, None] * hats[0, 1][:, None, :]
        + high_row[None, :, None] * hats[1, 1][:, None, :]
    )
    result = (
        result
        + low_row[None, None, :] * hats[0, 2][:, :, None]
        + high_row[None, None, :] * hats[1, 2][:, :, None]
    )
    return result


def trace_solved(transform, solved):
    points = transform.shape[0]
    end_rows = jnp.stack([transform[0], transform[points - 1]])
    along_a = jnp.sum(end_rows[:, :, None, None] * solved[None], axis=1)
    along_b = jnp.sum(end_rows[:, None, :, None] * solved[None], axis=2)
    along_c = jnp.sum(end_rows[:, None, None, :] * solved[None], axis=3)
    planes = jnp.stack([along_a, along_b, along_c], axis=1)
    traces = jnp.einsum("bj,edjk,ck->edbc", transform, planes, transform, precision=PRECISE)
    return traces.reshape(2, 3, points * points)


def setup_one(patch_load, one_transform, one_inverse):
    return trace_solved(one_transform, one_inverse * spectral(patch_load, one_transform))


def apply_one(one_transform, one_inverse, low_side, high_side):
    return trace_solved(
        one_transform, one_inverse * face_spectrum(one_transform, low_side, high_side)
    )


def slot_before(vector):
    return jnp.concatenate([jnp.zeros_like(vector[:1]), vector[:-1]], axis=0)


def slot_after(vector):
    return jnp.concatenate([vector[1:], jnp.zeros_like(vector[:1])], axis=0)


def on_device(load_vector, transform, diagonal, scaling, live_count, coarse_inverse):
    patch_loads = load_vector[0, 0]
    transforms = transform[0, 0]
    diagonals = diagonal[0, 0]
    weights = scaling[0, 0]
    coarse_rows = coarse_inverse[0, 0]
    slot_count = patch_loads.shape[0]
    coarse_size = coarse_rows.shape[-1]
    group_index = lax.axis_index("grp")
    owner_index = lax.axis_index("dev")
    groups = lax.axis_size("grp")
    owners = lax.axis_size("dev")
    prev_owner = (owner_index + owners - 1) % owners
    prev_group = (group_index + groups - 1) % groups

    rows = coarse_rows.reshape(slot_count, 3, coarse_size)
    extra_owner = jnp.concatenate([rows[:, 0], weights[:, 0:1]], axis=1)
    extra_group = jnp.concatenate([rows[:, 1], weights[:, 1:2]], axis=1)

    slot_index = jnp.arange(slot_count, dtype=jnp.int32)
    in_use = slot_index[None, None, :] < live_count[:, :, None]
    nothing = jnp.zeros_like(in_use[:, :, :1])
    alive = jnp.stack(
        [
            in_use & jnp.roll(in_use, -1, axis=1),
            in_use & jnp.roll(in_use, -1, axis=0),
            in_use & jnp.concatenate([in_use[:, :, 1:], nothing], axis=2),
        ],
        axis=-1,
    ).astype(jnp.float32)
    live_own = alive[group_index, owner_index]
    live_in = jnp.stack(
        [alive[group_index, prev_owner, :, 0], alive[prev_group, owner_index, :, 1]], axis=1
    )

    inverses = jax.vmap(inverse_diagonal)(diagonals)
    solver = jax.vmap(apply_one)

    def gather_all(payload):
        count = groups * owners
        spread = jnp.broadcast_to(payload[None], (count,) + payload.shape)
        got = lax.all_to_all(spread, ("grp", "dev"), 0, 0, tiled=True)
        return got.reshape(groups, owners, -1)

    def face_means(traces):
        return jnp.mean(traces, axis=-1).reshape(-1)

    def interface_means(raw):
        raw = raw.reshape(groups, owners, slot_count, 2, 3)
        low = raw[:, :, :, 0]
        high = raw[:, :, :, 1]
        following = jnp.stack(
            [
                jnp.roll(low[..., 0], -1, axis=1),
                jnp.roll(low[..., 1], -1, axis=0),
                jnp.concatenate([low[:, :, 1:, 2], jnp.zeros_like(low[:, :, :1, 2])], axis=2),
            ],
            axis=-1,
        )
        return (alive * (high - following)).reshape(groups, coarse_size)

    def coarse(means):
        here = means[group_index]
        before = means[prev_group]
        own = jnp.dot(coarse_rows, here, precision=PRECISE).reshape(slot_count, 3)
        first = jnp.dot(rows_in[:, 0], here, precision=PRECISE)
        second = jnp.dot(rows_in[:, 1], before, precision=PRECISE)
        return own, jnp.stack([first, second], axis=1)

    def jumps(traces_now, both, extra=None):
        low_side = traces_now[:, 0]
        high_side = traces_now[:, 1]
        low_next_owner = shifted(low_side[:, 0], "dev", -1)
        low_next_group = shifted(low_side[:, 1], "grp", -1)
        following = jnp.stack(
            [low_next_owner, low_next_group, slot_after(low_side[:, 2])], axis=1
        )
        own = live_own[..., None] * (high_side - following)
        if not both:
            return own
        face_size = high_side.shape[-1]
        high_prev_owner = shifted(
            jnp.concatenate([high_side[:, 0], extra[0]], axis=1), "dev", 1
        )
        high_prev_group = shifted(
            jnp.concatenate([high_side[:, 1], extra[1]], axis=1), "grp", 1
        )
        leading = jnp.stack(
            [high_prev_owner[:, :face_size], high_prev_group[:, :face_size]], axis=1
        )
        incoming = live_in[..., None] * (leading - low_side[:, :2])
        return own, incoming, (high_prev_owner[:, face_size:], high_prev_group[:, face_size:])

    def solve(v_own, v_in):
        preceding = jnp.stack([v_in[:, 0], v_in[:, 1], slot_before(v_own[:, 2])], axis=1)
        return solver(transforms, inverses, -preceding, v_own)

    def split_dot(v_own, v_in, traces_now):
        low_side = traces_now[:, 0]
        high_side = traces_now[:, 1]
        inner = live_own[:, 2, None] * (high_side[:, 2] - slot_after(low_side[:, 2]))
        first = jnp.sum(live_own[:, :2, None] * v_own[:, :2] * high_side[:, :2])
        second = jnp.sum(live_in[..., None] * v_in * low_side[:, :2])
        return first - second + jnp.sum(v_own[:, 2] * inner)

    def precondition(res_own, res_in, c_own, c_in):
        z_own = weights[..., None] * res_own + live_own[..., None] * c_own[..., None]
        z_in = weights_in[..., None] * res_in + live_in[..., None] * c_in[..., None]
        return z_own, z_in

    start_traces = jax.vmap(setup_one)(patch_loads, transforms, inverses)
    gathered = gather_all(face_means(start_traces))
    res_own, res_in, received = jumps(start_traces, True, (extra_owner, extra_group))
    rows_in = jnp.stack([received[0][:, :coarse_size], received[1][:, :coarse_size]], axis=1)
    weights_in = jnp.stack([received[0][:, coarse_size], received[1][:, coarse_size]], axis=1)
    c_own, c_in = coarse(interface_means(gathered))
    dir_own, dir_in = precondition(res_own, res_in, c_own, c_in)
    rz_part = jnp.sum(res_own * dir_own)

    traces_one = solve(dir_own, dir_in)
    dq_part = split_dot(dir_own, dir_in, traces_one)
    gathered = gather_all(
        jnp.concatenate([face_means(traces_one), jnp.stack([rz_part, dq_part])])
    )
    img_own, img_in, _ = jumps(traces_one, True, (extra_owner[:, :0], extra_group[:, :0]))
    totals = jnp.sum(gathered[:, :, slot_count * 6 :], axis=(0, 1))
    product = totals[0]
    curve = totals[1]
    step_len = product / curve
    cq_own, cq_in = coarse(interface_means(gathered[:, :, : slot_count * 6]))
    multiplier = step_len * dir_own
    res_own = res_own - step_len * img_own
    res_in = res_in - step_len * img_in
    z_own, z_in = precondition(
        res_own, res_in, c_own - step_len * cq_own, c_in - step_len * cq_in
    )
    new_part = jnp.sum(res_own * z_own)
    zq_part = jnp.sum(z_own * img_own)

    traces_two = solve(z_own, z_in)
    zfz_part = split_dot(z_own, z_in, traces_two)
    dfz_part = split_dot(dir_own, dir_in, traces_two)
    gathered = gather_all(jnp.stack([new_part, zq_part, zfz_part, dfz_part]))
    fz_own = jumps(traces_two, False)
    totals = jnp.sum(gathered, axis=(0, 1))
    new_product = totals[0]
    ratio = new_product / product
    curve_two = totals[2] + ratio * (totals[1] + totals[3]) + ratio * ratio * curve
    step_two = new_product / curve_two
    direction = z_own + ratio * dir_own
    applied = fz_own + ratio * img_own
    multiplier = multiplier + step_two * direction
    residual = res_own - step_two * applied
    return (multiplier[None, None], residual[None, None])


def solution(mesh):
    return jax.shard_map(
        on_device,
        mesh=mesh,
        in_specs=(
            P("grp", "dev", None, None, None),
            P("grp", "dev", None, None, None),
            P("grp", "dev", None, None),
            P("grp", "dev", None, None),
            P(),
            P("grp", "dev", None, None),
        ),
        out_specs=(P("grp", "dev", None, None, None), P("grp", "dev", None, None, None)),
        check_vma=False,
    )
```

profile of v0, /device:TPU:0, one launch (start us, length us, event | category | flops | bytes accessed | tf_op | source)
XLA Modules:
  0.0 103.9 jit_solution(16113003315557445853)
XLA Ops:
  1.5 2.7 %reshape.804 = bf16[2,48,48,48]{3,2,1,0:T(8,128)(2,1)S(1)} reshape(bf16[1,1,2,48,2304]{4,3,2,1,0:T(8,128)(2,1)} %param.6) | data formatting | bytes 884736 | tf_op jit(solution)/shard_map/vmap()/reshape | solution.py:21
  4.1 1.9 %fusion.7 = f32[2,48,48,48]{3,1,2,0:T(8,128)S(1)} fusion(bf16[2,48,48,48]{3,2,1,0:T(8,128)(2,1)S(1)} %reshape.804, f32[1,1,2,48,48]{4,3,2,1,0:T(8,128)} %param.7), kind=kOutput, calls=%fused_computation.17 | convolution fusion | flops 127401984 | bytes 1345536 | tf_op jit(solution)/shard_map/vmap(ai,abc->ibc)/dot_general | solution.py:22
  6.1 4.1 %fusion.2 = f32[2,48,48,48]{3,2,1,0:T(8,128)S(1)} fusion(f32[2,48,48,48]{3,1,2,0:T(8,128)S(1)} %fusion.7, f32[1,1,2,48,48]{4,3,2,1,0:T(8,128)S(1)} %copy-done), kind=kOutput, calls=%fused_computation.11 | convolution fusion | flops 127401984 | bytes 1787904 | tf_op jit(solution)/shard_map/vmap(bj,ibc->ijc)/dot_general | solution.py:23
  10.3 4.3 %fusion.4 = f32[2,48,48,48]{3,2,1,0:T(8,128)S(1)} fusion(f32[2,48,48,48]{3,2,1,0:T(8,128)S(1)} %fusion.2, f32[2,48]{1,0:T(2,128)S(1)} %bitcast.412, f32[2,48,48]{2,1,0:T(8,128)S(1)} %broadcast_add_fusion, f32[1,1,2,48,48]{4,3,2,1,0:T(8,128)S(1)} %copy-done), kind=kOutput, calls=%fused_computation.16 | convolution fusion | flops 128065536 | bytes 1806720 | tf_op jit(solution)/shard_map/vmap(ck,ijc->ijk)/dot_general | solution.py:24
  14.7 2.5 %multiply_reduce_fusion.8 = (f32[2,2,48,48]{3,2,1,0:T(8,128)S(1)}, f32[2,2,48,48]{3,2,1,0:T(8,128)S(1)}, f32[2,2,48,48]{3,2,1,0:T(8,128)S(1)}) fusion(f32[2,48,48,48]{3,2,1,0:T(8,128)S(1)} %fusion.4, f32[2,2,48]{2,1,0:T(2,128)S(1)} %copy.342), kind=kLoop, calls=%fused_computation.8 | loop fusion | flops 2626560 | bytes 996096 | tf_op jit(solution)/shard_map/vmap()/reduce_sum | solution.py:50
  17.4 1.1 %fusion.9 = f32[2,2,3,48,48]{3,4,2,1,0:T(8,128)S(1)} fusion(f32[2,2,1,48,48]{3,4,2,1,0:T(8,128)S(1)} %bitcast.371, f32[2,2,1,48,48]{3,4,2,1,0:T(8,128)S(1)} %bitcast.368, f32[2,2,1,48,48]{3,4,2,1,0:T(8,128)S(1)} %bitcast.365, f32[1,1,2,48,48]{4,3,2,1,0:T(8,128)S(1)} %copy-done), kind=kOutput, calls=%fused_computation.23 | convolution fusion | flops 15980544 | bytes 239616 | tf_op jit(solution)/shard_map/vmap(bj,edjk,ck->edbc)/dot_general | solution.py:54
  19.8 7.3 %all-to-all-start = ((f32[32,1,12]{2,1,0:T(1,128)}), f32[32,1,12]{2,1,0:T(1,128)S(1)}, u32[]{:S(2)}, u32[]{:S(2)}) async-start(f32[32,1,12]{2,1,0:T(1,128)} %broadcast_in_dim.6), calls=%async_computation | async-start | bytes 32768 | tf_op jit(solution)/shard_map/all_to_all | solution.py:117
  27.4 3.4 %collective-permute-start.2 = (f32[2,2304]{1,0:T(2,128)S(1)}, f32[2,2304]{1,0:T(2,128)S(1)}, u32[]{:S(2)}, u32[]{:S(2)}) collective-permute-start(f32[2,2304]{1,0:T(2,128)S(1)} %get-tuple-element.74), channel_id=1, source_target_pairs={{1,0},{2,1},{3,2},{4,3},{5,4},{6,5},{7,6},{0,7},{9,8},{10,9},{11,1... | collective-permute-start | bytes 55304 | tf_op jit(solution)/shard_map/ppermute | solution.py:12
  30.8 2.4 %collective-permute-start.3 = (f32[2,2304]{1,0:T(2,128)S(1)}, f32[2,2304]{1,0:T(2,128)S(1)}, u32[]{:S(2)}, u32[]{:S(2)}) collective-permute-start(f32[2,2304]{1,0:T(2,128)S(1)} %get-tuple-element.75), channel_id=1, source_target_pairs={{8,0},{16,8},{24,16},{0,24},{9,1},{17,9},{25,17},{1,25},{10,2},{18... | collective-permute-start | bytes 55304 | tf_op jit(solution)/shard_map/ppermute | solution.py:12
  38.2 3.8 %collective-permute-done = f32[2,2353]{1,0:T(2,128)S(1)} collective-permute-done((f32[2,2353]{1,0:T(2,128)S(1)}, f32[2,2353]{1,0:T(2,128)S(1)}, u32[]{:S(2)}, u32[]{:S(2)}) %collective-permute-start) | collective-permute-done | bytes 18856 | tf_op jit(solution)/shard_map/ppermute | solution.py:12
  43.8 2.3 %add_multiply_fusion.1 = f32[2,48,48,48]{3,2,1,0:T(8,128)S(1)} fusion(f32[2,48,48]{2,1,0:T(8,128)S(1)} %get-tuple-element.53, f32[2,48]{1,0:T(2,128)S(1)} %bitcast.402, f32[2,48,48]{2,1,0:T(8,128)S(1)} %get-tuple-element.54, f32[2,48]{1,0:T(2,128)S(1)} %bitcast.399, f32[2,48,48]{2,1,0:T(8,128)S(1)} %get-tuple-element.55, ...), kind=kLoop, calls=%fused_computation.14 | loop fusion | flops 3096576 | bytes 1014912 | tf_op jit(solution)/shard_map/vmap()/mul | solution.py:64
  46.1 2.3 %multiply_reduce_fusion.5 = (f32[2,2,48,48]{3,2,1,0:T(8,128)S(1)}, f32[2,2,48,48]{3,2,1,0:T(8,128)S(1)}, f32[2,2,48,48]{3,2,1,0:T(8,128)S(1)}) fusion(f32[2,48,48,48]{3,2,1,0:T(8,128)S(1)} %add_multiply_fusion.1, f32[2,2,48]{2,1,0:T(2,128)S(1)} %copy.342), kind=kLoop, calls=%fused_computation.5 | loop fusion | flops 2626560 | bytes 996096 | tf_op jit(solution)/shard_map/vmap()/reduce_sum | solution.py:50
  56.3 2.8 %all-to-all-start.1 = ((f32[32,1,14]{2,1,0:T(1,128)}), f32[32,1,14]{2,1,0:T(1,128)S(1)}, u32[]{:S(2)}, u32[]{:S(2)}) async-start(f32[32,1,14]{2,1,0:T(1,128)} %broadcast_in_dim.7), calls=%async_computation.1 | async-start | bytes 32768 | tf_op jit(solution)/shard_map/all_to_all | solution.py:117
  59.4 1.7 %collective-permute-start.7 = (f32[2,2304]{1,0:T(2,128)S(1)}, f32[2,2304]{1,0:T(2,128)S(1)}, u32[]{:S(2)}, u32[]{:S(2)}) collective-permute-start(f32[2,2304]{1,0:T(2,128)S(1)} %get-tuple-element.69), channel_id=1, source_target_pairs={{24,0},{0,8},{8,16},{16,24},{25,1},{1,9},{9,17},{17,25},{26,2},{2,... | collective-permute-start | bytes 55304 | tf_op jit(solution)/shard_map/ppermute | solution.py:12
  61.1 3.1 %collective-permute-start.4 = (f32[2,2304]{1,0:T(2,128)S(1)}, f32[2,2304]{1,0:T(2,128)S(1)}, u32[]{:S(2)}, u32[]{:S(2)}) collective-permute-start(f32[2,2304]{1,0:T(2,128)S(1)} %get-tuple-element.70), channel_id=1, source_target_pairs={{1,0},{2,1},{3,2},{4,3},{5,4},{6,5},{7,6},{0,7},{9,8},{10,9},{11,1... | collective-permute-start | bytes 55304 | tf_op jit(solution)/shard_map/ppermute | solution.py:12
  64.2 1.2 %collective-permute-start.5 = (f32[2,2304]{1,0:T(2,128)S(1)}, f32[2,2304]{1,0:T(2,128)S(1)}, u32[]{:S(2)}, u32[]{:S(2)}) collective-permute-start(f32[2,2304]{1,0:T(2,128)S(1)} %get-tuple-element.71), channel_id=1, source_target_pairs={{8,0},{16,8},{24,16},{0,24},{9,1},{17,9},{25,17},{1,25},{10,2},{18... | collective-permute-start | bytes 55304 | tf_op jit(solution)/shard_map/ppermute | solution.py:12
  72.1 2.5 %add_multiply_fusion = f32[2,48,48,48]{3,2,1,0:T(8,128)S(1)} fusion(f32[2,48,48]{2,1,0:T(8,128)S(1)} %get-tuple-element.47, f32[2,48,48]{2,1,0:T(8,128)S(1)} %get-tuple-element.48, f32[2,48,48]{2,1,0:T(8,128)S(1)} %get-tuple-element.49, f32[2,48,48]{2,1,0:T(8,128)S(1)} %get-tuple-element.50, f32[2,48,48]{2,1,0:T(8,128)S(1)} %get-tuple-element.51, ...), kind=kLoop, calls=%fused_computation.13 | loop fusion | flops 3096576 | bytes 1014912 | tf_op jit(solution)/shard_map/vmap()/mul | solution.py:64
  74.7 2.3 %multiply_reduce_fusion.2 = (f32[2,2,48,48]{3,2,1,0:T(8,128)S(1)}, f32[2,2,48,48]{3,2,1,0:T(8,128)S(1)}, f32[2,2,48,48]{3,2,1,0:T(8,128)S(1)}) fusion(f32[2,48,48,48]{3,2,1,0:T(8,128)S(1)} %add_multiply_fusion, f32[2,2,48]{2,1,0:T(2,128)S(1)} %copy.342), kind=kLoop, calls=%fused_computation.2 | loop fusion | flops 2626560 | bytes 996096 | tf_op jit(solution)/shard_map/vmap()/reduce_sum | solution.py:50
  77.2 1.1 %fusion.21 = f32[2,2,3,48,48]{3,4,2,1,0:T(8,128)S(1)} fusion(f32[2,2,1,48,48]{3,4,2,1,0:T(8,128)S(1)} %bitcast.373, f32[2,2,1,48,48]{3,4,2,1,0:T(8,128)S(1)} %bitcast.370, f32[2,2,1,48,48]{3,4,2,1,0:T(8,128)S(1)} %bitcast.367, f32[1,1,2,48,48]{4,3,2,1,0:T(8,128)S(1)} %copy-done), kind=kOutput, calls=%fused_computation.35 | convolution fusion | flops 15980544 | bytes 239616 | tf_op jit(solution)/shard_map/vmap(bj,edjk,ck->edbc)/dot_general | solution.py:54
  85.3 1.3 %pad_maximum_fusion.9 = f32[4]{0:T(128)S(1)} fusion(f32[1]{0:T(128)} %bitcast.133, f32[1]{0:T(128)} %bitcast.132, f32[1]{0:T(128)} %bitcast.98, f32[1]{0:T(128)} %bitcast.97), kind=kLoop, calls=%fused_computation.230 | loop fusion | flops 12 | bytes 32 | tf_op jit(solution)/shard_map/stack | solution.py:218
  87.2 2.5 %all-to-all-start.2 = ((f32[32,1,4]{2,1,0:T(1,128)}), f32[32,1,4]{2,1,0:T(1,128)S(1)}, u32[]{:S(2)}, u32[]{:S(2)}) async-start(f32[32,1,4]{2,1,0:T(1,128)} %broadcast_in_dim.8), calls=%async_computation.2 | async-start | bytes 32768 | tf_op jit(solution)/shard_map/all_to_all | solution.py:117
  89.7 3.4 %collective-permute-start.8 = (f32[2,2304]{1,0:T(2,128)S(1)}, f32[2,2304]{1,0:T(2,128)S(1)}, u32[]{:S(2)}, u32[]{:S(2)}) collective-permute-start(f32[2,2304]{1,0:T(2,128)S(1)} %get-tuple-element.66), channel_id=1, source_target_pairs={{1,0},{2,1},{3,2},{4,3},{5,4},{6,5},{7,6},{0,7},{9,8},{10,9},{11,1... | collective-permute-start | bytes 55304 | tf_op jit(solution)/shard_map/ppermute | solution.py:12
  93.1 2.4 %collective-permute-start.9 = (f32[2,2304]{1,0:T(2,128)S(1)}, f32[2,2304]{1,0:T(2,128)S(1)}, u32[]{:S(2)}, u32[]{:S(2)}) collective-permute-start(f32[2,2304]{1,0:T(2,128)S(1)} %get-tuple-element.67), channel_id=1, source_target_pairs={{8,0},{16,8},{24,16},{0,24},{9,1},{17,9},{25,17},{1,25},{10,2},{18... | collective-permute-start | bytes 55304 | tf_op jit(solution)/shard_map/ppermute | solution.py:12
  95.6 1.2 %all-to-all-done.2 = f32[32,1,4]{2,1,0:T(1,128)S(1)} async-done(((f32[32,1,4]{2,1,0:T(1,128)}), f32[32,1,4]{2,1,0:T(1,128)S(1)}, u32[]{:S(2)}, u32[]{:S(2)}) %all-to-all-start.2) | async-done | bytes 544 | tf_op jit(solution)/shard_map/all_to_all | solution.py:117
  (193 shorter events, 27.0 us)
Async XLA Ops:
  1.5 4.6 %copy-start = (f32[1,1,2,48,48]{4,3,2,1,0:T(8,128)S(1)}, f32[1,1,2,48,48]{4,3,2,1,0:T(8,128)}, u32[]{:S(2)}) copy-start(f32[1,1,2,48,48]{4,3,2,1,0:T(8,128)} %param.7) | copy-start | bytes 55300
  6.1 4.2 %copy-start.2 = (f32[1,1,2,48]{3,2,1,0:T(2,128)S(1)}, f32[1,1,2,48]{3,2,1,0:T(2,128)}, u32[]{:S(2)}) copy-start(f32[1,1,2,48]{3,2,1,0:T(2,128)} %param.8) | copy-start | bytes 1156
  14.6 18.6 %copy-start.1 = (s32[4,8]{1,0:T(4,128)S(1)}, s32[4,8]{1,0:T(4,128)}, u32[]{:S(2)}) copy-start(s32[4,8]{1,0:T(4,128)} %param.10) | copy-start | bytes 388
  14.6 19.0 %copy-start.4 = (f32[1,1,6,48]{3,1,2,0:T(1,128)S(1)}, f32[1,1,6,48]{3,1,2,0:T(1,128)}, u32[]{:S(2)}) copy-start(f32[1,1,6,48]{3,1,2,0:T(1,128)} %param.11) | copy-start | bytes 3460
  14.7 19.0 %copy-start.3 = (f32[1,1,2,3]{3,2,1,0:T(2,128)S(1)}, f32[1,1,2,3]{3,2,1,0:T(2,128)}, u32[]{:S(2)}) copy-start(f32[1,1,2,3]{3,2,1,0:T(2,128)} %param.9) | copy-start | bytes 76
  19.8 15.1 %all-to-all-start = ((f32[32,1,12]{2,1,0:T(1,128)}), f32[32,1,12]{2,1,0:T(1,128)S(1)}, u32[]{:S(2)}, u32[]{:S(2)}) async-start(f32[32,1,12]{2,1,0:T(1,128)} %broadcast_in_dim.6), calls=%async_computation | async-start | bytes 32768 | tf_op jit(solution)/shard_map/all_to_all | solution.py:117
  27.4 8.7 %collective-permute-start.2 = (f32[2,2304]{1,0:T(2,128)S(1)}, f32[2,2304]{1,0:T(2,128)S(1)}, u32[]{:S(2)}, u32[]{:S(2)}) collective-permute-start(f32[2,2304]{1,0:T(2,128)S(1)} %get-tuple-element.74), channel_id=1, source_target_pairs={{1,0},{2,1},{3,2},{4,3},{5,4},{6,5},{7,6},{0,7},{9,8},{10,9},{11,1... | collective-permute-start | bytes 55304 | tf_op jit(solution)/shard_map/ppermute | solution.py:12
  30.8 5.3 %collective-permute-start.3 = (f32[2,2304]{1,0:T(2,128)S(1)}, f32[2,2304]{1,0:T(2,128)S(1)}, u32[]{:S(2)}, u32[]{:S(2)}) collective-permute-start(f32[2,2304]{1,0:T(2,128)S(1)} %get-tuple-element.75), channel_id=1, source_target_pairs={{8,0},{16,8},{24,16},{0,24},{9,1},{17,9},{25,17},{1,25},{10,2},{18... | collective-permute-start | bytes 55304 | tf_op jit(solution)/shard_map/ppermute | solution.py:12
  36.9 5.0 %collective-permute-start = (f32[2,2353]{1,0:T(2,128)S(1)}, f32[2,2353]{1,0:T(2,128)S(1)}, u32[]{:S(2)}, u32[]{:S(2)}) collective-permute-start(f32[2,2353]{1,0:T(2,128)S(1)} %concatenate.161), channel_id=1, source_target_pairs={{7,0},{0,1},{1,2},{2,3},{3,4},{4,5},{5,6},{6,7},{15,8},{8,9},{9,10... | collective-permute-start | bytes 56480 | tf_op jit(solution)/shard_map/ppermute | solution.py:12
  37.0 5.0 %collective-permute-start.1 = (f32[2,2353]{1,0:T(2,128)S(1)}, f32[2,2353]{1,0:T(2,128)S(1)}, u32[]{:S(2)}, u32[]{:S(2)}) collective-permute-start(f32[2,2353]{1,0:T(2,128)S(1)} %concatenate.162), channel_id=1, source_target_pairs={{24,0},{0,8},{8,16},{16,24},{25,1},{1,9},{9,17},{17,25},{26,2},{2,... | collective-permute-start | bytes 56480 | tf_op jit(solution)/shard_map/ppermute | solution.py:12
  56.3 9.9 %all-to-all-start.1 = ((f32[32,1,14]{2,1,0:T(1,128)}), f32[32,1,14]{2,1,0:T(1,128)S(1)}, u32[]{:S(2)}, u32[]{:S(2)}) async-start(f32[32,1,14]{2,1,0:T(1,128)} %broadcast_in_dim.7), calls=%async_computation.1 | async-start | bytes 32768 | tf_op jit(solution)/shard_map/all_to_all | solution.py:117
  59.1 11.6 %collective-permute-start.6 = (f32[2,2304]{1,0:T(2,128)S(1)}, f32[2,2304]{1,0:T(2,128)S(1)}, u32[]{:S(2)}, u32[]{:S(2)}) collective-permute-start(f32[2,2304]{1,0:T(2,128)S(1)} %get-tuple-element.68), channel_id=1, source_target_pairs={{7,0},{0,1},{1,2},{2,3},{3,4},{4,5},{5,6},{6,7},{15,8},{8,9},{9,10... | collective-permute-start | bytes 55304 | tf_op jit(solution)/shard_map/ppermute | solution.py:12
  59.4 11.3 %collective-permute-start.7 = (f32[2,2304]{1,0:T(2,128)S(1)}, f32[2,2304]{1,0:T(2,128)S(1)}, u32[]{:S(2)}, u32[]{:S(2)}) collective-permute-start(f32[2,2304]{1,0:T(2,128)S(1)} %get-tuple-element.69), channel_id=1, source_target_pairs={{24,0},{0,8},{8,16},{16,24},{25,1},{1,9},{9,17},{17,25},{26,2},{2,... | collective-permute-start | bytes 55304 | tf_op jit(solution)/shard_map/ppermute | solution.py:12
  61.1 8.7 %collective-permute-start.4 = (f32[2,2304]{1,0:T(2,128)S(1)}, f32[2,2304]{1,0:T(2,128)S(1)}, u32[]{:S(2)}, u32[]{:S(2)}) collective-permute-start(f32[2,2304]{1,0:T(2,128)S(1)} %get-tuple-element.70), channel_id=1, source_target_pairs={{1,0},{2,1},{3,2},{4,3},{5,4},{6,5},{7,6},{0,7},{9,8},{10,9},{11,1... | collective-permute-start | bytes 55304 | tf_op jit(solution)/shard_map/ppermute | solution.py:12
  64.2 5.6 %collective-permute-start.5 = (f32[2,2304]{1,0:T(2,128)S(1)}, f32[2,2304]{1,0:T(2,128)S(1)}, u32[]{:S(2)}, u32[]{:S(2)}) collective-permute-start(f32[2,2304]{1,0:T(2,128)S(1)} %get-tuple-element.71), channel_id=1, source_target_pairs={{8,0},{16,8},{24,16},{0,24},{9,1},{17,9},{25,17},{1,25},{10,2},{18... | collective-permute-start | bytes 55304 | tf_op jit(solution)/shard_map/ppermute | solution.py:12
  87.2 9.6 %all-to-all-start.2 = ((f32[32,1,4]{2,1,0:T(1,128)}), f32[32,1,4]{2,1,0:T(1,128)S(1)}, u32[]{:S(2)}, u32[]{:S(2)}) async-start(f32[32,1,4]{2,1,0:T(1,128)} %broadcast_in_dim.8), calls=%async_computation.2 | async-start | bytes 32768 | tf_op jit(solution)/shard_map/all_to_all | solution.py:117
  89.7 12.2 %collective-permute-start.8 = (f32[2,2304]{1,0:T(2,128)S(1)}, f32[2,2304]{1,0:T(2,128)S(1)}, u32[]{:S(2)}, u32[]{:S(2)}) collective-permute-start(f32[2,2304]{1,0:T(2,128)S(1)} %get-tuple-element.66), channel_id=1, source_target_pairs={{1,0},{2,1},{3,2},{4,3},{5,4},{6,5},{7,6},{0,7},{9,8},{10,9},{11,1... | collective-permute-start | bytes 55304 | tf_op jit(solution)/shard_map/ppermute | solution.py:12
  93.1 8.8 %collective-permute-start.9 = (f32[2,2304]{1,0:T(2,128)S(1)}, f32[2,2304]{1,0:T(2,128)S(1)}, u32[]{:S(2)}, u32[]{:S(2)}) collective-permute-start(f32[2,2304]{1,0:T(2,128)S(1)} %get-tuple-element.67), channel_id=1, source_target_pairs={{8,0},{16,8},{24,16},{0,24},{9,1},{17,9},{25,17},{1,25},{10,2},{18... | collective-permute-start | bytes 55304 | tf_op jit(solution)/shard_map/ppermute | solution.py:12
where the time goes:
time: 104 us
  starting transfers between devices  31.4 us (30%)
  other arithmetic  22.8 us (22%)
  matrix products  17.7 us (17%)
  between operations  13.2 us (13%)
  local copies, waits for them, and re-layouts  13 us (12%)
  waiting for transfers between devices  5.8 us (6%)
    ppermute x10, starting transfers between devices, shifted(): return lax.ppermute(block, axis, route)  18.8 us
    all_to_all x3, starting transfers between devices, gather_all(): got = lax.all_to_all(spread, ('grp', 'dev'), 0, 0, tiled=True)  12.6 us
    reduce_sum x3, other arithmetic, trace_solved(): along_a = jnp.sum(end_rows[:, :, None, None] * solved[None], axis=1)  7.11 us
    mul x2, other arithmetic, apply_one(): one_inverse * face_spectrum(one_transform, low_side, high_side)  4.8 us
    dot_general x6, matrix products, trace_solved(): jnp.einsum('bj,edjk,ck->edbc', transform, planes, transform, precision=PR...  4.75 us
    dot_general x1, matrix products, spectral(): return jnp.einsum('ck,ijc->ijk', transform, moved, precision=PRECISE)  4.35 us
    dot_general x1, matrix products, spectral(): moved = jnp.einsum('bj,ibc->ijc', transform, moved, precision=PRECISE)  4.12 us
    ppermute x10, waiting for transfers between devices, shifted(): return lax.ppermute(block, axis, route)  3.79 us
  transfers between devices with their start and end apart: 13, of which 3 were waited for; matrix products, arithmetic and copies ran while one was open for 7% of the time, Pallas kernels for 0%

commit v1 on v0

--- a/solution.py
+++ b/solution.py
@@ -170,13 +170,20 @@
         preceding = jnp.stack([v_in[:, 0], v_in[:, 1], slot_before(v_own[:, 2])], axis=1)
         return solver(transforms, inverses, -preceding, v_own)
 
-    def split_dot(v_own, v_in, traces_now):
+    def split_terms(v_own, v_in, traces_now):
         low_side = traces_now[:, 0]
         high_side = traces_now[:, 1]
-        inner = live_own[:, 2, None] * (high_side[:, 2] - slot_after(low_side[:, 2]))
-        first = jnp.sum(live_own[:, :2, None] * v_own[:, :2] * high_side[:, :2])
-        second = jnp.sum(live_in[..., None] * v_in * low_side[:, :2])
-        return first - second + jnp.sum(v_own[:, 2] * inner)
+        second = jnp.concatenate(
+            [
+                live_in[..., None] * v_in * low_side[:, :2],
+                (live_own[:, 2, None] * v_own[:, 2] * slot_after(low_side[:, 2]))[:, None],
+            ],
+            axis=1,
+        )
+        return live_own[..., None] * v_own * high_side - second
+
+    def partial_sums(terms):
+        return jnp.sum(jnp.stack(terms), axis=(1, 2, 3))
 
     def precondition(res_own, res_in, c_own, c_in):
         z_own = weights[..., None] * res_own + live_own[..., None] * c_own[..., None]
@@ -190,38 +197,39 @@
     weights_in = jnp.stack([received[0][:, coarse_size], received[1][:, coarse_size]], axis=1)
     c_own, c_in = coarse(interface_means(gathered))
     dir_own, dir_in = precondition(res_own, res_in, c_own, c_in)
-    rz_part = jnp.sum(res_own * dir_own)
-
     traces_one = solve(dir_own, dir_in)
-    dq_part = split_dot(dir_own, dir_in, traces_one)
-    gathered = gather_all(
-        jnp.concatenate([face_means(traces_one), jnp.stack([rz_part, dq_part])])
-    )
+    parts = partial_sums([res_own * dir_own, split_terms(dir_own, dir_in, traces_one)])
+    gathered = gather_all(jnp.concatenate([face_means(traces_one), parts]))
     img_own, img_in, _ = jumps(traces_one, True, (extra_owner[:, :0], extra_group[:, :0]))
     totals = jnp.sum(gathered[:, :, slot_count * 6 :], axis=(0, 1))
-    product = totals[0]
-    curve = totals[1]
-    step_len = product / curve
+    product = totals[0:1]
+    curve = totals[1:2]
+    step_len = (product / curve)[:, None, None]
     cq_own, cq_in = coarse(interface_means(gathered[:, :, : slot_count * 6]))
     multiplier = step_len * dir_own
     res_own = res_own - step_len * img_own
     res_in = res_in - step_len * img_in
     z_own, z_in = precondition(
-        res_own, res_in, c_own - step_len * cq_own, c_in - step_len * cq_in
-    )
-    new_part = jnp.sum(res_own * z_own)
-    zq_part = jnp.sum(z_own * img_own)
+        res_own, res_in, c_own - step_len[0] * cq_own, c_in - step_len[0] * cq_in
+    )
 
     traces_two = solve(z_own, z_in)
-    zfz_part = split_dot(z_own, z_in, traces_two)
-    dfz_part = split_dot(dir_own, dir_in, traces_two)
-    gathered = gather_all(jnp.stack([new_part, zq_part, zfz_part, dfz_part]))
+    parts = partial_sums(
+        [
+            res_own * z_own,
+            z_own * img_own,
+            split_terms(z_own, z_in, traces_two),
+            split_terms(dir_own, dir_in, traces_two),
+        ]
+    )
+    gathered = gather_all(parts)
     fz_own = jumps(traces_two, False)
     totals = jnp.sum(gathered, axis=(0, 1))
-    new_product = totals[0]
+    new_product = totals[0:1]
     ratio = new_product / product
-    curve_two = totals[2] + ratio * (totals[1] + totals[3]) + ratio * ratio * curve
-    step_two = new_product / curve_two
+    curve_two = totals[2:3] + ratio * (totals[1:2] + totals[3:4]) + ratio * ratio * curve
+    step_two = (new_product / curve_two)[:, None, None]
+    ratio = ratio[:, None, None]
     direction = z_own + ratio * dir_own
     applied = fz_own + ratio * img_own
     multiplier = multiplier + step_two * direction

time: 104 us -> 91.6 us (0.88)
  other arithmetic: 22.8 us -> 16.1 us
  between operations: 13.2 us -> 7.25 us
    reduce_sum x7 -> x2, other arithmetic: 5.28 us -> 0.38 us  [partial_sums(): return jnp.sum(jnp.stack(terms), axis=(1, 2, 3))]
    another operation x1 -> x0, other arithmetic: 1.28 us -> none  [on_device(): gathered = gather_all(jnp.stack([new_part, zq_part, zfz_part, dfz_part]))]
where the time goes in v1:
time: 91.6 us; the launch traced here: 91.2 us
  starting transfers between devices  31.6 us (34%)
  matrix products  17.7 us (19%)
  other arithmetic  16.1 us (18%)
  local copies, waits for them, and re-layouts  12.9 us (14%)
  between operations  7.25 us (8%)
  waiting for transfers between devices  5.72 us (6%)
    ppermute x10, starting transfers between devices, shifted(): return lax.ppermute(block, axis, route)  18.9 us
    all_to_all x3, starting transfers between devices, gather_all(): got = lax.all_to_all(spread, ('grp', 'dev'), 0, 0, tiled=True)  12.7 us
    reduce_sum x3, other arithmetic, trace_solved(): along_a = jnp.sum(end_rows[:, :, None, None] * solved[None], axis=1)  7.11 us
    mul x2, other arithmetic, apply_one(): one_inverse * face_spectrum(one_transform, low_side, high_side)  4.82 us
    dot_general x6, matrix products, trace_solved(): jnp.einsum('bj,edjk,ck->edbc', transform, planes, transform, precision=PR...  4.75 us
    dot_general x1, matrix products, spectral(): return jnp.einsum('ck,ijc->ijk', transform, moved, precision=PRECISE)  4.35 us
    dot_general x1, matrix products, spectral(): moved = jnp.einsum('bj,ibc->ijc', transform, moved, precision=PRECISE)  4.12 us
    ppermute x10, waiting for transfers between devices, shifted(): return lax.ppermute(block, axis, route)  3.72 us
  transfers between devices with their start and end apart: 13, of which 3 were waited for; matrix products, arithmetic and copies ran while one was open for 7% of the time, Pallas kernels for 0%

profile of v1, /device:TPU:0, one launch (start us, length us, event | category | flops | bytes accessed | tf_op | source)
XLA Modules:
  0.0 91.2 jit_solution(6199082547558076990)
XLA Ops:
  1.5 2.7 %reshape.1193 = bf16[2,48,48,48]{3,2,1,0:T(8,128)(2,1)S(1)} reshape(bf16[1,1,2,48,2304]{4,3,2,1,0:T(8,128)(2,1)} %param.6) | data formatting | bytes 884736 | tf_op jit(solution)/shard_map/vmap()/reshape | solution.py:21
  4.1 1.9 %fusion.7 = f32[2,48,48,48]{3,1,2,0:T(8,128)S(1)} fusion(bf16[2,48,48,48]{3,2,1,0:T(8,128)(2,1)S(1)} %reshape.1193, f32[1,1,2,48,48]{4,3,2,1,0:T(8,128)} %param.7), kind=kOutput, calls=%fused_computation.17 | convolution fusion | flops 127401984 | bytes 1345536 | tf_op jit(solution)/shard_map/vmap(ai,abc->ibc)/dot_general | solution.py:22
  6.1 4.1 %fusion.2 = f32[2,48,48,48]{3,2,1,0:T(8,128)S(1)} fusion(f32[2,48,48,48]{3,1,2,0:T(8,128)S(1)} %fusion.7, f32[1,1,2,48,48]{4,3,2,1,0:T(8,128)S(1)} %copy-done), kind=kOutput, calls=%fused_computation.11 | convolution fusion | flops 127401984 | bytes 1787904 | tf_op jit(solution)/shard_map/vmap(bj,ibc->ijc)/dot_general | solution.py:23
  10.3 4.3 %fusion.4 = f32[2,48,48,48]{3,2,1,0:T(8,128)S(1)} fusion(f32[2,48,48,48]{3,2,1,0:T(8,128)S(1)} %fusion.2, f32[2,48]{1,0:T(2,128)S(1)} %bitcast.406, f32[2,48,48]{2,1,0:T(8,128)S(1)} %broadcast_add_fusion, f32[1,1,2,48,48]{4,3,2,1,0:T(8,128)S(1)} %copy-done), kind=kOutput, calls=%fused_computation.16 | convolution fusion | flops 128065536 | bytes 1806720 | tf_op jit(solution)/shard_map/vmap(ck,ijc->ijk)/dot_general | solution.py:24
  14.7 2.5 %multiply_reduce_fusion.8 = (f32[2,2,48,48]{3,2,1,0:T(8,128)S(1)}, f32[2,2,48,48]{3,2,1,0:T(8,128)S(1)}, f32[2,2,48,48]{3,2,1,0:T(8,128)S(1)}) fusion(f32[2,48,48,48]{3,2,1,0:T(8,128)S(1)} %fusion.4, f32[2,2,48]{2,1,0:T(2,128)S(1)} %copy.336), kind=kLoop, calls=%fused_computation.8 | loop fusion | flops 2626560 | bytes 996096 | tf_op jit(solution)/shard_map/vmap()/reduce_sum | solution.py:50
  17.4 1.1 %fusion.9 = f32[2,2,3,48,48]{3,4,2,1,0:T(8,128)S(1)} fusion(f32[2,2,1,48,48]{3,4,2,1,0:T(8,128)S(1)} %bitcast.364, f32[2,2,1,48,48]{3,4,2,1,0:T(8,128)S(1)} %bitcast.361, f32[2,2,1,48,48]{3,4,2,1,0:T(8,128)S(1)} %bitcast.358, f32[1,1,2,48,48]{4,3,2,1,0:T(8,128)S(1)} %copy-done), kind=kOutput, calls=%fused_computation.23 | convolution fusion | flops 15980544 | bytes 239616 | tf_op jit(solution)/shard_map/vmap(bj,edjk,ck->edbc)/dot_general | solution.py:54
  19.8 7.3 %all-to-all-start = ((f32[32,1,12]{2,1,0:T(1,128)}), f32[32,1,12]{2,1,0:T(1,128)S(1)}, u32[]{:S(2)}, u32[]{:S(2)}) async-start(f32[32,1,12]{2,1,0:T(1,128)} %broadcast_in_dim.6), calls=%async_computation | async-start | bytes 32768 | tf_op jit(solution)/shard_map/all_to_all | solution.py:117
  27.4 3.4 %collective-permute-start.2 = (f32[2,2304]{1,0:T(2,128)S(1)}, f32[2,2304]{1,0:T(2,128)S(1)}, u32[]{:S(2)}, u32[]{:S(2)}) collective-permute-start(f32[2,2304]{1,0:T(2,128)S(1)} %get-tuple-element.72), channel_id=1, source_target_pairs={{1,0},{2,1},{3,2},{4,3},{5,4},{6,5},{7,6},{0,7},{9,8},{10,9},{11,1... | collective-permute-start | bytes 55304 | tf_op jit(solution)/shard_map/ppermute | solution.py:12
  30.8 2.4 %collective-permute-start.3 = (f32[2,2304]{1,0:T(2,128)S(1)}, f32[2,2304]{1,0:T(2,128)S(1)}, u32[]{:S(2)}, u32[]{:S(2)}) collective-permute-start(f32[2,2304]{1,0:T(2,128)S(1)} %get-tuple-element.73), channel_id=1, source_target_pairs={{8,0},{16,8},{24,16},{0,24},{9,1},{17,9},{25,17},{1,25},{10,2},{18... | collective-permute-start | bytes 55304 | tf_op jit(solution)/shard_map/ppermute | solution.py:12
  37.5 3.7 %collective-permute-done = f32[2,2353]{1,0:T(2,128)S(1)} collective-permute-done((f32[2,2353]{1,0:T(2,128)S(1)}, f32[2,2353]{1,0:T(2,128)S(1)}, u32[]{:S(2)}, u32[]{:S(2)}) %collective-permute-start) | collective-permute-done | bytes 18856 | tf_op jit(solution)/shard_map/ppermute | solution.py:12
  43.1 2.3 %add_multiply_fusion.1 = f32[2,48,48,48]{3,2,1,0:T(8,128)S(1)} fusion(f32[2,48,48]{2,1,0:T(8,128)S(1)} %get-tuple-element.46, f32[2,48]{1,0:T(2,128)S(1)} %bitcast.397, f32[2,48,48]{2,1,0:T(8,128)S(1)} %get-tuple-element.47, f32[2,48]{1,0:T(2,128)S(1)} %bitcast.394, f32[2,48,48]{2,1,0:T(8,128)S(1)} %get-tuple-element.48, ...), kind=kLoop, calls=%fused_computation.14 | loop fusion | flops 3096576 | bytes 1014912 | tf_op jit(solution)/shard_map/vmap()/mul | solution.py:64
  45.5 2.3 %multiply_reduce_fusion.5 = (f32[2,2,48,48]{3,2,1,0:T(8,128)S(1)}, f32[2,2,48,48]{3,2,1,0:T(8,128)S(1)}, f32[2,2,48,48]{3,2,1,0:T(8,128)S(1)}) fusion(f32[2,48,48,48]{3,2,1,0:T(8,128)S(1)} %add_multiply_fusion.1, f32[2,2,48]{2,1,0:T(2,128)S(1)} %copy.336), kind=kLoop, calls=%fused_computation.5 | loop fusion | flops 2626560 | bytes 996096 | tf_op jit(solution)/shard_map/vmap()/reduce_sum | solution.py:50
  48.0 1.1 %fusion.15 = f32[2,2,3,48,48]{3,4,2,1,0:T(8,128)S(1)} fusion(f32[2,2,1,48,48]{3,4,2,1,0:T(8,128)S(1)} %bitcast.365, f32[2,2,1,48,48]{3,4,2,1,0:T(8,128)S(1)} %bitcast.362, f32[2,2,1,48,48]{3,4,2,1,0:T(8,128)S(1)} %bitcast.359, f32[1,1,2,48,48]{4,3,2,1,0:T(8,128)S(1)} %copy-done), kind=kOutput, calls=%fused_computation.29 | convolution fusion | flops 15980544 | bytes 239616 | tf_op jit(solution)/shard_map/vmap(bj,edjk,ck->edbc)/dot_general | solution.py:54
  51.3 2.9 %all-to-all-start.1 = ((f32[32,1,14]{2,1,0:T(1,128)}), f32[32,1,14]{2,1,0:T(1,128)S(1)}, u32[]{:S(2)}, u32[]{:S(2)}) async-start(f32[32,1,14]{2,1,0:T(1,128)} %broadcast_in_dim.7), calls=%async_computation.1 | async-start | bytes 32768 | tf_op jit(solution)/shard_map/all_to_all | solution.py:117
  54.5 1.7 %collective-permute-start.7 = (f32[2,2304]{1,0:T(2,128)S(1)}, f32[2,2304]{1,0:T(2,128)S(1)}, u32[]{:S(2)}, u32[]{:S(2)}) collective-permute-start(f32[2,2304]{1,0:T(2,128)S(1)} %get-tuple-element.67), channel_id=1, source_target_pairs={{24,0},{0,8},{8,16},{16,24},{25,1},{1,9},{9,17},{17,25},{26,2},{2,... | collective-permute-start | bytes 55304 | tf_op jit(solution)/shard_map/ppermute | solution.py:12
  56.1 3.1 %collective-permute-start.4 = (f32[2,2304]{1,0:T(2,128)S(1)}, f32[2,2304]{1,0:T(2,128)S(1)}, u32[]{:S(2)}, u32[]{:S(2)}) collective-permute-start(f32[2,2304]{1,0:T(2,128)S(1)} %get-tuple-element.68), channel_id=1, source_target_pairs={{1,0},{2,1},{3,2},{4,3},{5,4},{6,5},{7,6},{0,7},{9,8},{10,9},{11,1... | collective-permute-start | bytes 55304 | tf_op jit(solution)/shard_map/ppermute | solution.py:12
  59.2 1.2 %collective-permute-start.5 = (f32[2,2304]{1,0:T(2,128)S(1)}, f32[2,2304]{1,0:T(2,128)S(1)}, u32[]{:S(2)}, u32[]{:S(2)}) collective-permute-start(f32[2,2304]{1,0:T(2,128)S(1)} %get-tuple-element.69), channel_id=1, source_target_pairs={{8,0},{16,8},{24,16},{0,24},{9,1},{17,9},{25,17},{1,25},{10,2},{18... | collective-permute-start | bytes 55304 | tf_op jit(solution)/shard_map/ppermute | solution.py:12
  66.3 2.5 %add_multiply_fusion = f32[2,48,48,48]{3,2,1,0:T(8,128)S(1)} fusion(f32[2,48,48]{2,1,0:T(8,128)S(1)} %get-tuple-element.40, f32[2,48,48]{2,1,0:T(8,128)S(1)} %get-tuple-element.41, f32[2,48,48]{2,1,0:T(8,128)S(1)} %get-tuple-element.42, f32[2,48,48]{2,1,0:T(8,128)S(1)} %get-tuple-element.43, f32[2,48,48]{2,1,0:T(8,128)S(1)} %get-tuple-element.44, ...), kind=kLoop, calls=%fused_computation.13 | loop fusion | flops 3096576 | bytes 1014912 | tf_op jit(solution)/shard_map/vmap()/mul | solution.py:64
  68.8 2.3 %multiply_reduce_fusion.2 = (f32[2,2,48,48]{3,2,1,0:T(8,128)S(1)}, f32[2,2,48,48]{3,2,1,0:T(8,128)S(1)}, f32[2,2,48,48]{3,2,1,0:T(8,128)S(1)}) fusion(f32[2,48,48,48]{3,2,1,0:T(8,128)S(1)} %add_multiply_fusion, f32[2,2,48]{2,1,0:T(2,128)S(1)} %copy.336), kind=kLoop, calls=%fused_computation.2 | loop fusion | flops 2626560 | bytes 996096 | tf_op jit(solution)/shard_map/vmap()/reduce_sum | solution.py:50
  71.4 1.1 %fusion.21 = f32[2,2,3,48,48]{3,4,2,1,0:T(8,128)S(1)} fusion(f32[2,2,1,48,48]{3,4,2,1,0:T(8,128)S(1)} %bitcast.366, f32[2,2,1,48,48]{3,4,2,1,0:T(8,128)S(1)} %bitcast.363, f32[2,2,1,48,48]{3,4,2,1,0:T(8,128)S(1)} %bitcast.360, f32[1,1,2,48,48]{4,3,2,1,0:T(8,128)S(1)} %copy-done), kind=kOutput, calls=%fused_computation.35 | convolution fusion | flops 15980544 | bytes 239616 | tf_op jit(solution)/shard_map/vmap(bj,edjk,ck->edbc)/dot_general | solution.py:54
  74.5 2.5 %all-to-all-start.2 = ((f32[32,1,4]{2,1,0:T(1,128)}), f32[32,1,4]{2,1,0:T(1,128)S(1)}, u32[]{:S(2)}, u32[]{:S(2)}) async-start(f32[32,1,4]{2,1,0:T(1,128)} %broadcast_in_dim.8), calls=%async_computation.2 | async-start | bytes 32768 | tf_op jit(solution)/shard_map/all_to_all | solution.py:117
  77.1 3.4 %collective-permute-start.8 = (f32[2,2304]{1,0:T(2,128)S(1)}, f32[2,2304]{1,0:T(2,128)S(1)}, u32[]{:S(2)}, u32[]{:S(2)}) collective-permute-start(f32[2,2304]{1,0:T(2,128)S(1)} %get-tuple-element.64), channel_id=1, source_target_pairs={{1,0},{2,1},{3,2},{4,3},{5,4},{6,5},{7,6},{0,7},{9,8},{10,9},{11,1... | collective-permute-start | bytes 55304 | tf_op jit(solution)/shard_map/ppermute | solution.py:12
  80.5 2.4 %collective-permute-start.9 = (f32[2,2304]{1,0:T(2,128)S(1)}, f32[2,2304]{1,0:T(2,128)S(1)}, u32[]{:S(2)}, u32[]{:S(2)}) collective-permute-start(f32[2,2304]{1,0:T(2,128)S(1)} %get-tuple-element.65), channel_id=1, source_target_pairs={{8,0},{16,8},{24,16},{0,24},{9,1},{17,9},{25,17},{1,25},{10,2},{18... | collective-permute-start | bytes 55304 | tf_op jit(solution)/shard_map/ppermute | solution.py:12
  83.0 1.2 %all-to-all-done.2 = f32[32,1,4]{2,1,0:T(1,128)S(1)} async-done(((f32[32,1,4]{2,1,0:T(1,128)}), f32[32,1,4]{2,1,0:T(1,128)S(1)}, u32[]{:S(2)}, u32[]{:S(2)}) %all-to-all-start.2) | async-done | bytes 544 | tf_op jit(solution)/shard_map/all_to_all | solution.py:117
  (190 shorter events, 20.4 us)
Async XLA Ops:
  1.5 4.6 %copy-start = (f32[1,1,2,48,48]{4,3,2,1,0:T(8,128)S(1)}, f32[1,1,2,48,48]{4,3,2,1,0:T(8,128)}, u32[]{:S(2)}) copy-start(f32[1,1,2,48,48]{4,3,2,1,0:T(8,128)} %param.7) | copy-start | bytes 55300
  6.1 4.2 %copy-start.2 = (f32[1,1,2,48]{3,2,1,0:T(2,128)S(1)}, f32[1,1,2,48]{3,2,1,0:T(2,128)}, u32[]{:S(2)}) copy-start(f32[1,1,2,48]{3,2,1,0:T(2,128)} %param.8) | copy-start | bytes 1156
  14.6 18.6 %copy-start.1 = (s32[4,8]{1,0:T(4,128)S(1)}, s32[4,8]{1,0:T(4,128)}, u32[]{:S(2)}) copy-start(s32[4,8]{1,0:T(4,128)} %param.10) | copy-start | bytes 388
  14.6 19.0 %copy-start.4 = (f32[1,1,6,48]{3,1,2,0:T(1,128)S(1)}, f32[1,1,6,48]{3,1,2,0:T(1,128)}, u32[]{:S(2)}) copy-start(f32[1,1,6,48]{3,1,2,0:T(1,128)} %param.11) | copy-start | bytes 3460
  14.7 19.0 %copy-start.3 = (f32[1,1,2,3]{3,2,1,0:T(2,128)S(1)}, f32[1,1,2,3]{3,2,1,0:T(2,128)}, u32[]{:S(2)}) copy-start(f32[1,1,2,3]{3,2,1,0:T(2,128)} %param.9) | copy-start | bytes 76
  19.8 15.0 %all-to-all-start = ((f32[32,1,12]{2,1,0:T(1,128)}), f32[32,1,12]{2,1,0:T(1,128)S(1)}, u32[]{:S(2)}, u32[]{:S(2)}) async-start(f32[32,1,12]{2,1,0:T(1,128)} %broadcast_in_dim.6), calls=%async_computation | async-start | bytes 32768 | tf_op jit(solution)/shard_map/all_to_all | solution.py:117
  27.4 8.6 %collective-permute-start.2 = (f32[2,2304]{1,0:T(2,128)S(1)}, f32[2,2304]{1,0:T(2,128)S(1)}, u32[]{:S(2)}, u32[]{:S(2)}) collective-permute-start(f32[2,2304]{1,0:T(2,128)S(1)} %get-tuple-element.72), channel_id=1, source_target_pairs={{1,0},{2,1},{3,2},{4,3},{5,4},{6,5},{7,6},{0,7},{9,8},{10,9},{11,1... | collective-permute-start | bytes 55304 | tf_op jit(solution)/shard_map/ppermute | solution.py:12
  30.8 5.2 %collective-permute-start.3 = (f32[2,2304]{1,0:T(2,128)S(1)}, f32[2,2304]{1,0:T(2,128)S(1)}, u32[]{:S(2)}, u32[]{:S(2)}) collective-permute-start(f32[2,2304]{1,0:T(2,128)S(1)} %get-tuple-element.73), channel_id=1, source_target_pairs={{8,0},{16,8},{24,16},{0,24},{9,1},{17,9},{25,17},{1,25},{10,2},{18... | collective-permute-start | bytes 55304 | tf_op jit(solution)/shard_map/ppermute | solution.py:12
  36.2 5.0 %collective-permute-start = (f32[2,2353]{1,0:T(2,128)S(1)}, f32[2,2353]{1,0:T(2,128)S(1)}, u32[]{:S(2)}, u32[]{:S(2)}) collective-permute-start(f32[2,2353]{1,0:T(2,128)S(1)} %concatenate.239), channel_id=1, source_target_pairs={{7,0},{0,1},{1,2},{2,3},{3,4},{4,5},{5,6},{6,7},{15,8},{8,9},{9,10... | collective-permute-start | bytes 56480 | tf_op jit(solution)/shard_map/ppermute | solution.py:12
  36.3 5.0 %collective-permute-start.1 = (f32[2,2353]{1,0:T(2,128)S(1)}, f32[2,2353]{1,0:T(2,128)S(1)}, u32[]{:S(2)}, u32[]{:S(2)}) collective-permute-start(f32[2,2353]{1,0:T(2,128)S(1)} %concatenate.240), channel_id=1, source_target_pairs={{24,0},{0,8},{8,16},{16,24},{25,1},{1,9},{9,17},{17,25},{26,2},{2,... | collective-permute-start | bytes 56480 | tf_op jit(solution)/shard_map/ppermute | solution.py:12
  51.3 10.0 %all-to-all-start.1 = ((f32[32,1,14]{2,1,0:T(1,128)}), f32[32,1,14]{2,1,0:T(1,128)S(1)}, u32[]{:S(2)}, u32[]{:S(2)}) async-start(f32[32,1,14]{2,1,0:T(1,128)} %broadcast_in_dim.7), calls=%async_computation.1 | async-start | bytes 32768 | tf_op jit(solution)/shard_map/all_to_all | solution.py:117
  54.2 10.7 %collective-permute-start.6 = (f32[2,2304]{1,0:T(2,128)S(1)}, f32[2,2304]{1,0:T(2,128)S(1)}, u32[]{:S(2)}, u32[]{:S(2)}) collective-permute-start(f32[2,2304]{1,0:T(2,128)S(1)} %get-tuple-element.66), channel_id=1, source_target_pairs={{7,0},{0,1},{1,2},{2,3},{3,4},{4,5},{5,6},{6,7},{15,8},{8,9},{9,10... | collective-permute-start | bytes 55304 | tf_op jit(solution)/shard_map/ppermute | solution.py:12
  54.5 10.4 %collective-permute-start.7 = (f32[2,2304]{1,0:T(2,128)S(1)}, f32[2,2304]{1,0:T(2,128)S(1)}, u32[]{:S(2)}, u32[]{:S(2)}) collective-permute-start(f32[2,2304]{1,0:T(2,128)S(1)} %get-tuple-element.67), channel_id=1, source_target_pairs={{24,0},{0,8},{8,16},{16,24},{25,1},{1,9},{9,17},{17,25},{26,2},{2,... | collective-permute-start | bytes 55304 | tf_op jit(solution)/shard_map/ppermute | solution.py:12
  56.1 8.5 %collective-permute-start.4 = (f32[2,2304]{1,0:T(2,128)S(1)}, f32[2,2304]{1,0:T(2,128)S(1)}, u32[]{:S(2)}, u32[]{:S(2)}) collective-permute-start(f32[2,2304]{1,0:T(2,128)S(1)} %get-tuple-element.68), channel_id=1, source_target_pairs={{1,0},{2,1},{3,2},{4,3},{5,4},{6,5},{7,6},{0,7},{9,8},{10,9},{11,1... | collective-permute-start | bytes 55304 | tf_op jit(solution)/shard_map/ppermute | solution.py:12
  59.2 5.4 %collective-permute-start.5 = (f32[2,2304]{1,0:T(2,128)S(1)}, f32[2,2304]{1,0:T(2,128)S(1)}, u32[]{:S(2)}, u32[]{:S(2)}) collective-permute-start(f32[2,2304]{1,0:T(2,128)S(1)} %get-tuple-element.69), channel_id=1, source_target_pairs={{8,0},{16,8},{24,16},{0,24},{9,1},{17,9},{25,17},{1,25},{10,2},{18... | collective-permute-start | bytes 55304 | tf_op jit(solution)/shard_map/ppermute | solution.py:12
  74.5 9.6 %all-to-all-start.2 = ((f32[32,1,4]{2,1,0:T(1,128)}), f32[32,1,4]{2,1,0:T(1,128)S(1)}, u32[]{:S(2)}, u32[]{:S(2)}) async-start(f32[32,1,4]{2,1,0:T(1,128)} %broadcast_in_dim.8), calls=%async_computation.2 | async-start | bytes 32768 | tf_op jit(solution)/shard_map/all_to_all | solution.py:117
  77.1 12.1 %collective-permute-start.8 = (f32[2,2304]{1,0:T(2,128)S(1)}, f32[2,2304]{1,0:T(2,128)S(1)}, u32[]{:S(2)}, u32[]{:S(2)}) collective-permute-start(f32[2,2304]{1,0:T(2,128)S(1)} %get-tuple-element.64), channel_id=1, source_target_pairs={{1,0},{2,1},{3,2},{4,3},{5,4},{6,5},{7,6},{0,7},{9,8},{10,9},{11,1... | collective-permute-start | bytes 55304 | tf_op jit(solution)/shard_map/ppermute | solution.py:12
  80.5 8.7 %collective-permute-start.9 = (f32[2,2304]{1,0:T(2,128)S(1)}, f32[2,2304]{1,0:T(2,128)S(1)}, u32[]{:S(2)}, u32[]{:S(2)}) collective-permute-start(f32[2,2304]{1,0:T(2,128)S(1)} %get-tuple-element.65), channel_id=1, source_target_pairs={{8,0},{16,8},{24,16},{0,24},{9,1},{17,9},{25,17},{1,25},{10,2},{18... | collective-permute-start | bytes 55304 | tf_op jit(solution)/shard_map/ppermute | solution.py:12

commit v2 on v1

--- a/solution.py
+++ b/solution.py
@@ -4,6 +4,7 @@
 from jax.sharding import PartitionSpec as P
 
 PRECISE = lax.Precision.HIGHEST
+FAST = lax.Precision.HIGH
 
 
 def shifted(block, axis, distance):
@@ -19,15 +20,15 @@
 def spectral(patch_load, transform):
     points = transform.shape[0]
     spatial = patch_load.astype(jnp.float32).reshape(points, points, points)
-    moved = jnp.einsum("ai,abc->ibc", transform, spatial, precision=PRECISE)
-    moved = jnp.einsum("bj,ibc->ijc", transform, moved, precision=PRECISE)
-    return jnp.einsum("ck,ijc->ijk", transform, moved, precision=PRECISE)
+    moved = jnp.einsum("ai,abc->ibc", transform, spatial, precision=FAST)
+    moved = jnp.einsum("bj,ibc->ijc", transform, moved, precision=FAST)
+    return jnp.einsum("ck,ijc->ijk", transform, moved, precision=FAST)
 
 
 def face_spectrum(transform, low_side, high_side):
     points = transform.shape[0]
     planes = jnp.stack([low_side, high_side]).reshape(2, 3, points, points)
-    hats = jnp.einsum("bj,edbc,ck->edjk", transform, planes, transform, precision=PRECISE)
+    hats = jnp.einsum("bj,edbc,ck->edjk", transform, planes, transform, precision=FAST)
     low_row = transform[0]
     high_row = transform[points - 1]
     result = low_row[:, None, None] * hats[0, 0][None] + high_row[:, None, None] * hats[1, 0][None]
@@ -51,7 +52,7 @@
     along_b = jnp.sum(end_rows[:, None, :, None] * solved[None], axis=2)
     along_c = jnp.sum(end_rows[:, None, None, :] * solved[None], axis=3)
     planes = jnp.stack([along_a, along_b, along_c], axis=1)
-    traces = jnp.einsum("bj,edjk,ck->edbc", transform, planes, transform, precision=PRECISE)
+    traces = jnp.einsum("bj,edjk,ck->edbc", transform, planes, transform, precision=FAST)
     return traces.reshape(2, 3, points * points)
 
 

time: 91.6 us -> 85 us (0.928)
  matrix products: 17.7 us -> 11.3 us
    dot_general x13, matrix products: 16.8 us -> 10.4 us  [the longest x6 2.85 us: trace_solved(): jnp.einsum('bj,edjk,ck->edbc', transform, planes, transform, precision=FAST)]
where the time goes in v2:
time: 85 us; the launch traced here: 84.6 us
  starting transfers between devices  31.9 us (38%)
  other arithmetic  15.7 us (18%)
  local copies, waits for them, and re-layouts  12.9 us (15%)
  matrix products  11.3 us (13%)
  between operations  7.25 us (9%)
  waiting for transfers between devices  5.55 us (7%)
    ppermute x10, starting transfers between devices, shifted(): return lax.ppermute(block, axis, route)  19 us
    all_to_all x3, starting transfers between devices, gather_all(): got = lax.all_to_all(spread, ('grp', 'dev'), 0, 0, tiled=True)  12.9 us
    reduce_sum x3, other arithmetic, trace_solved(): along_a = jnp.sum(end_rows[:, :, None, None] * solved[None], axis=1)  6.94 us
    mul x2, other arithmetic, apply_one(): one_inverse * face_spectrum(one_transform, low_side, high_side)  4.6 us
    ppermute x10, waiting for transfers between devices, shifted(): return lax.ppermute(block, axis, route)  3.54 us
    dot_general x6, matrix products, trace_solved(): jnp.einsum('bj,edjk,ck->edbc', transform, planes, transform, precision=FAST)  2.85 us
    reshape x1, local copies, waits for them, and re-layouts, spectral(): spatial = patch_load.astype(jnp.float32).reshape(points, points, points)  2.66 us
    dot_general x1, matrix products, spectral(): return jnp.einsum('ck,ijc->ijk', transform, moved, precision=FAST)  2.59 us
  transfers between devices with their start and end apart: 13, of which 3 were waited for; matrix products, arithmetic and copies ran while one was open for 7% of the time, Pallas kernels for 0%

profile of v2, /device:TPU:0, one launch (start us, length us, event | category | flops | bytes accessed | tf_op | source)
XLA Modules:
  0.0 84.6 jit_solution(12113437319486252722)
XLA Ops:
  0.6 0.8 broadcast_add_fusion
  1.5 2.7 %reshape.1193 = bf16[2,48,48,48]{3,2,1,0:T(8,128)(2,1)S(1)} reshape(bf16[1,1,2,48,2304]{4,3,2,1,0:T(8,128)(2,1)} %param.6) | data formatting | bytes 884736 | tf_op jit(solution)/shard_map/vmap()/reshape | solution.py:22
  4.1 1.6 %fusion.7 = f32[2,48,48,48]{3,1,2,0:T(8,128)S(1)} fusion(bf16[2,48,48,48]{3,2,1,0:T(8,128)(2,1)S(1)} %reshape.1193, f32[1,1,2,48,48]{4,3,2,1,0:T(8,128)} %param.7), kind=kOutput, calls=%fused_computation.17 | convolution fusion | flops 63700992 | bytes 1345536 | tf_op jit(solution)/shard_map/vmap(ai,abc->ibc)/dot_general | solution.py:23
  5.8 2.2 %fusion.2 = f32[2,48,48,48]{3,2,1,0:T(8,128)S(1)} fusion(f32[2,48,48,48]{3,1,2,0:T(8,128)S(1)} %fusion.7, f32[1,1,2,48,48]{4,3,2,1,0:T(8,128)S(1)} %copy-done), kind=kOutput, calls=%fused_computation.11 | convolution fusion | flops 63700992 | bytes 1787904 | tf_op jit(solution)/shard_map/vmap(bj,ibc->ijc)/dot_general | solution.py:24
  8.1 2.6 %fusion.4 = f32[2,48,48,48]{3,2,1,0:T(8,128)S(1)} fusion(f32[2,48,48,48]{3,2,1,0:T(8,128)S(1)} %fusion.2, f32[2,48]{1,0:T(2,128)S(1)} %bitcast.406, f32[2,48,48]{2,1,0:T(8,128)S(1)} %broadcast_add_fusion, f32[1,1,2,48,48]{4,3,2,1,0:T(8,128)S(1)} %copy-done), kind=kOutput, calls=%fused_computation.16 | convolution fusion | flops 64364544 | bytes 1806720 | tf_op jit(solution)/shard_map/vmap(ck,ijc->ijk)/dot_general | solution.py:25
  10.7 2.3 %multiply_reduce_fusion.8 = (f32[2,2,48,48]{3,2,1,0:T(8,128)S(1)}, f32[2,2,48,48]{3,2,1,0:T(8,128)S(1)}, f32[2,2,48,48]{3,2,1,0:T(8,128)S(1)}) fusion(f32[2,48,48,48]{3,2,1,0:T(8,128)S(1)} %fusion.4, f32[2,2,48]{2,1,0:T(2,128)S(1)} %copy.336), kind=kLoop, calls=%fused_computation.8 | loop fusion | flops 2626560 | bytes 996096 | tf_op jit(solution)/shard_map/vmap()/reduce_sum | solution.py:51
  15.0 7.3 %all-to-all-start = ((f32[32,1,12]{2,1,0:T(1,128)}), f32[32,1,12]{2,1,0:T(1,128)S(1)}, u32[]{:S(2)}, u32[]{:S(2)}) async-start(f32[32,1,12]{2,1,0:T(1,128)} %broadcast_in_dim.6), calls=%async_computation | async-start | bytes 32768 | tf_op jit(solution)/shard_map/all_to_all | solution.py:118
  22.6 3.4 %collective-permute-start.2 = (f32[2,2304]{1,0:T(2,128)S(1)}, f32[2,2304]{1,0:T(2,128)S(1)}, u32[]{:S(2)}, u32[]{:S(2)}) collective-permute-start(f32[2,2304]{1,0:T(2,128)S(1)} %get-tuple-element.72), channel_id=1, source_target_pairs={{1,0},{2,1},{3,2},{4,3},{5,4},{6,5},{7,6},{0,7},{9,8},{10,9},{11,1... | collective-permute-start | bytes 55304 | tf_op jit(solution)/shard_map/ppermute | solution.py:13
  26.0 2.4 %collective-permute-start.3 = (f32[2,2304]{1,0:T(2,128)S(1)}, f32[2,2304]{1,0:T(2,128)S(1)}, u32[]{:S(2)}, u32[]{:S(2)}) collective-permute-start(f32[2,2304]{1,0:T(2,128)S(1)} %get-tuple-element.73), channel_id=1, source_target_pairs={{8,0},{16,8},{24,16},{0,24},{9,1},{17,9},{25,17},{1,25},{10,2},{18... | collective-permute-start | bytes 55304 | tf_op jit(solution)/shard_map/ppermute | solution.py:13
  31.6 1.1 %collective-permute-start.1 = (f32[2,2353]{1,0:T(2,128)S(1)}, f32[2,2353]{1,0:T(2,128)S(1)}, u32[]{:S(2)}, u32[]{:S(2)}) collective-permute-start(f32[2,2353]{1,0:T(2,128)S(1)} %concatenate.240), channel_id=1, source_target_pairs={{24,0},{0,8},{8,16},{16,24},{25,1},{1,9},{9,17},{17,25},{26,2},{2,... | collective-permute-start | bytes 56480 | tf_op jit(solution)/shard_map/ppermute | solution.py:13
  33.0 3.5 %collective-permute-done = f32[2,2353]{1,0:T(2,128)S(1)} collective-permute-done((f32[2,2353]{1,0:T(2,128)S(1)}, f32[2,2353]{1,0:T(2,128)S(1)}, u32[]{:S(2)}, u32[]{:S(2)}) %collective-permute-start) | collective-permute-done | bytes 18856 | tf_op jit(solution)/shard_map/ppermute | solution.py:13
  38.1 2.3 %add_multiply_fusion.1 = f32[2,48,48,48]{3,2,1,0:T(8,128)S(1)} fusion(f32[2,48,48]{2,1,0:T(8,128)S(1)} %get-tuple-element.46, f32[2,48]{1,0:T(2,128)S(1)} %bitcast.397, f32[2,48,48]{2,1,0:T(8,128)S(1)} %get-tuple-element.47, f32[2,48]{1,0:T(2,128)S(1)} %bitcast.394, f32[2,48,48]{2,1,0:T(8,128)S(1)} %get-tuple-element.48, ...), kind=kLoop, calls=%fused_computation.14 | loop fusion | flops 3096576 | bytes 1014912 | tf_op jit(solution)/shard_map/vmap()/mul | solution.py:65
  40.4 2.3 %multiply_reduce_fusion.5 = (f32[2,2,48,48]{3,2,1,0:T(8,128)S(1)}, f32[2,2,48,48]{3,2,1,0:T(8,128)S(1)}, f32[2,2,48,48]{3,2,1,0:T(8,128)S(1)}) fusion(f32[2,48,48,48]{3,2,1,0:T(8,128)S(1)} %add_multiply_fusion.1, f32[2,2,48]{2,1,0:T(2,128)S(1)} %copy.336), kind=kLoop, calls=%fused_computation.5 | loop fusion | flops 2626560 | bytes 996096 | tf_op jit(solution)/shard_map/vmap()/reduce_sum | solution.py:51
  45.6 3.0 %all-to-all-start.1 = ((f32[32,1,14]{2,1,0:T(1,128)}), f32[32,1,14]{2,1,0:T(1,128)S(1)}, u32[]{:S(2)}, u32[]{:S(2)}) async-start(f32[32,1,14]{2,1,0:T(1,128)} %broadcast_in_dim.7), calls=%async_computation.1 | async-start | bytes 32768 | tf_op jit(solution)/shard_map/all_to_all | solution.py:118
  49.0 1.7 %collective-permute-start.7 = (f32[2,2304]{1,0:T(2,128)S(1)}, f32[2,2304]{1,0:T(2,128)S(1)}, u32[]{:S(2)}, u32[]{:S(2)}) collective-permute-start(f32[2,2304]{1,0:T(2,128)S(1)} %get-tuple-element.67), channel_id=1, source_target_pairs={{24,0},{0,8},{8,16},{16,24},{25,1},{1,9},{9,17},{17,25},{26,2},{2,... | collective-permute-start | bytes 55304 | tf_op jit(solution)/shard_map/ppermute | solution.py:13
  50.6 3.1 %collective-permute-start.4 = (f32[2,2304]{1,0:T(2,128)S(1)}, f32[2,2304]{1,0:T(2,128)S(1)}, u32[]{:S(2)}, u32[]{:S(2)}) collective-permute-start(f32[2,2304]{1,0:T(2,128)S(1)} %get-tuple-element.68), channel_id=1, source_target_pairs={{1,0},{2,1},{3,2},{4,3},{5,4},{6,5},{7,6},{0,7},{9,8},{10,9},{11,1... | collective-permute-start | bytes 55304 | tf_op jit(solution)/shard_map/ppermute | solution.py:13
  53.8 1.2 %collective-permute-start.5 = (f32[2,2304]{1,0:T(2,128)S(1)}, f32[2,2304]{1,0:T(2,128)S(1)}, u32[]{:S(2)}, u32[]{:S(2)}) collective-permute-start(f32[2,2304]{1,0:T(2,128)S(1)} %get-tuple-element.69), channel_id=1, source_target_pairs={{8,0},{16,8},{24,16},{0,24},{9,1},{17,9},{25,17},{1,25},{10,2},{18... | collective-permute-start | bytes 55304 | tf_op jit(solution)/shard_map/ppermute | solution.py:13
  55.0 0.8 all-to-all-done.1
  60.5 2.3 %add_multiply_fusion = f32[2,48,48,48]{3,2,1,0:T(8,128)S(1)} fusion(f32[2,48,48]{2,1,0:T(8,128)S(1)} %get-tuple-element.40, f32[2,48,48]{2,1,0:T(8,128)S(1)} %get-tuple-element.41, f32[2,48,48]{2,1,0:T(8,128)S(1)} %get-tuple-element.42, f32[2,48,48]{2,1,0:T(8,128)S(1)} %get-tuple-element.43, f32[2,48,48]{2,1,0:T(8,128)S(1)} %get-tuple-element.44, ...), kind=kLoop, calls=%fused_computation.13 | loop fusion | flops 3096576 | bytes 1014912 | tf_op jit(solution)/shard_map/vmap()/mul | solution.py:65
  62.9 2.3 %multiply_reduce_fusion.2 = (f32[2,2,48,48]{3,2,1,0:T(8,128)S(1)}, f32[2,2,48,48]{3,2,1,0:T(8,128)S(1)}, f32[2,2,48,48]{3,2,1,0:T(8,128)S(1)}) fusion(f32[2,48,48,48]{3,2,1,0:T(8,128)S(1)} %add_multiply_fusion, f32[2,2,48]{2,1,0:T(2,128)S(1)} %copy.336), kind=kLoop, calls=%fused_computation.2 | loop fusion | flops 2626560 | bytes 996096 | tf_op jit(solution)/shard_map/vmap()/reduce_sum | solution.py:51
  67.9 2.5 %all-to-all-start.2 = ((f32[32,1,4]{2,1,0:T(1,128)}), f32[32,1,4]{2,1,0:T(1,128)S(1)}, u32[]{:S(2)}, u32[]{:S(2)}) async-start(f32[32,1,4]{2,1,0:T(1,128)} %broadcast_in_dim.8), calls=%async_computation.2 | async-start | bytes 32768 | tf_op jit(solution)/shard_map/all_to_all | solution.py:118
  70.5 3.4 %collective-permute-start.8 = (f32[2,2304]{1,0:T(2,128)S(1)}, f32[2,2304]{1,0:T(2,128)S(1)}, u32[]{:S(2)}, u32[]{:S(2)}) collective-permute-start(f32[2,2304]{1,0:T(2,128)S(1)} %get-tuple-element.64), channel_id=1, source_target_pairs={{1,0},{2,1},{3,2},{4,3},{5,4},{6,5},{7,6},{0,7},{9,8},{10,9},{11,1... | collective-permute-start | bytes 55304 | tf_op jit(solution)/shard_map/ppermute | solution.py:13
  73.9 2.4 %collective-permute-start.9 = (f32[2,2304]{1,0:T(2,128)S(1)}, f32[2,2304]{1,0:T(2,128)S(1)}, u32[]{:S(2)}, u32[]{:S(2)}) collective-permute-start(f32[2,2304]{1,0:T(2,128)S(1)} %get-tuple-element.65), channel_id=1, source_target_pairs={{8,0},{16,8},{24,16},{0,24},{9,1},{17,9},{25,17},{1,25},{10,2},{18... | collective-permute-start | bytes 55304 | tf_op jit(solution)/shard_map/ppermute | solution.py:13
  76.4 1.2 %all-to-all-done.2 = f32[32,1,4]{2,1,0:T(1,128)S(1)} async-done(((f32[32,1,4]{2,1,0:T(1,128)}), f32[32,1,4]{2,1,0:T(1,128)S(1)}, u32[]{:S(2)}, u32[]{:S(2)}) %all-to-all-start.2) | async-done | bytes 544 | tf_op jit(solution)/shard_map/all_to_all | solution.py:118
  (190 shorter events, 18.8 us)
Async XLA Ops:
  1.5 4.3 %copy-start = (f32[1,1,2,48,48]{4,3,2,1,0:T(8,128)S(1)}, f32[1,1,2,48,48]{4,3,2,1,0:T(8,128)}, u32[]{:S(2)}) copy-start(f32[1,1,2,48,48]{4,3,2,1,0:T(8,128)} %param.7) | copy-start | bytes 55300
  5.8 2.3 %copy-start.2 = (f32[1,1,2,48]{3,2,1,0:T(2,128)S(1)}, f32[1,1,2,48]{3,2,1,0:T(2,128)}, u32[]{:S(2)}) copy-start(f32[1,1,2,48]{3,2,1,0:T(2,128)} %param.8) | copy-start | bytes 1156
  10.7 17.8 %copy-start.1 = (s32[4,8]{1,0:T(4,128)S(1)}, s32[4,8]{1,0:T(4,128)}, u32[]{:S(2)}) copy-start(s32[4,8]{1,0:T(4,128)} %param.10) | copy-start | bytes 388
  10.7 18.2 %copy-start.4 = (f32[1,1,6,48]{3,1,2,0:T(1,128)S(1)}, f32[1,1,6,48]{3,1,2,0:T(1,128)}, u32[]{:S(2)}) copy-start(f32[1,1,6,48]{3,1,2,0:T(1,128)} %param.11) | copy-start | bytes 3460
  10.7 18.2 %copy-start.3 = (f32[1,1,2,3]{3,2,1,0:T(2,128)S(1)}, f32[1,1,2,3]{3,2,1,0:T(2,128)}, u32[]{:S(2)}) copy-start(f32[1,1,2,3]{3,2,1,0:T(2,128)} %param.9) | copy-start | bytes 76
  15.0 15.0 %all-to-all-start = ((f32[32,1,12]{2,1,0:T(1,128)}), f32[32,1,12]{2,1,0:T(1,128)S(1)}, u32[]{:S(2)}, u32[]{:S(2)}) async-start(f32[32,1,12]{2,1,0:T(1,128)} %broadcast_in_dim.6), calls=%async_computation | async-start | bytes 32768 | tf_op jit(solution)/shard_map/all_to_all | solution.py:118
  22.6 8.6 %collective-permute-start.2 = (f32[2,2304]{1,0:T(2,128)S(1)}, f32[2,2304]{1,0:T(2,128)S(1)}, u32[]{:S(2)}, u32[]{:S(2)}) collective-permute-start(f32[2,2304]{1,0:T(2,128)S(1)} %get-tuple-element.72), channel_id=1, source_target_pairs={{1,0},{2,1},{3,2},{4,3},{5,4},{6,5},{7,6},{0,7},{9,8},{10,9},{11,1... | collective-permute-start | bytes 55304 | tf_op jit(solution)/shard_map/ppermute | solution.py:13
  26.0 5.2 %collective-permute-start.3 = (f32[2,2304]{1,0:T(2,128)S(1)}, f32[2,2304]{1,0:T(2,128)S(1)}, u32[]{:S(2)}, u32[]{:S(2)}) collective-permute-start(f32[2,2304]{1,0:T(2,128)S(1)} %get-tuple-element.73), channel_id=1, source_target_pairs={{8,0},{16,8},{24,16},{0,24},{9,1},{17,9},{25,17},{1,25},{10,2},{18... | collective-permute-start | bytes 55304 | tf_op jit(solution)/shard_map/ppermute | solution.py:13
  31.5 5.0 %collective-permute-start = (f32[2,2353]{1,0:T(2,128)S(1)}, f32[2,2353]{1,0:T(2,128)S(1)}, u32[]{:S(2)}, u32[]{:S(2)}) collective-permute-start(f32[2,2353]{1,0:T(2,128)S(1)} %concatenate.239), channel_id=1, source_target_pairs={{7,0},{0,1},{1,2},{2,3},{3,4},{4,5},{5,6},{6,7},{15,8},{8,9},{9,10... | collective-permute-start | bytes 56480 | tf_op jit(solution)/shard_map/ppermute | solution.py:13
  31.6 5.0 %collective-permute-start.1 = (f32[2,2353]{1,0:T(2,128)S(1)}, f32[2,2353]{1,0:T(2,128)S(1)}, u32[]{:S(2)}, u32[]{:S(2)}) collective-permute-start(f32[2,2353]{1,0:T(2,128)S(1)} %concatenate.240), channel_id=1, source_target_pairs={{24,0},{0,8},{8,16},{16,24},{25,1},{1,9},{9,17},{17,25},{26,2},{2,... | collective-permute-start | bytes 56480 | tf_op jit(solution)/shard_map/ppermute | solution.py:13
  45.6 10.2 %all-to-all-start.1 = ((f32[32,1,14]{2,1,0:T(1,128)}), f32[32,1,14]{2,1,0:T(1,128)S(1)}, u32[]{:S(2)}, u32[]{:S(2)}) async-start(f32[32,1,14]{2,1,0:T(1,128)} %broadcast_in_dim.7), calls=%async_computation.1 | async-start | bytes 32768 | tf_op jit(solution)/shard_map/all_to_all | solution.py:118
  48.7 10.7 %collective-permute-start.6 = (f32[2,2304]{1,0:T(2,128)S(1)}, f32[2,2304]{1,0:T(2,128)S(1)}, u32[]{:S(2)}, u32[]{:S(2)}) collective-permute-start(f32[2,2304]{1,0:T(2,128)S(1)} %get-tuple-element.66), channel_id=1, source_target_pairs={{7,0},{0,1},{1,2},{2,3},{3,4},{4,5},{5,6},{6,7},{15,8},{8,9},{9,10... | collective-permute-start | bytes 55304 | tf_op jit(solution)/shard_map/ppermute | solution.py:13
  49.0 10.4 %collective-permute-start.7 = (f32[2,2304]{1,0:T(2,128)S(1)}, f32[2,2304]{1,0:T(2,128)S(1)}, u32[]{:S(2)}, u32[]{:S(2)}) collective-permute-start(f32[2,2304]{1,0:T(2,128)S(1)} %get-tuple-element.67), channel_id=1, source_target_pairs={{24,0},{0,8},{8,16},{16,24},{25,1},{1,9},{9,17},{17,25},{26,2},{2,... | collective-permute-start | bytes 55304 | tf_op jit(solution)/shard_map/ppermute | solution.py:13
  50.6 8.5 %collective-permute-start.4 = (f32[2,2304]{1,0:T(2,128)S(1)}, f32[2,2304]{1,0:T(2,128)S(1)}, u32[]{:S(2)}, u32[]{:S(2)}) collective-permute-start(f32[2,2304]{1,0:T(2,128)S(1)} %get-tuple-element.68), channel_id=1, source_target_pairs={{1,0},{2,1},{3,2},{4,3},{5,4},{6,5},{7,6},{0,7},{9,8},{10,9},{11,1... | collective-permute-start | bytes 55304 | tf_op jit(solution)/shard_map/ppermute | solution.py:13
  53.8 5.4 %collective-permute-start.5 = (f32[2,2304]{1,0:T(2,128)S(1)}, f32[2,2304]{1,0:T(2,128)S(1)}, u32[]{:S(2)}, u32[]{:S(2)}) collective-permute-start(f32[2,2304]{1,0:T(2,128)S(1)} %get-tuple-element.69), channel_id=1, source_target_pairs={{8,0},{16,8},{24,16},{0,24},{9,1},{17,9},{25,17},{1,25},{10,2},{18... | collective-permute-start | bytes 55304 | tf_op jit(solution)/shard_map/ppermute | solution.py:13
  67.9 9.6 %all-to-all-start.2 = ((f32[32,1,4]{2,1,0:T(1,128)}), f32[32,1,4]{2,1,0:T(1,128)S(1)}, u32[]{:S(2)}, u32[]{:S(2)}) async-start(f32[32,1,4]{2,1,0:T(1,128)} %broadcast_in_dim.8), calls=%async_computation.2 | async-start | bytes 32768 | tf_op jit(solution)/shard_map/all_to_all | solution.py:118
  70.5 12.1 %collective-permute-start.8 = (f32[2,2304]{1,0:T(2,128)S(1)}, f32[2,2304]{1,0:T(2,128)S(1)}, u32[]{:S(2)}, u32[]{:S(2)}) collective-permute-start(f32[2,2304]{1,0:T(2,128)S(1)} %get-tuple-element.64), channel_id=1, source_target_pairs={{1,0},{2,1},{3,2},{4,3},{5,4},{6,5},{7,6},{0,7},{9,8},{10,9},{11,1... | collective-permute-start | bytes 55304 | tf_op jit(solution)/shard_map/ppermute | solution.py:13
  73.9 8.7 %collective-permute-start.9 = (f32[2,2304]{1,0:T(2,128)S(1)}, f32[2,2304]{1,0:T(2,128)S(1)}, u32[]{:S(2)}, u32[]{:S(2)}) collective-permute-start(f32[2,2304]{1,0:T(2,128)S(1)} %get-tuple-element.65), channel_id=1, source_target_pairs={{8,0},{16,8},{24,16},{0,24},{9,1},{17,9},{25,17},{1,25},{10,2},{18... | collective-permute-start | bytes 55304 | tf_op jit(solution)/shard_map/ppermute | solution.py:13

commit v3 on v2

--- a/solution.py
+++ b/solution.py
@@ -146,21 +146,24 @@
     def jumps(traces_now, both, extra=None):
         low_side = traces_now[:, 0]
         high_side = traces_now[:, 1]
-        low_next_owner = shifted(low_side[:, 0], "dev", -1)
-        low_next_group = shifted(low_side[:, 1], "grp", -1)
+        face_size = high_side.shape[-1]
+        sends = [low_side[:, 0], low_side[:, 1]]
+        if both:
+            sends += [
+                jnp.concatenate([high_side[:, 0], extra[0]], axis=1),
+                jnp.concatenate([high_side[:, 1], extra[1]], axis=1),
+            ]
+        sends = lax.optimization_barrier(sends)
+        low_next_owner = shifted(sends[0], "dev", -1)
+        low_next_group = shifted(sends[1], "grp", -1)
         following = jnp.stack(
             [low_next_owner, low_next_group, slot_after(low_side[:, 2])], axis=1
         )
         own = live_own[..., None] * (high_side - following)
         if not both:
             return own
-        face_size = high_side.shape[-1]
-        high_prev_owner = shifted(
-            jnp.concatenate([high_side[:, 0], extra[0]], axis=1), "dev", 1
-        )
-        high_prev_group = shifted(
-            jnp.concatenate([high_side[:, 1], extra[1]], axis=1), "grp", 1
-        )
+        high_prev_owner = shifted(sends[2], "dev", 1)
+        high_prev_group = shifted(sends[3], "grp", 1)
         leading = jnp.stack(
             [high_prev_owner[:, :face_size], high_prev_group[:, :face_size]], axis=1
         )

time: 85 us -> 85.3 us (level)
  waiting for transfers between devices: 5.55 us -> 7.45 us
  starting transfers between devices: 31.9 us -> 30.3 us
    all_to_all x3, waiting for transfers between devices: 2.01 us -> 7.42 us  [gather_all(): got = lax.all_to_all(spread, ('grp', 'dev'), 0, 0, tiled=True)]
    ppermute x10, waiting for transfers between devices: 3.54 us -> 0.03 us  [shifted(): return lax.ppermute(block, axis, route)]
    all_to_all x3, starting transfers between devices: 12.9 us -> 11.3 us  [gather_all(): got = lax.all_to_all(spread, ('grp', 'dev'), 0, 0, tiled=True)]
  transfers between devices with their start and end apart: 13 -> 13, of which waited for: 3 -> 3; matrix products, arithmetic and copies ran while one was open for 7% -> 8% of each run, Pallas kernels for 0% -> 0%
where the time goes in v3:
time: 85.3 us; the launch traced here: 84.9 us
  starting transfers between devices  30.3 us (36%)
  other arithmetic  15.7 us (18%)
  local copies, waits for them, and re-layouts  12.9 us (15%)
  matrix products  11.3 us (13%)
  waiting for transfers between devices  7.45 us (9%)
  between operations  7.28 us (9%)
    ppermute x10, starting transfers between devices, shifted(): return lax.ppermute(block, axis, route)  19 us
    all_to_all x3, starting transfers between devices, gather_all(): got = lax.all_to_all(spread, ('grp', 'dev'), 0, 0, tiled=True)  11.3 us
    all_to_all x3, waiting for transfers between devices, gather_all(): got = lax.all_to_all(spread, ('grp', 'dev'), 0, 0, tiled=True)  7.42 us
    reduce_sum x3, other arithmetic, trace_solved(): along_a = jnp.sum(end_rows[:, :, None, None] * solved[None], axis=1)  6.94 us
    mul x2, other arithmetic, apply_one(): one_inverse * face_spectrum(one_transform, low_side, high_side)  4.56 us
    dot_general x6, matrix products, trace_solved(): jnp.einsum('bj,edjk,ck->edbc', transform, planes, transform, precision=FAST)  2.85 us
    reshape x1, local copies, waits for them, and re-layouts, spectral(): spatial = patch_load.astype(jnp.float32).reshape(points, points, points)  2.66 us
    dot_general x1, matrix products, spectral(): return jnp.einsum('ck,ijc->ijk', transform, moved, precision=FAST)  2.59 us
  transfers between devices with their start and end apart: 13, of which 3 were waited for; matrix products, arithmetic and copies ran while one was open for 8% of the time, Pallas kernels for 0%

profile of v3, /device:TPU:0, one launch (start us, length us, event | category | flops | bytes accessed | tf_op | source)
XLA Modules:
  0.0 84.9 jit_solution(10961297585471777965)
XLA Ops:
  0.6 0.8 broadcast_add_fusion
  1.5 2.7 %reshape.1193 = bf16[2,48,48,48]{3,2,1,0:T(8,128)(2,1)S(1)} reshape(bf16[1,1,2,48,2304]{4,3,2,1,0:T(8,128)(2,1)} %param.6) | data formatting | bytes 884736 | tf_op jit(solution)/shard_map/vmap()/reshape | solution.py:22
  4.1 1.6 %fusion.7 = f32[2,48,48,48]{3,1,2,0:T(8,128)S(1)} fusion(bf16[2,48,48,48]{3,2,1,0:T(8,128)(2,1)S(1)} %reshape.1193, f32[1,1,2,48,48]{4,3,2,1,0:T(8,128)} %param.7), kind=kOutput, calls=%fused_computation.17 | convolution fusion | flops 63700992 | bytes 1345536 | tf_op jit(solution)/shard_map/vmap(ai,abc->ibc)/dot_general | solution.py:23
  5.8 2.2 %fusion.2 = f32[2,48,48,48]{3,2,1,0:T(8,128)S(1)} fusion(f32[2,48,48,48]{3,1,2,0:T(8,128)S(1)} %fusion.7, f32[1,1,2,48,48]{4,3,2,1,0:T(8,128)S(1)} %copy-done), kind=kOutput, calls=%fused_computation.11 | convolution fusion | flops 63700992 | bytes 1787904 | tf_op jit(solution)/shard_map/vmap(bj,ibc->ijc)/dot_general | solution.py:24
  8.1 2.6 %fusion.4 = f32[2,48,48,48]{3,2,1,0:T(8,128)S(1)} fusion(f32[2,48,48,48]{3,2,1,0:T(8,128)S(1)} %fusion.2, f32[2,48]{1,0:T(2,128)S(1)} %bitcast.401, f32[2,48,48]{2,1,0:T(8,128)S(1)} %broadcast_add_fusion, f32[1,1,2,48,48]{4,3,2,1,0:T(8,128)S(1)} %copy-done), kind=kOutput, calls=%fused_computation.16 | convolution fusion | flops 64364544 | bytes 1806720 | tf_op jit(solution)/shard_map/vmap(ck,ijc->ijk)/dot_general | solution.py:25
  10.7 2.3 %multiply_reduce_fusion.8 = (f32[2,2,48,48]{3,2,1,0:T(8,128)S(1)}, f32[2,2,48,48]{3,2,1,0:T(8,128)S(1)}, f32[2,2,48,48]{3,2,1,0:T(8,128)S(1)}) fusion(f32[2,48,48,48]{3,2,1,0:T(8,128)S(1)} %fusion.4, f32[2,2,48]{2,1,0:T(2,128)S(1)} %copy.342), kind=kLoop, calls=%fused_computation.8 | loop fusion | flops 2626560 | bytes 996096 | tf_op jit(solution)/shard_map/vmap()/reduce_sum | solution.py:51
  15.0 4.5 %collective-permute-start.2 = (f32[2,2304]{1,0:T(2,128)S(1)}, f32[2,2304]{1,0:T(2,128)S(1)}, u32[]{:S(2)}, u32[]{:S(2)}) collective-permute-start(f32[2,2304]{1,0:T(2,128)S(1)} %get-tuple-element.14), channel_id=1, source_target_pairs={{1,0},{2,1},{3,2},{4,3},{5,4},{6,5},{7,6},{0,7},{9,8},{10,9},{11,1... | collective-permute-start | bytes 55304 | tf_op jit(solution)/shard_map/ppermute | solution.py:13
  19.5 2.4 %collective-permute-start.3 = (f32[2,2304]{1,0:T(2,128)S(1)}, f32[2,2304]{1,0:T(2,128)S(1)}, u32[]{:S(2)}, u32[]{:S(2)}) collective-permute-start(f32[2,2304]{1,0:T(2,128)S(1)} %get-tuple-element.15), channel_id=1, source_target_pairs={{8,0},{16,8},{24,16},{0,24},{9,1},{17,9},{25,17},{1,25},{10,2},{18... | collective-permute-start | bytes 55304 | tf_op jit(solution)/shard_map/ppermute | solution.py:13
  22.6 6.2 %all-to-all-start = ((f32[32,1,12]{2,1,0:T(1,128)}), f32[32,1,12]{2,1,0:T(1,128)S(1)}, u32[]{:S(2)}, u32[]{:S(2)}) async-start(f32[32,1,12]{2,1,0:T(1,128)} %broadcast_in_dim.6), calls=%async_computation | async-start | bytes 32768 | tf_op jit(solution)/shard_map/all_to_all | solution.py:118
  30.3 5.4 %all-to-all-done = f32[32,1,12]{2,1,0:T(1,128)S(1)} async-done(((f32[32,1,12]{2,1,0:T(1,128)}), f32[32,1,12]{2,1,0:T(1,128)S(1)}, u32[]{:S(2)}, u32[]{:S(2)}) %all-to-all-start) | async-done | bytes 1568 | tf_op jit(solution)/shard_map/all_to_all | solution.py:118
  39.0 2.3 %add_multiply_fusion.1 = f32[2,48,48,48]{3,2,1,0:T(8,128)S(1)} fusion(f32[2,48,48]{2,1,0:T(8,128)S(1)} %get-tuple-element.66, f32[2,48]{1,0:T(2,128)S(1)} %bitcast.392, f32[2,48,48]{2,1,0:T(8,128)S(1)} %get-tuple-element.67, f32[2,48]{1,0:T(2,128)S(1)} %bitcast.389, f32[2,48,48]{2,1,0:T(8,128)S(1)} %get-tuple-element.68, ...), kind=kLoop, calls=%fused_computation.14 | loop fusion | flops 3096576 | bytes 1014912 | tf_op jit(solution)/shard_map/vmap()/mul | solution.py:65
  41.3 2.3 %multiply_reduce_fusion.5 = (f32[2,2,48,48]{3,2,1,0:T(8,128)S(1)}, f32[2,2,48,48]{3,2,1,0:T(8,128)S(1)}, f32[2,2,48,48]{3,2,1,0:T(8,128)S(1)}) fusion(f32[2,48,48,48]{3,2,1,0:T(8,128)S(1)} %add_multiply_fusion.1, f32[2,2,48]{2,1,0:T(2,128)S(1)} %copy.342), kind=kLoop, calls=%fused_computation.5 | loop fusion | flops 2626560 | bytes 996096 | tf_op jit(solution)/shard_map/vmap()/reduce_sum | solution.py:51
  46.5 2.5 %all-to-all-start.1 = ((f32[32,1,14]{2,1,0:T(1,128)}), f32[32,1,14]{2,1,0:T(1,128)S(1)}, u32[]{:S(2)}, u32[]{:S(2)}) async-start(f32[32,1,14]{2,1,0:T(1,128)} %broadcast_in_dim.7), calls=%async_computation.1 | async-start | bytes 32768 | tf_op jit(solution)/shard_map/all_to_all | solution.py:118
  49.2 1.7 %collective-permute-start.7 = (f32[2,2304]{1,0:T(2,128)S(1)}, f32[2,2304]{1,0:T(2,128)S(1)}, u32[]{:S(2)}, u32[]{:S(2)}) collective-permute-start(f32[2,2304]{1,0:T(2,128)S(1)} %get-tuple-element.19), channel_id=1, source_target_pairs={{24,0},{0,8},{8,16},{16,24},{25,1},{1,9},{9,17},{17,25},{26,2},{2,... | collective-permute-start | bytes 55304 | tf_op jit(solution)/shard_map/ppermute | solution.py:13
  50.9 3.1 %collective-permute-start.4 = (f32[2,2304]{1,0:T(2,128)S(1)}, f32[2,2304]{1,0:T(2,128)S(1)}, u32[]{:S(2)}, u32[]{:S(2)}) collective-permute-start(f32[2,2304]{1,0:T(2,128)S(1)} %get-tuple-element.16), channel_id=1, source_target_pairs={{1,0},{2,1},{3,2},{4,3},{5,4},{6,5},{7,6},{0,7},{9,8},{10,9},{11,1... | collective-permute-start | bytes 55304 | tf_op jit(solution)/shard_map/ppermute | solution.py:13
  54.0 1.3 %collective-permute-start.5 = (f32[2,2304]{1,0:T(2,128)S(1)}, f32[2,2304]{1,0:T(2,128)S(1)}, u32[]{:S(2)}, u32[]{:S(2)}) collective-permute-start(f32[2,2304]{1,0:T(2,128)S(1)} %get-tuple-element.17), channel_id=1, source_target_pairs={{8,0},{16,8},{24,16},{0,24},{9,1},{17,9},{25,17},{1,25},{10,2},{18... | collective-permute-start | bytes 55304 | tf_op jit(solution)/shard_map/ppermute | solution.py:13
  55.3 0.8 all-to-all-done.1
  60.9 2.3 %add_multiply_fusion = f32[2,48,48,48]{3,2,1,0:T(8,128)S(1)} fusion(f32[2,48,48]{2,1,0:T(8,128)S(1)} %get-tuple-element.60, f32[2,48,48]{2,1,0:T(8,128)S(1)} %get-tuple-element.61, f32[2,48,48]{2,1,0:T(8,128)S(1)} %get-tuple-element.62, f32[2,48,48]{2,1,0:T(8,128)S(1)} %get-tuple-element.63, f32[2,48,48]{2,1,0:T(8,128)S(1)} %get-tuple-element.64, ...), kind=kLoop, calls=%fused_computation.13 | loop fusion | flops 3096576 | bytes 1014912 | tf_op jit(solution)/shard_map/vmap()/mul | solution.py:65
  63.1 2.3 %multiply_reduce_fusion.2 = (f32[2,2,48,48]{3,2,1,0:T(8,128)S(1)}, f32[2,2,48,48]{3,2,1,0:T(8,128)S(1)}, f32[2,2,48,48]{3,2,1,0:T(8,128)S(1)}) fusion(f32[2,48,48,48]{3,2,1,0:T(8,128)S(1)} %add_multiply_fusion, f32[2,2,48]{2,1,0:T(2,128)S(1)} %copy.342), kind=kLoop, calls=%fused_computation.2 | loop fusion | flops 2626560 | bytes 996096 | tf_op jit(solution)/shard_map/vmap()/reduce_sum | solution.py:51
  68.2 2.5 %all-to-all-start.2 = ((f32[32,1,4]{2,1,0:T(1,128)}), f32[32,1,4]{2,1,0:T(1,128)S(1)}, u32[]{:S(2)}, u32[]{:S(2)}) async-start(f32[32,1,4]{2,1,0:T(1,128)} %broadcast_in_dim.8), calls=%async_computation.2 | async-start | bytes 32768 | tf_op jit(solution)/shard_map/all_to_all | solution.py:118
  70.8 3.4 %collective-permute-start.8 = (f32[2,2304]{1,0:T(2,128)S(1)}, f32[2,2304]{1,0:T(2,128)S(1)}, u32[]{:S(2)}, u32[]{:S(2)}) collective-permute-start(f32[2,2304]{1,0:T(2,128)S(1)} %get-tuple-element.20), channel_id=1, source_target_pairs={{1,0},{2,1},{3,2},{4,3},{5,4},{6,5},{7,6},{0,7},{9,8},{10,9},{11,1... | collective-permute-start | bytes 55304 | tf_op jit(solution)/shard_map/ppermute | solution.py:13
  74.2 2.4 %collective-permute-start.9 = (f32[2,2304]{1,0:T(2,128)S(1)}, f32[2,2304]{1,0:T(2,128)S(1)}, u32[]{:S(2)}, u32[]{:S(2)}) collective-permute-start(f32[2,2304]{1,0:T(2,128)S(1)} %get-tuple-element.21), channel_id=1, source_target_pairs={{8,0},{16,8},{24,16},{0,24},{9,1},{17,9},{25,17},{1,25},{10,2},{18... | collective-permute-start | bytes 55304 | tf_op jit(solution)/shard_map/ppermute | solution.py:13
  76.7 1.2 %all-to-all-done.2 = f32[32,1,4]{2,1,0:T(1,128)S(1)} async-done(((f32[32,1,4]{2,1,0:T(1,128)}), f32[32,1,4]{2,1,0:T(1,128)S(1)}, u32[]{:S(2)}, u32[]{:S(2)}) %all-to-all-start.2) | async-done | bytes 544 | tf_op jit(solution)/shard_map/all_to_all | solution.py:118
  83.6 0.7 copy.413
  (190 shorter events, 18.0 us)
Async XLA Ops:
  1.5 4.3 %copy-start = (f32[1,1,2,48,48]{4,3,2,1,0:T(8,128)S(1)}, f32[1,1,2,48,48]{4,3,2,1,0:T(8,128)}, u32[]{:S(2)}) copy-start(f32[1,1,2,48,48]{4,3,2,1,0:T(8,128)} %param.7) | copy-start | bytes 55300
  5.8 2.3 %copy-start.2 = (f32[1,1,2,48]{3,2,1,0:T(2,128)S(1)}, f32[1,1,2,48]{3,2,1,0:T(2,128)}, u32[]{:S(2)}) copy-start(f32[1,1,2,48]{3,2,1,0:T(2,128)} %param.8) | copy-start | bytes 1156
  10.7 4.0 %copy-start.4 = (f32[1,1,6,48]{3,1,2,0:T(1,128)S(1)}, f32[1,1,6,48]{3,1,2,0:T(1,128)}, u32[]{:S(2)}) copy-start(f32[1,1,6,48]{3,1,2,0:T(1,128)} %param.11) | copy-start | bytes 3460
  10.7 4.0 %copy-start.3 = (f32[1,1,2,3]{3,2,1,0:T(2,128)S(1)}, f32[1,1,2,3]{3,2,1,0:T(2,128)}, u32[]{:S(2)}) copy-start(f32[1,1,2,3]{3,2,1,0:T(2,128)} %param.9) | copy-start | bytes 76
  10.7 18.1 %copy-start.1 = (s32[4,8]{1,0:T(4,128)S(1)}, s32[4,8]{1,0:T(4,128)}, u32[]{:S(2)}) copy-start(s32[4,8]{1,0:T(4,128)} %param.10) | copy-start | bytes 388
  15.0 21.9 %collective-permute-start.2 = (f32[2,2304]{1,0:T(2,128)S(1)}, f32[2,2304]{1,0:T(2,128)S(1)}, u32[]{:S(2)}, u32[]{:S(2)}) collective-permute-start(f32[2,2304]{1,0:T(2,128)S(1)} %get-tuple-element.14), channel_id=1, source_target_pairs={{1,0},{2,1},{3,2},{4,3},{5,4},{6,5},{7,6},{0,7},{9,8},{10,9},{11,1... | collective-permute-start | bytes 55304 | tf_op jit(solution)/shard_map/ppermute | solution.py:13
  19.5 17.4 %collective-permute-start.3 = (f32[2,2304]{1,0:T(2,128)S(1)}, f32[2,2304]{1,0:T(2,128)S(1)}, u32[]{:S(2)}, u32[]{:S(2)}) collective-permute-start(f32[2,2304]{1,0:T(2,128)S(1)} %get-tuple-element.15), channel_id=1, source_target_pairs={{8,0},{16,8},{24,16},{0,24},{9,1},{17,9},{25,17},{1,25},{10,2},{18... | collective-permute-start | bytes 55304 | tf_op jit(solution)/shard_map/ppermute | solution.py:13
  21.9 15.4 %collective-permute-start = (f32[2,2353]{1,0:T(2,128)S(1)}, f32[2,2353]{1,0:T(2,128)S(1)}, u32[]{:S(2)}, u32[]{:S(2)}) collective-permute-start(f32[2,2353]{1,0:T(2,128)S(1)} %concatenate.239), channel_id=1, source_target_pairs={{7,0},{0,1},{1,2},{2,3},{3,4},{4,5},{5,6},{6,7},{15,8},{8,9},{9,10... | collective-permute-start | bytes 56480 | tf_op jit(solution)/shard_map/ppermute | solution.py:13
  21.9 15.5 %collective-permute-start.1 = (f32[2,2353]{1,0:T(2,128)S(1)}, f32[2,2353]{1,0:T(2,128)S(1)}, u32[]{:S(2)}, u32[]{:S(2)}) collective-permute-start(f32[2,2353]{1,0:T(2,128)S(1)} %concatenate.240), channel_id=1, source_target_pairs={{24,0},{0,8},{8,16},{16,24},{25,1},{1,9},{9,17},{17,25},{26,2},{2,... | collective-permute-start | bytes 56480 | tf_op jit(solution)/shard_map/ppermute | solution.py:13
  22.6 13.1 %all-to-all-start = ((f32[32,1,12]{2,1,0:T(1,128)}), f32[32,1,12]{2,1,0:T(1,128)S(1)}, u32[]{:S(2)}, u32[]{:S(2)}) async-start(f32[32,1,12]{2,1,0:T(1,128)} %broadcast_in_dim.6), calls=%async_computation | async-start | bytes 32768 | tf_op jit(solution)/shard_map/all_to_all | solution.py:118
  46.5 9.7 %all-to-all-start.1 = ((f32[32,1,14]{2,1,0:T(1,128)}), f32[32,1,14]{2,1,0:T(1,128)S(1)}, u32[]{:S(2)}, u32[]{:S(2)}) async-start(f32[32,1,14]{2,1,0:T(1,128)} %broadcast_in_dim.7), calls=%async_computation.1 | async-start | bytes 32768 | tf_op jit(solution)/shard_map/all_to_all | solution.py:118
  49.0 10.7 %collective-permute-start.6 = (f32[2,2304]{1,0:T(2,128)S(1)}, f32[2,2304]{1,0:T(2,128)S(1)}, u32[]{:S(2)}, u32[]{:S(2)}) collective-permute-start(f32[2,2304]{1,0:T(2,128)S(1)} %get-tuple-element.18), channel_id=1, source_target_pairs={{7,0},{0,1},{1,2},{2,3},{3,4},{4,5},{5,6},{6,7},{15,8},{8,9},{9,10... | collective-permute-start | bytes 55304 | tf_op jit(solution)/shard_map/ppermute | solution.py:13
  49.2 10.5 %collective-permute-start.7 = (f32[2,2304]{1,0:T(2,128)S(1)}, f32[2,2304]{1,0:T(2,128)S(1)}, u32[]{:S(2)}, u32[]{:S(2)}) collective-permute-start(f32[2,2304]{1,0:T(2,128)S(1)} %get-tuple-element.19), channel_id=1, source_target_pairs={{24,0},{0,8},{8,16},{16,24},{25,1},{1,9},{9,17},{17,25},{26,2},{2,... | collective-permute-start | bytes 55304 | tf_op jit(solution)/shard_map/ppermute | solution.py:13
  50.9 8.6 %collective-permute-start.4 = (f32[2,2304]{1,0:T(2,128)S(1)}, f32[2,2304]{1,0:T(2,128)S(1)}, u32[]{:S(2)}, u32[]{:S(2)}) collective-permute-start(f32[2,2304]{1,0:T(2,128)S(1)} %get-tuple-element.16), channel_id=1, source_target_pairs={{1,0},{2,1},{3,2},{4,3},{5,4},{6,5},{7,6},{0,7},{9,8},{10,9},{11,1... | collective-permute-start | bytes 55304 | tf_op jit(solution)/shard_map/ppermute | solution.py:13
  54.0 5.5 %collective-permute-start.5 = (f32[2,2304]{1,0:T(2,128)S(1)}, f32[2,2304]{1,0:T(2,128)S(1)}, u32[]{:S(2)}, u32[]{:S(2)}) collective-permute-start(f32[2,2304]{1,0:T(2,128)S(1)} %get-tuple-element.17), channel_id=1, source_target_pairs={{8,0},{16,8},{24,16},{0,24},{9,1},{17,9},{25,17},{1,25},{10,2},{18... | collective-permute-start | bytes 55304 | tf_op jit(solution)/shard_map/ppermute | solution.py:13
  68.2 9.6 %all-to-all-start.2 = ((f32[32,1,4]{2,1,0:T(1,128)}), f32[32,1,4]{2,1,0:T(1,128)S(1)}, u32[]{:S(2)}, u32[]{:S(2)}) async-start(f32[32,1,4]{2,1,0:T(1,128)} %broadcast_in_dim.8), calls=%async_computation.2 | async-start | bytes 32768 | tf_op jit(solution)/shard_map/all_to_all | solution.py:118
  70.8 12.1 %collective-permute-start.8 = (f32[2,2304]{1,0:T(2,128)S(1)}, f32[2,2304]{1,0:T(2,128)S(1)}, u32[]{:S(2)}, u32[]{:S(2)}) collective-permute-start(f32[2,2304]{1,0:T(2,128)S(1)} %get-tuple-element.20), channel_id=1, source_target_pairs={{1,0},{2,1},{3,2},{4,3},{5,4},{6,5},{7,6},{0,7},{9,8},{10,9},{11,1... | collective-permute-start | bytes 55304 | tf_op jit(solution)/shard_map/ppermute | solution.py:13
  74.2 8.7 %collective-permute-start.9 = (f32[2,2304]{1,0:T(2,128)S(1)}, f32[2,2304]{1,0:T(2,128)S(1)}, u32[]{:S(2)}, u32[]{:S(2)}) collective-permute-start(f32[2,2304]{1,0:T(2,128)S(1)} %get-tuple-element.21), channel_id=1, source_target_pairs={{8,0},{16,8},{24,16},{0,24},{9,1},{17,9},{25,17},{1,25},{10,2},{18... | collective-permute-start | bytes 55304 | tf_op jit(solution)/shard_map/ppermute | solution.py:13

commit v4 on v3

--- a/solution.py
+++ b/solution.py
@@ -25,45 +25,42 @@
     return jnp.einsum("ck,ijc->ijk", transform, moved, precision=FAST)
 
 
-def face_spectrum(transform, low_side, high_side):
+def expansions(transform):
     points = transform.shape[0]
-    planes = jnp.stack([low_side, high_side]).reshape(2, 3, points, points)
-    hats = jnp.einsum("bj,edbc,ck->edjk", transform, planes, transform, precision=FAST)
-    low_row = transform[0]
-    high_row = transform[points - 1]
-    result = low_row[:, None, None] * hats[0, 0][None] + high_row[:, None, None] * hats[1, 0][None]
-    result = (
-        result
-        + low_row[None, :, None] * hats[0, 1][:, None, :]
-        + high_row[None, :, None] * hats[1, 1][:, None, :]
-    )
-    result = (
-        result
-        + low_row[None, None, :] * hats[0, 2][:, :, None]
-        + high_row[None, None, :] * hats[1, 2][:, :, None]
-    )
-    return result
-
-
-def trace_solved(transform, solved):
+    eye = jnp.eye(points, dtype=transform.dtype)
+    ends = [transform[0], transform[points - 1]]
+    across = [jnp.kron(row[None, :], eye) for row in ends]
+    along = [jnp.kron(eye, row[None, :]) for row in ends]
+    return jnp.stack(across + along)
+
+
+def flat_traces(transform, expand, solved):
     points = transform.shape[0]
     end_rows = jnp.stack([transform[0], transform[points - 1]])
-    along_a = jnp.sum(end_rows[:, :, None, None] * solved[None], axis=1)
-    along_b = jnp.sum(end_rows[:, None, :, None] * solved[None], axis=2)
-    along_c = jnp.sum(end_rows[:, None, None, :] * solved[None], axis=3)
+    along_a = jnp.dot(end_rows, solved, precision=FAST).reshape(2, points, points)
+    along_b = jnp.einsum("ix,ekx->eik", solved, expand[:2], precision=FAST)
+    along_c = jnp.einsum("ix,ejx->eij", solved, expand[2:], precision=FAST)
     planes = jnp.stack([along_a, along_b, along_c], axis=1)
     traces = jnp.einsum("bj,edjk,ck->edbc", transform, planes, transform, precision=FAST)
     return traces.reshape(2, 3, points * points)
 
 
-def setup_one(patch_load, one_transform, one_inverse):
-    return trace_solved(one_transform, one_inverse * spectral(patch_load, one_transform))
-
-
-def apply_one(one_transform, one_inverse, low_side, high_side):
-    return trace_solved(
-        one_transform, one_inverse * face_spectrum(one_transform, low_side, high_side)
-    )
+def setup_one(patch_load, one_transform, one_inverse, expand):
+    points = one_transform.shape[0]
+    solved = (one_inverse * spectral(patch_load, one_transform)).reshape(points, points * points)
+    return flat_traces(one_transform, expand, solved)
+
+
+def apply_one(one_transform, one_inverse, expand, low_side, high_side):
+    points = one_transform.shape[0]
+    planes = jnp.stack([low_side, high_side]).reshape(2, 3, points, points)
+    hats = jnp.einsum("bj,edbc,ck->edjk", one_transform, planes, one_transform, precision=FAST)
+    end_rows = jnp.stack([one_transform[0], one_transform[points - 1]])
+    result = jnp.dot(end_rows.T, hats[:, 0].reshape(2, points * points), precision=FAST)
+    mixed = jnp.concatenate([hats[0, 1], hats[1, 1], hats[0, 2], hats[1, 2]], axis=1)
+    result = result + jnp.dot(mixed, expand.reshape(-1, points * points), precision=FAST)
+    solved = one_inverse.reshape(points, points * points) * result
+    return flat_traces(one_transform, expand, solved)
 
 
 def slot_before(vector):
@@ -110,6 +107,7 @@
     )
 
     inverses = jax.vmap(inverse_diagonal)(diagonals)
+    expands = jax.vmap(expansions)(transforms)
     solver = jax.vmap(apply_one)
 
     def gather_all(payload):
@@ -172,7 +170,7 @@
 
     def solve(v_own, v_in):
         preceding = jnp.stack([v_in[:, 0], v_in[:, 1], slot_before(v_own[:, 2])], axis=1)
-        return solver(transforms, inverses, -preceding, v_own)
+        return solver(transforms, inverses, expands, -preceding, v_own)
 
     def split_terms(v_own, v_in, traces_now):
         low_side = traces_now[:, 0]
@@ -194,7 +192,7 @@
         z_in = weights_in[..., None] * res_in + live_in[..., None] * c_in[..., None]
         return z_own, z_in
 
-    start_traces = jax.vmap(setup_one)(patch_loads, transforms, inverses)
+    start_traces = jax.vmap(setup_one)(patch_loads, transforms, inverses, expands)
     gathered = gather_all(face_means(start_traces))
     res_own, res_in, received = jumps(start_traces, True, (extra_owner, extra_group))
     rows_in = jnp.stack([received[0][:, :coarse_size], received[1][:, :coarse_size]], axis=1)

time: 85.3 us -> 211 us (2.47); the launches traced: 84.9 us -> 207 us
  local copies, waits for them, and re-layouts: 12.9 us -> 88.6 us
  matrix products: 11.3 us -> 38.8 us
  other arithmetic: 15.7 us -> 35.2 us
  waiting for transfers between devices: 7.45 us -> 0.03 us
  starting transfers between devices: 30.3 us -> 36.7 us
    dot_general x10 -> x23, matrix products: 4 us -> 27 us  [the longest x6 5.85 us: flat_traces(): jnp.einsum('bj,edjk,ck->edbc', transform, planes, transform, precision=FAST)]
    reshape x5 -> x13, local copies, waits for them, and re-layouts: 1.04 us -> 12.5 us  [the longest x2 3.66 us: apply_one(): planes = jnp.stack([low_side, high_side]).reshape(2, 3, points, points)]
    add x0 -> x4, local copies, waits for them, and re-layouts: none -> 8.45 us  [inverse_diagonal(): diagonal[:, None, None] + diagonal[None, :, None] + diagonal[None, None, :]]
    all_to_all x3, starting transfers between devices: 11.3 us -> 19.4 us  [gather_all(): got = lax.all_to_all(spread, ('grp', 'dev'), 0, 0, tiled=True)]
    all_to_all x3, waiting for transfers between devices: 7.42 us -> 0.01 us  [gather_all(): got = lax.all_to_all(spread, ('grp', 'dev'), 0, 0, tiled=True)]
    reduce_sum x3 -> x0, other arithmetic: 6.94 us -> none  [trace_solved(): along_a = jnp.sum(end_rows[:, :, None, None] * solved[None], axis=1)]
    unnamed x15 -> x156, local copies, waits for them, and re-layouts: 1.42 us -> 7.96 us
    squeeze x4, local copies, waits for them, and re-layouts: 0.27 us -> 5.61 us  [interface_means(): high = raw[:, :, :, 1]]
  transfers between devices with their start and end apart: 13 -> 13, of which waited for: 3 -> 0; matrix products, arithmetic and copies ran while one was open for 8% -> 32% of each run, Pallas kernels for 0% -> 0%
where the time goes in v4:
time: 211 us; the launch traced here: 207 us
  local copies, waits for them, and re-layouts  88.6 us (42%)
  matrix products  38.8 us (18%)
  starting transfers between devices  36.7 us (17%)
  other arithmetic  35.2 us (17%)
  between operations  7.95 us (4%)
    all_to_all x3, starting transfers between devices, gather_all(): got = lax.all_to_all(spread, ('grp', 'dev'), 0, 0, tiled=True)  19.4 us
    ppermute x10, starting transfers between devices, shifted(): return lax.ppermute(block, axis, route)  17.3 us
    add x4, local copies, waits for them, and re-layouts, inverse_diagonal(): diagonal[:, None, None] + diagonal[None, :, None] + diagonal[None, None, :]  8.45 us
    unnamed x156, local copies, waits for them, and re-layouts  7.96 us
    dot_general x6, matrix products, flat_traces(): jnp.einsum('bj,edjk,ck->edbc', transform, planes, transform, precision=FAST)  5.85 us
    squeeze x4, local copies, waits for them, and re-layouts, interface_means(): high = raw[:, :, :, 1]  5.61 us
    dot_general x3, matrix products, flat_traces(): along_c = jnp.einsum('ix,ejx->eij', solved, expand[2:], precision=FAST)  5.03 us
    another operation x6, local copies, waits for them, and re-layouts, interface_means(): jnp.stack([jnp.roll(low[..., 0], -1, axis=1), jnp.roll(low[..., 1], -1, a...  4.92 us
  transfers between devices with their start and end apart: 13, of which 0 were waited for; matrix products, arithmetic and copies ran while one was open for 32% of the time, Pallas kernels for 0%

profile of v4, /device:TPU:0, one launch (start us, length us, event | category | flops | bytes accessed | tf_op | source)
XLA Modules:
  0.0 207.2 jit_solution(16109355367416501948)
XLA Ops:
  1.5 3.4 %reshape.1231 = bf16[2,48,48,48]{3,2,1,0:T(8,128)(2,1)} reshape(bf16[1,1,2,48,2304]{4,3,2,1,0:T(8,128)(2,1)} %param.6) | data formatting | bytes 884736 | tf_op jit(solution)/shard_map/vmap()/reshape | solution.py:22
  4.9 2.1 %fusion.20 = f32[2,48,48,48]{3,1,2,0:T(8,128)S(1)} fusion(bf16[2,48,48,48]{3,2,1,0:T(8,128)(2,1)} %reshape.1231, f32[1,1,2,48,48]{4,3,2,1,0:T(8,128)} %param.7), kind=kOutput, calls=%fused_computation.22 | convolution fusion | flops 63700992 | bytes 1345536 | tf_op jit(solution)/shard_map/vmap(ai,abc->ibc)/dot_general | solution.py:23
  7.1 2.2 %fusion.16 = f32[2,48,48,48]{3,2,1,0:T(8,128)S(1)} fusion(f32[2,48,48,48]{3,1,2,0:T(8,128)S(1)} %fusion.20, f32[1,1,2,48,48]{4,3,2,1,0:T(8,128)S(1)} %copy-done), kind=kOutput, calls=%fused_computation.19 | convolution fusion | flops 63700992 | bytes 1787904 | tf_op jit(solution)/shard_map/vmap(bj,ibc->ijc)/dot_general | solution.py:24
  9.3 2.5 %divide_multiply_fusion = f32[2,48,48,48]{3,2,1,0:T(8,128)S(1)} fusion(f32[2,48,48,48]{3,2,1,0:T(8,128)S(1)} %fusion.16, f32[2,48]{1,0:T(2,128)S(1)} %bitcast.483, f32[2,48,48]{2,1,0:T(8,128)S(1)} %broadcast_add_fusion, f32[1,1,2,48,48]{4,3,2,1,0:T(8,128)S(1)} %copy-done), kind=kOutput, calls=%fused_computation.21 | convolution fusion | flops 64364544 | bytes 1806720 | tf_op jit(solution)/shard_map/vmap(ck,ijc->ijk)/dot_general | solution.py:25
  11.8 2.0 reshape.1246
  19.1 2.7 %fusion.31 = f32[2,2,1,48,48]{3,4,1,0,2:T(8,128)S(1)} fusion(f32[2,48,2304,1]{2,1,0,3:T(8,128)} %reshape.1246, f32[1,2,48,2304]{3,2,0,1:T(8,128)S(1)} %get-tuple-element.53, f32[1,2,48,2304]{3,2,0,1:T(8,128)S(1)} %get-tuple-element.52, f32[1,2,48,2304]{3,2,0,1:T(8,128)S(1)} %get-tuple-element.123, f32[1,2,48,2304]{3,2,0,1:T(8,128)S(1)} %get-tuple-element.124), kind=kOutput, calls=%fused_computation.27 | convolution fusion | flops 130056192 | bytes 4460544 | tf_op jit(solution)/shard_map/vmap(ix,ejx->eij)/dot_general | solution.py:42
  25.1 7.4 %all-to-all-start = ((f32[32,1,12]{2,1,0:T(1,128)}), f32[32,1,12]{2,1,0:T(1,128)}, u32[]{:S(2)}, u32[]{:S(2)}) async-start(f32[32,1,12]{2,1,0:T(1,128)} %broadcast_in_dim.18), calls=%async_computation | async-start | bytes 32768 | tf_op jit(solution)/shard_map/all_to_all | solution.py:116
  35.1 3.3 %collective-permute-start.2 = (f32[2,2304]{1,0:T(2,128)}, f32[2,2304]{1,0:T(2,128)}, u32[]{:S(2)}, u32[]{:S(2)}) collective-permute-start(f32[2,2304]{1,0:T(2,128)} %get-tuple-element.14), channel_id=1, source_target_pairs={{1,0},{2,1},{3,2},{4,3},{5,4},{6,5},{7,6},{0,7},{9,8},{10,9},{11,1... | collective-permute-start | bytes 55304 | tf_op jit(solution)/shard_map/ppermute | solution.py:13
  38.4 2.4 %collective-permute-start.3 = (f32[2,2304]{1,0:T(2,128)}, f32[2,2304]{1,0:T(2,128)}, u32[]{:S(2)}, u32[]{:S(2)}) collective-permute-start(f32[2,2304]{1,0:T(2,128)} %get-tuple-element.15), channel_id=1, source_target_pairs={{8,0},{16,8},{24,16},{0,24},{9,1},{17,9},{25,17},{1,25},{10,2},{18... | collective-permute-start | bytes 55304 | tf_op jit(solution)/shard_map/ppermute | solution.py:13
  43.0 2.3 %pad_maximum_fusion = f32[4,2,48,2304]{3,2,0,1:T(8,128)S(1)} fusion(f32[1,2,48,2304]{3,2,0,1:T(8,128)} %copy-done.5, f32[1,2,48,2304]{3,2,0,1:T(8,128)} %copy-done.2, f32[1,2,48,2304]{3,2,0,1:T(8,128)} %copy-done.8, f32[1,2,48,2304]{3,2,0,1:T(8,128)} %copy-done.11), kind=kLoop, calls=%fused_computation.4 | loop fusion | flops 2654208 | bytes 7077888 | tf_op jit(solution)/shard_map/vmap()/stack | solution.py:34
  58.0 2.5 %add.238 = f32[2,48,48,48]{3,2,1,0:T(8,128)} broadcast(f32[2,48,48]{2,1,0:T(8,128)} %copy-done.32), dimensions={0,1,2} | broadcast | bytes 903168 | tf_op jit(solution)/shard_map/vmap()/add | solution.py:17
  60.5 3.1 %add.239 = f32[2,48,2304]{2,1,0:T(8,128)} reshape(f32[2,48,48,48]{3,2,1,0:T(8,128)} %add.238) | data formatting | bytes 1769472 | tf_op jit(solution)/shard_map/vmap()/add | solution.py:17
  98.0 1.8 reshape.1269
  105.2 2.3 %fusion.58 = f32[2,48,2304]{2,1,0:T(8,128)S(1)} fusion(f32[2,192,2304]{2,1,0:T(8,128)S(1)} %bitcast.449, f32[2,48,48]{2,1,0:T(8,128)} %get-tuple-element.60, f32[2,48,48]{2,1,0:T(8,128)} %get-tuple-element.61, f32[2,48,48]{2,1,0:T(8,128)} %get-tuple-element.59, f32[2,48,48]{2,1,0:T(8,128)} %get-tuple-element.58), kind=kOutput, calls=%fused_computation.64 | convolution fusion | flops 254859264 | bytes 4497408 | tf_op jit(solution)/shard_map/vmap()/dot_general | solution.py:61
  117.7 2.4 %fusion.156 = (f32[2,2,3]{2,1,0:T(2,128)}, f32[2,2,3,48,48]{4,3,2,1,0:T(8,128)}) fusion(f32[2,2,3,48,48]{3,4,2,1,0:T(8,128)S(1)} %fusion.54, f32[1,1,2,48,48]{4,3,2,1,0:T(8,128)} %param.7), kind=kOutput, calls=%fused_computation.281 | convolution fusion | flops 7990260 | bytes 239664 | tf_op jit(solution)/shard_map/vmap(bj,edjk,ck->edbc)/dot_general | solution.py:44
  120.1 1.8 reshape.1270
  134.5 6.0 %all-to-all-start.1 = ((f32[32,1,14]{2,1,0:T(1,128)}), f32[32,1,14]{2,1,0:T(1,128)S(1)}, u32[]{:S(2)}, u32[]{:S(2)}) async-start(f32[32,1,14]{2,1,0:T(1,128)} %broadcast_in_dim.19), calls=%async_computation.1 | async-start | bytes 32768 | tf_op jit(solution)/shard_map/all_to_all | solution.py:116
  141.8 3.4 %collective-permute-start.4 = (f32[2,2304]{1,0:T(2,128)}, f32[2,2304]{1,0:T(2,128)}, u32[]{:S(2)}, u32[]{:S(2)}) collective-permute-start(f32[2,2304]{1,0:T(2,128)} %get-tuple-element.16), channel_id=1, source_target_pairs={{1,0},{2,1},{3,2},{4,3},{5,4},{6,5},{7,6},{0,7},{9,8},{10,9},{11,1... | collective-permute-start | bytes 55304 | tf_op jit(solution)/shard_map/ppermute | solution.py:13
  145.2 2.4 %collective-permute-start.5 = (f32[2,2304]{1,0:T(2,128)}, f32[2,2304]{1,0:T(2,128)}, u32[]{:S(2)}, u32[]{:S(2)}) collective-permute-start(f32[2,2304]{1,0:T(2,128)} %get-tuple-element.17), channel_id=1, source_target_pairs={{8,0},{16,8},{24,16},{0,24},{9,1},{17,9},{25,17},{1,25},{10,2},{18... | collective-permute-start | bytes 55304 | tf_op jit(solution)/shard_map/ppermute | solution.py:13
  170.6 1.8 reshape.1276
  177.8 2.3 %fusion.66 = f32[2,48,2304]{2,1,0:T(8,128)S(1)} fusion(f32[2,192,2304]{2,1,0:T(8,128)S(1)} %bitcast.450, f32[2,48,48]{2,1,0:T(8,128)} %get-tuple-element.56, f32[2,48,48]{2,1,0:T(8,128)} %get-tuple-element.57, f32[2,48,48]{2,1,0:T(8,128)} %get-tuple-element.55, f32[2,48,48]{2,1,0:T(8,128)} %get-tuple-element.54), kind=kOutput, calls=%fused_computation.72 | convolution fusion | flops 254859264 | bytes 4497408 | tf_op jit(solution)/shard_map/vmap()/dot_general | solution.py:61
  186.7 6.0 %all-to-all-start.2 = ((f32[32,1,4]{2,1,0:T(1,128)}), f32[32,1,4]{2,1,0:T(1,128)S(1)}, u32[]{:S(2)}, u32[]{:S(2)}) async-start(f32[32,1,4]{2,1,0:T(1,128)} %broadcast_in_dim.20), calls=%async_computation.2 | async-start | bytes 32768 | tf_op jit(solution)/shard_map/all_to_all | solution.py:116
  194.2 3.4 %collective-permute-start.8 = (f32[2,2304]{1,0:T(2,128)S(1)}, f32[2,2304]{1,0:T(2,128)S(1)}, u32[]{:S(2)}, u32[]{:S(2)}) collective-permute-start(f32[2,2304]{1,0:T(2,128)S(1)} %get-tuple-element.20), channel_id=1, source_target_pairs={{1,0},{2,1},{3,2},{4,3},{5,4},{6,5},{7,6},{0,7},{9,8},{10,9},{11,1... | collective-permute-start | bytes 55304 | tf_op jit(solution)/shard_map/ppermute | solution.py:13
  197.6 2.4 %collective-permute-start.9 = (f32[2,2304]{1,0:T(2,128)S(1)}, f32[2,2304]{1,0:T(2,128)S(1)}, u32[]{:S(2)}, u32[]{:S(2)}) collective-permute-start(f32[2,2304]{1,0:T(2,128)S(1)} %get-tuple-element.21), channel_id=1, source_target_pairs={{8,0},{16,8},{24,16},{0,24},{9,1},{17,9},{25,17},{1,25},{10,2},{18... | collective-permute-start | bytes 55304 | tf_op jit(solution)/shard_map/ppermute | solution.py:13
  (360 shorter events, 127.2 us)
Async XLA Ops:
  25.1 39.9 %all-to-all-start = ((f32[32,1,12]{2,1,0:T(1,128)}), f32[32,1,12]{2,1,0:T(1,128)}, u32[]{:S(2)}, u32[]{:S(2)}) async-start(f32[32,1,12]{2,1,0:T(1,128)} %broadcast_in_dim.18), calls=%async_computation | async-start | bytes 32768 | tf_op jit(solution)/shard_map/all_to_all | solution.py:116
  35.1 45.5 %collective-permute-start.2 = (f32[2,2304]{1,0:T(2,128)}, f32[2,2304]{1,0:T(2,128)}, u32[]{:S(2)}, u32[]{:S(2)}) collective-permute-start(f32[2,2304]{1,0:T(2,128)} %get-tuple-element.14), channel_id=1, source_target_pairs={{1,0},{2,1},{3,2},{4,3},{5,4},{6,5},{7,6},{0,7},{9,8},{10,9},{11,1... | collective-permute-start | bytes 55304 | tf_op jit(solution)/shard_map/ppermute | solution.py:13
  38.4 42.2 %collective-permute-start.3 = (f32[2,2304]{1,0:T(2,128)}, f32[2,2304]{1,0:T(2,128)}, u32[]{:S(2)}, u32[]{:S(2)}) collective-permute-start(f32[2,2304]{1,0:T(2,128)} %get-tuple-element.15), channel_id=1, source_target_pairs={{8,0},{16,8},{24,16},{0,24},{9,1},{17,9},{25,17},{1,25},{10,2},{18... | collective-permute-start | bytes 55304 | tf_op jit(solution)/shard_map/ppermute | solution.py:13
  40.8 46.4 %collective-permute-start = (f32[2,2353]{1,0:T(2,128)}, f32[2,2353]{1,0:T(2,128)}, u32[]{:S(2)}, u32[]{:S(2)}) collective-permute-start(f32[2,2353]{1,0:T(2,128)} %concatenate.245), channel_id=1, source_target_pairs={{7,0},{0,1},{1,2},{2,3},{3,4},{4,5},{5,6},{6,7},{15,8},{8,9},{9,10... | collective-permute-start | bytes 56480 | tf_op jit(solution)/shard_map/ppermute | solution.py:13
  40.8 47.1 %collective-permute-start.1 = (f32[2,2353]{1,0:T(2,128)}, f32[2,2353]{1,0:T(2,128)}, u32[]{:S(2)}, u32[]{:S(2)}) collective-permute-start(f32[2,2353]{1,0:T(2,128)} %concatenate.246), channel_id=1, source_target_pairs={{24,0},{0,8},{8,16},{16,24},{25,1},{1,9},{9,17},{17,25},{26,2},{2,... | collective-permute-start | bytes 56480 | tf_op jit(solution)/shard_map/ppermute | solution.py:13
  53.6 77.5 %copy-start.36 = (f32[2,3]{0,1:T(4,128)}, f32[2,3]{0,1:T(4,128)S(1)}, u32[]{:S(2)}) copy-start(f32[2,3]{0,1:T(4,128)S(1)} %copy.417) | copy-start | bytes 76
  53.7 77.4 %copy-start.34 = (f32[2,3]{0,1:T(4,128)}, f32[2,3]{0,1:T(4,128)S(1)}, u32[]{:S(2)}) copy-start(f32[2,3]{0,1:T(4,128)S(1)} %copy.418) | copy-start | bytes 76
  80.5 50.6 %copy-start.39 = (f32[2,3]{0,1:T(4,128)}, f32[2,3]{0,1:T(4,128)S(1)}, u32[]{:S(2)}) copy-start(f32[2,3]{0,1:T(4,128)S(1)} %copy.419) | copy-start | bytes 76
  89.9 37.4 %copy-start.45 = (f32[2,2]{0,1:T(2,128)}, f32[2,2]{0,1:T(2,128)S(1)}, u32[]{:S(2)}) copy-start(f32[2,2]{0,1:T(2,128)S(1)} %copy.405) | copy-start | bytes 52
  134.5 14.5 %all-to-all-start.1 = ((f32[32,1,14]{2,1,0:T(1,128)}), f32[32,1,14]{2,1,0:T(1,128)S(1)}, u32[]{:S(2)}, u32[]{:S(2)}) async-start(f32[32,1,14]{2,1,0:T(1,128)} %broadcast_in_dim.19), calls=%async_computation.1 | async-start | bytes 32768 | tf_op jit(solution)/shard_map/all_to_all | solution.py:116
  141.8 22.5 %collective-permute-start.4 = (f32[2,2304]{1,0:T(2,128)}, f32[2,2304]{1,0:T(2,128)}, u32[]{:S(2)}, u32[]{:S(2)}) collective-permute-start(f32[2,2304]{1,0:T(2,128)} %get-tuple-element.16), channel_id=1, source_target_pairs={{1,0},{2,1},{3,2},{4,3},{5,4},{6,5},{7,6},{0,7},{9,8},{10,9},{11,1... | collective-permute-start | bytes 55304 | tf_op jit(solution)/shard_map/ppermute | solution.py:13
  145.2 19.1 %collective-permute-start.5 = (f32[2,2304]{1,0:T(2,128)}, f32[2,2304]{1,0:T(2,128)}, u32[]{:S(2)}, u32[]{:S(2)}) collective-permute-start(f32[2,2304]{1,0:T(2,128)} %get-tuple-element.17), channel_id=1, source_target_pairs={{8,0},{16,8},{24,16},{0,24},{9,1},{17,9},{25,17},{1,25},{10,2},{18... | collective-permute-start | bytes 55304 | tf_op jit(solution)/shard_map/ppermute | solution.py:13
  147.6 17.9 %collective-permute-start.6 = (f32[2,2304]{1,0:T(2,128)}, f32[2,2304]{1,0:T(2,128)}, u32[]{:S(2)}, u32[]{:S(2)}) collective-permute-start(f32[2,2304]{1,0:T(2,128)} %get-tuple-element.18), channel_id=1, source_target_pairs={{7,0},{0,1},{1,2},{2,3},{3,4},{4,5},{5,6},{6,7},{15,8},{8,9},{9,10... | collective-permute-start | bytes 55304 | tf_op jit(solution)/shard_map/ppermute | solution.py:13
  147.6 18.0 %collective-permute-start.7 = (f32[2,2304]{1,0:T(2,128)}, f32[2,2304]{1,0:T(2,128)}, u32[]{:S(2)}, u32[]{:S(2)}) collective-permute-start(f32[2,2304]{1,0:T(2,128)} %get-tuple-element.19), channel_id=1, source_target_pairs={{24,0},{0,8},{8,16},{16,24},{25,1},{1,9},{9,17},{17,25},{26,2},{2,... | collective-permute-start | bytes 55304 | tf_op jit(solution)/shard_map/ppermute | solution.py:13
  182.2 23.1 %copy-start.15 = (f32[2,1,3,2304]{3,2,1,0:T(4,128)S(1)}, f32[2,1,3,2304]{3,2,1,0:T(4,128)}, u32[]{:S(2)}) copy-start(f32[2,1,3,2304]{3,2,1,0:T(4,128)} %copy-done.14) | copy-start | bytes 165892
  182.2 23.1 %copy-start.25 = (f32[2,1,3,2304]{3,0,2,1:T(2,128)S(1)}, f32[2,1,3,2304]{3,0,2,1:T(2,128)}, u32[]{:S(2)}) copy-start(f32[2,1,3,2304]{3,0,2,1:T(2,128)} %copy.592) | copy-start | bytes 165892
  182.2 23.1 %copy-start.30 = (f32[1,1,2,3,2304]{4,2,3,1,0:T(2,128)S(1)}, f32[1,1,2,3,2304]{4,2,3,1,0:T(2,128)}, u32[]{:S(2)}) copy-start(f32[1,1,2,3,2304]{4,2,3,1,0:T(2,128)} %pad_maximum_fusion.4) | copy-start | bytes 165892
  182.2 23.1 %copy-start.41 = (f32[1,1,2,1,2304]{4,0,3,2,1:T(1,128)S(1)}, f32[1,1,2,1,2304]{4,0,3,2,1:T(1,128)}, u32[]{:S(2)}) copy-start(f32[1,1,2,1,2304]{4,0,3,2,1:T(1,128)} %stack.299) | copy-start | bytes 55300
  182.2 23.1 %copy-start.50 = (f32[2,3]{1,0:T(2,128)S(1)}, f32[2,3]{1,0:T(2,128)}, u32[]{:S(2)}) copy-start(f32[2,3]{1,0:T(2,128)} %copy-done.49) | copy-start | bytes 76
  182.2 24.0 %copy-start.64 = (f32[1,1,2,3]{3,2,1,0:T(2,128)S(1)}, f32[1,1,2,3]{3,2,1,0:T(2,128)}, u32[]{:S(2)}) copy-start(f32[1,1,2,3]{3,2,1,0:T(2,128)} %param.9) | copy-start | bytes 76
  182.3 24.0 %copy-start.66 = (f32[2,3]{1,0:T(2,128)S(1)}, f32[2,3]{1,0:T(2,128)}, u32[]{:S(2)}) copy-start(f32[2,3]{1,0:T(2,128)} %mul.750) | copy-start | bytes 76
  186.7 13.3 %all-to-all-start.2 = ((f32[32,1,4]{2,1,0:T(1,128)}), f32[32,1,4]{2,1,0:T(1,128)S(1)}, u32[]{:S(2)}, u32[]{:S(2)}) async-start(f32[32,1,4]{2,1,0:T(1,128)} %broadcast_in_dim.20), calls=%async_computation.2 | async-start | bytes 32768 | tf_op jit(solution)/shard_map/all_to_all | solution.py:116
  194.2 11.0 %collective-permute-start.8 = (f32[2,2304]{1,0:T(2,128)S(1)}, f32[2,2304]{1,0:T(2,128)S(1)}, u32[]{:S(2)}, u32[]{:S(2)}) collective-permute-start(f32[2,2304]{1,0:T(2,128)S(1)} %get-tuple-element.20), channel_id=1, source_target_pairs={{1,0},{2,1},{3,2},{4,3},{5,4},{6,5},{7,6},{0,7},{9,8},{10,9},{11,1... | collective-permute-start | bytes 55304 | tf_op jit(solution)/shard_map/ppermute | solution.py:13
  197.6 7.6 %collective-permute-start.9 = (f32[2,2304]{1,0:T(2,128)S(1)}, f32[2,2304]{1,0:T(2,128)S(1)}, u32[]{:S(2)}, u32[]{:S(2)}) collective-permute-start(f32[2,2304]{1,0:T(2,128)S(1)} %get-tuple-element.21), channel_id=1, source_target_pairs={{8,0},{16,8},{24,16},{0,24},{9,1},{17,9},{25,17},{1,25},{10,2},{18... | collective-permute-start | bytes 55304 | tf_op jit(solution)/shard_map/ppermute | solution.py:13
  (64 other events, 277.8 us)

commit v5 on v3

--- a/solution.py
+++ b/solution.py
@@ -19,8 +19,8 @@
 
 def spectral(patch_load, transform):
     points = transform.shape[0]
-    spatial = patch_load.astype(jnp.float32).reshape(points, points, points)
-    moved = jnp.einsum("ai,abc->ibc", transform, spatial, precision=FAST)
+    flat = jnp.dot(transform.T, patch_load.astype(jnp.float32), precision=FAST)
+    moved = flat.reshape(points, points, points)
     moved = jnp.einsum("bj,ibc->ijc", transform, moved, precision=FAST)
     return jnp.einsum("ck,ijc->ijk", transform, moved, precision=FAST)
 
@@ -138,10 +138,11 @@
     def coarse(means):
         here = means[group_index]
         before = means[prev_group]
-        own = jnp.dot(coarse_rows, here, precision=PRECISE).reshape(slot_count, 3)
-        first = jnp.dot(rows_in[:, 0], here, precision=PRECISE)
-        second = jnp.dot(rows_in[:, 1], before, precision=PRECISE)
-        return own, jnp.stack([first, second], axis=1)
+        near = jnp.concatenate([coarse_rows, rows_in[:, 0]], axis=0)
+        values = jnp.sum(near * here[None, :], axis=1)
+        second = jnp.sum(rows_in[:, 1] * before[None, :], axis=1)
+        own = values[: slot_count * 3].reshape(slot_count, 3)
+        return own, jnp.stack([values[slot_count * 3 :], second], axis=1)
 
     def jumps(traces_now, both, extra=None):
         low_side = traces_now[:, 0]

time: 85.3 us -> 85.8 us (level)
    dot_general x7 -> x1, matrix products: 2.52 us -> 2.15 us  [spectral(): flat = jnp.dot(transform.T, patch_load.astype(jnp.float32), precision=FAST)]
  transfers between devices with their start and end apart: 13 -> 13, of which waited for: 3 -> 3; matrix products, arithmetic and copies ran while one was open for 8% -> 7% of each run, Pallas kernels for 0% -> 0%
where the time goes in v5:
time: 85.8 us; the launch traced here: 85.4 us
  starting transfers between devices  30.6 us (36%)
  other arithmetic  16.1 us (19%)
  local copies, waits for them, and re-layouts  13.3 us (16%)
  matrix products  10.8 us (13%)
  waiting for transfers between devices  7.44 us (9%)
  between operations  7.23 us (8%)
    ppermute x10, starting transfers between devices, shifted(): return lax.ppermute(block, axis, route)  19 us
    all_to_all x3, starting transfers between devices, gather_all(): got = lax.all_to_all(spread, ('grp', 'dev'), 0, 0, tiled=True)  11.5 us
    all_to_all x3, waiting for transfers between devices, gather_all(): got = lax.all_to_all(spread, ('grp', 'dev'), 0, 0, tiled=True)  7.41 us
    reduce_sum x3, other arithmetic, trace_solved(): along_a = jnp.sum(end_rows[:, :, None, None] * solved[None], axis=1)  6.94 us
    mul x2, other arithmetic, apply_one(): one_inverse * face_spectrum(one_transform, low_side, high_side)  4.56 us
    dot_general x6, matrix products, trace_solved(): jnp.einsum('bj,edjk,ck->edbc', transform, planes, transform, precision=FAST)  2.85 us
    dot_general x1, matrix products, spectral(): return jnp.einsum('ck,ijc->ijk', transform, moved, precision=FAST)  2.59 us
    reshape x1, local copies, waits for them, and re-layouts, spectral(): moved = flat.reshape(points, points, points)  2.59 us
  transfers between devices with their start and end apart: 13, of which 3 were waited for; matrix products, arithmetic and copies ran while one was open for 7% of the time, Pallas kernels for 0%

profile of v5, /device:TPU:0, one launch (start us, length us, event | category | flops | bytes accessed | tf_op | source)
XLA Modules:
  0.0 85.4 jit_solution(10135320883322397994)
XLA Ops:
  0.7 0.8 broadcast_add_fusion
  1.7 2.2 %fusion.5 = f32[2,48,2304]{2,1,0:T(8,128)} fusion(bf16[1,1,2,48,2304]{4,3,2,1,0:T(8,128)(2,1)S(1)} %copy-done, f32[1,1,2,48,48]{4,3,2,1,0:T(8,128)} %param.7), kind=kOutput, calls=%fused_computation.15 | convolution fusion | flops 63700992 | bytes 1345536 | tf_op jit(solution)/shard_map/vmap()/dot_general | solution.py:22
  3.8 2.6 %reshape.1195 = f32[2,48,48,48]{3,2,1,0:T(8,128)S(1)} reshape(f32[2,48,2304]{2,1,0:T(8,128)} %fusion.5) | data formatting | bytes 1769472 | tf_op jit(solution)/shard_map/vmap()/reshape | solution.py:23
  6.5 2.0 %fusion.45 = f32[2,48,48,48]{3,2,1,0:T(8,128)S(1)} fusion(f32[2,48,48,48]{3,2,1,0:T(8,128)S(1)} %reshape.1195, f32[1,1,2,48,48]{4,3,2,1,0:T(8,128)S(1)} %copy-done.1), kind=kOutput, calls=%fused_computation.98 | convolution fusion | flops 63700992 | bytes 1787904 | tf_op jit(solution)/shard_map/vmap(bj,ibc->ijc)/dot_general | solution.py:24
  8.5 2.6 %fusion.2 = f32[2,48,48,48]{3,2,1,0:T(8,128)S(1)} fusion(f32[2,48,48,48]{3,2,1,0:T(8,128)S(1)} %fusion.45, f32[2,48]{1,0:T(2,128)S(1)} %bitcast.376, f32[2,48,48]{2,1,0:T(8,128)S(1)} %broadcast_add_fusion, f32[1,1,2,48,48]{4,3,2,1,0:T(8,128)S(1)} %copy-done.1), kind=kOutput, calls=%fused_computation.14 | convolution fusion | flops 64364544 | bytes 1806720 | tf_op jit(solution)/shard_map/vmap(ck,ijc->ijk)/dot_general | solution.py:25
  11.2 2.3 %multiply_reduce_fusion.8 = (f32[2,2,48,48]{3,2,1,0:T(8,128)S(1)}, f32[2,2,48,48]{3,2,1,0:T(8,128)S(1)}, f32[2,2,48,48]{3,2,1,0:T(8,128)S(1)}) fusion(f32[2,48,48,48]{3,2,1,0:T(8,128)S(1)} %fusion.2, f32[2,2,48]{2,1,0:T(2,128)S(1)} %copy.340), kind=kLoop, calls=%fused_computation.8 | loop fusion | flops 2626560 | bytes 996096 | tf_op jit(solution)/shard_map/vmap()/reduce_sum | solution.py:51
  15.4 4.5 %collective-permute-start.2 = (f32[2,2304]{1,0:T(2,128)S(1)}, f32[2,2304]{1,0:T(2,128)S(1)}, u32[]{:S(2)}, u32[]{:S(2)}) collective-permute-start(f32[2,2304]{1,0:T(2,128)S(1)} %get-tuple-element.14), channel_id=1, source_target_pairs={{1,0},{2,1},{3,2},{4,3},{5,4},{6,5},{7,6},{0,7},{9,8},{10,9},{11,1... | collective-permute-start | bytes 55304 | tf_op jit(solution)/shard_map/ppermute | solution.py:13
  19.9 2.4 %collective-permute-start.3 = (f32[2,2304]{1,0:T(2,128)S(1)}, f32[2,2304]{1,0:T(2,128)S(1)}, u32[]{:S(2)}, u32[]{:S(2)}) collective-permute-start(f32[2,2304]{1,0:T(2,128)S(1)} %get-tuple-element.15), channel_id=1, source_target_pairs={{8,0},{16,8},{24,16},{0,24},{9,1},{17,9},{25,17},{1,25},{10,2},{18... | collective-permute-start | bytes 55304 | tf_op jit(solution)/shard_map/ppermute | solution.py:13
  23.1 6.4 %all-to-all-start = ((f32[32,1,12]{2,1,0:T(1,128)}), f32[32,1,12]{2,1,0:T(1,128)S(1)}, u32[]{:S(2)}, u32[]{:S(2)}) async-start(f32[32,1,12]{2,1,0:T(1,128)} %broadcast_in_dim.6), calls=%async_computation | async-start | bytes 32768 | tf_op jit(solution)/shard_map/all_to_all | solution.py:118
  31.0 5.4 %all-to-all-done = f32[32,1,12]{2,1,0:T(1,128)S(1)} async-done(((f32[32,1,12]{2,1,0:T(1,128)}), f32[32,1,12]{2,1,0:T(1,128)S(1)}, u32[]{:S(2)}, u32[]{:S(2)}) %all-to-all-start) | async-done | bytes 1568 | tf_op jit(solution)/shard_map/all_to_all | solution.py:118
  39.6 2.3 %add_multiply_fusion.1 = f32[2,48,48,48]{3,2,1,0:T(8,128)S(1)} fusion(f32[2,48,48]{2,1,0:T(8,128)S(1)} %get-tuple-element.66, f32[2,48]{1,0:T(2,128)S(1)} %bitcast.365, f32[2,48,48]{2,1,0:T(8,128)S(1)} %get-tuple-element.67, f32[2,48]{1,0:T(2,128)S(1)} %bitcast.362, f32[2,48,48]{2,1,0:T(8,128)S(1)} %get-tuple-element.68, ...), kind=kLoop, calls=%fused_computation.12 | loop fusion | flops 3096576 | bytes 1014912 | tf_op jit(solution)/shard_map/vmap()/mul | solution.py:65
  41.9 2.3 %multiply_reduce_fusion.5 = (f32[2,2,48,48]{3,2,1,0:T(8,128)S(1)}, f32[2,2,48,48]{3,2,1,0:T(8,128)S(1)}, f32[2,2,48,48]{3,2,1,0:T(8,128)S(1)}) fusion(f32[2,48,48,48]{3,2,1,0:T(8,128)S(1)} %add_multiply_fusion.1, f32[2,2,48]{2,1,0:T(2,128)S(1)} %copy.340), kind=kLoop, calls=%fused_computation.5 | loop fusion | flops 2626560 | bytes 996096 | tf_op jit(solution)/shard_map/vmap()/reduce_sum | solution.py:51
  47.1 2.5 %all-to-all-start.1 = ((f32[32,1,14]{2,1,0:T(1,128)}), f32[32,1,14]{2,1,0:T(1,128)S(1)}, u32[]{:S(2)}, u32[]{:S(2)}) async-start(f32[32,1,14]{2,1,0:T(1,128)} %broadcast_in_dim.7), calls=%async_computation.1 | async-start | bytes 32768 | tf_op jit(solution)/shard_map/all_to_all | solution.py:118
  49.8 1.7 %collective-permute-start.7 = (f32[2,2304]{1,0:T(2,128)S(1)}, f32[2,2304]{1,0:T(2,128)S(1)}, u32[]{:S(2)}, u32[]{:S(2)}) collective-permute-start(f32[2,2304]{1,0:T(2,128)S(1)} %get-tuple-element.19), channel_id=1, source_target_pairs={{24,0},{0,8},{8,16},{16,24},{25,1},{1,9},{9,17},{17,25},{26,2},{2,... | collective-permute-start | bytes 55304 | tf_op jit(solution)/shard_map/ppermute | solution.py:13
  51.5 3.1 %collective-permute-start.4 = (f32[2,2304]{1,0:T(2,128)S(1)}, f32[2,2304]{1,0:T(2,128)S(1)}, u32[]{:S(2)}, u32[]{:S(2)}) collective-permute-start(f32[2,2304]{1,0:T(2,128)S(1)} %get-tuple-element.16), channel_id=1, source_target_pairs={{1,0},{2,1},{3,2},{4,3},{5,4},{6,5},{7,6},{0,7},{9,8},{10,9},{11,1... | collective-permute-start | bytes 55304 | tf_op jit(solution)/shard_map/ppermute | solution.py:13
  54.6 1.3 %collective-permute-start.5 = (f32[2,2304]{1,0:T(2,128)S(1)}, f32[2,2304]{1,0:T(2,128)S(1)}, u32[]{:S(2)}, u32[]{:S(2)}) collective-permute-start(f32[2,2304]{1,0:T(2,128)S(1)} %get-tuple-element.17), channel_id=1, source_target_pairs={{8,0},{16,8},{24,16},{0,24},{9,1},{17,9},{25,17},{1,25},{10,2},{18... | collective-permute-start | bytes 55304 | tf_op jit(solution)/shard_map/ppermute | solution.py:13
  55.9 0.8 all-to-all-done.1
  61.4 2.3 %add_multiply_fusion = f32[2,48,48,48]{3,2,1,0:T(8,128)S(1)} fusion(f32[2,48,48]{2,1,0:T(8,128)S(1)} %get-tuple-element.60, f32[2,48,48]{2,1,0:T(8,128)S(1)} %get-tuple-element.61, f32[2,48,48]{2,1,0:T(8,128)S(1)} %get-tuple-element.62, f32[2,48,48]{2,1,0:T(8,128)S(1)} %get-tuple-element.63, f32[2,48,48]{2,1,0:T(8,128)S(1)} %get-tuple-element.64, ...), kind=kLoop, calls=%fused_computation.11 | loop fusion | flops 3096576 | bytes 1014912 | tf_op jit(solution)/shard_map/vmap()/mul | solution.py:65
  63.7 2.3 %multiply_reduce_fusion.2 = (f32[2,2,48,48]{3,2,1,0:T(8,128)S(1)}, f32[2,2,48,48]{3,2,1,0:T(8,128)S(1)}, f32[2,2,48,48]{3,2,1,0:T(8,128)S(1)}) fusion(f32[2,48,48,48]{3,2,1,0:T(8,128)S(1)} %add_multiply_fusion, f32[2,2,48]{2,1,0:T(2,128)S(1)} %copy.340), kind=kLoop, calls=%fused_computation.2 | loop fusion | flops 2626560 | bytes 996096 | tf_op jit(solution)/shard_map/vmap()/reduce_sum | solution.py:51
  68.7 2.5 %all-to-all-start.2 = ((f32[32,1,4]{2,1,0:T(1,128)}), f32[32,1,4]{2,1,0:T(1,128)S(1)}, u32[]{:S(2)}, u32[]{:S(2)}) async-start(f32[32,1,4]{2,1,0:T(1,128)} %broadcast_in_dim.8), calls=%async_computation.2 | async-start | bytes 32768 | tf_op jit(solution)/shard_map/all_to_all | solution.py:118
  71.3 3.4 %collective-permute-start.8 = (f32[2,2304]{1,0:T(2,128)S(1)}, f32[2,2304]{1,0:T(2,128)S(1)}, u32[]{:S(2)}, u32[]{:S(2)}) collective-permute-start(f32[2,2304]{1,0:T(2,128)S(1)} %get-tuple-element.20), channel_id=1, source_target_pairs={{1,0},{2,1},{3,2},{4,3},{5,4},{6,5},{7,6},{0,7},{9,8},{10,9},{11,1... | collective-permute-start | bytes 55304 | tf_op jit(solution)/shard_map/ppermute | solution.py:13
  74.7 2.4 %collective-permute-start.9 = (f32[2,2304]{1,0:T(2,128)S(1)}, f32[2,2304]{1,0:T(2,128)S(1)}, u32[]{:S(2)}, u32[]{:S(2)}) collective-permute-start(f32[2,2304]{1,0:T(2,128)S(1)} %get-tuple-element.21), channel_id=1, source_target_pairs={{8,0},{16,8},{24,16},{0,24},{9,1},{17,9},{25,17},{1,25},{10,2},{18... | collective-permute-start | bytes 55304 | tf_op jit(solution)/shard_map/ppermute | solution.py:13
  77.2 1.2 %all-to-all-done.2 = f32[32,1,4]{2,1,0:T(1,128)S(1)} async-done(((f32[32,1,4]{2,1,0:T(1,128)}), f32[32,1,4]{2,1,0:T(1,128)S(1)}, u32[]{:S(2)}, u32[]{:S(2)}) %all-to-all-start.2) | async-done | bytes 544 | tf_op jit(solution)/shard_map/all_to_all | solution.py:118
  84.1 0.7 copy.410
  (197 shorter events, 18.1 us)
Async XLA Ops:
  0.6 1.1 %copy-start = (bf16[1,1,2,48,2304]{4,3,2,1,0:T(8,128)(2,1)S(1)}, bf16[1,1,2,48,2304]{4,3,2,1,0:T(8,128)(2,1)}, u32[]{:S(2)}) copy-start(bf16[1,1,2,48,2304]{4,3,2,1,0:T(8,128)(2,1)} %param.6) | copy-start | bytes 1327108
  0.6 5.8 %copy-start.1 = (f32[1,1,2,48,48]{4,3,2,1,0:T(8,128)S(1)}, f32[1,1,2,48,48]{4,3,2,1,0:T(8,128)}, u32[]{:S(2)}) copy-start(f32[1,1,2,48,48]{4,3,2,1,0:T(8,128)} %param.7) | copy-start | bytes 55300
  6.4 2.1 %copy-start.3 = (f32[1,1,2,48]{3,2,1,0:T(2,128)S(1)}, f32[1,1,2,48]{3,2,1,0:T(2,128)}, u32[]{:S(2)}) copy-start(f32[1,1,2,48]{3,2,1,0:T(2,128)} %param.8) | copy-start | bytes 1156
  11.1 4.0 %copy-start.4 = (f32[1,1,2,3]{3,2,1,0:T(2,128)S(1)}, f32[1,1,2,3]{3,2,1,0:T(2,128)}, u32[]{:S(2)}) copy-start(f32[1,1,2,3]{3,2,1,0:T(2,128)} %param.9) | copy-start | bytes 76
  11.1 4.0 %copy-start.5 = (f32[1,1,6,48]{3,1,2,0:T(1,128)S(1)}, f32[1,1,6,48]{3,1,2,0:T(1,128)}, u32[]{:S(2)}) copy-start(f32[1,1,6,48]{3,1,2,0:T(1,128)} %param.11) | copy-start | bytes 3460
  11.2 18.4 %copy-start.2 = (s32[4,8]{1,0:T(4,128)S(1)}, s32[4,8]{1,0:T(4,128)}, u32[]{:S(2)}) copy-start(s32[4,8]{1,0:T(4,128)} %param.10) | copy-start | bytes 388
  15.4 21.9 %collective-permute-start.2 = (f32[2,2304]{1,0:T(2,128)S(1)}, f32[2,2304]{1,0:T(2,128)S(1)}, u32[]{:S(2)}, u32[]{:S(2)}) collective-permute-start(f32[2,2304]{1,0:T(2,128)S(1)} %get-tuple-element.14), channel_id=1, source_target_pairs={{1,0},{2,1},{3,2},{4,3},{5,4},{6,5},{7,6},{0,7},{9,8},{10,9},{11,1... | collective-permute-start | bytes 55304 | tf_op jit(solution)/shard_map/ppermute | solution.py:13
  19.9 17.4 %collective-permute-start.3 = (f32[2,2304]{1,0:T(2,128)S(1)}, f32[2,2304]{1,0:T(2,128)S(1)}, u32[]{:S(2)}, u32[]{:S(2)}) collective-permute-start(f32[2,2304]{1,0:T(2,128)S(1)} %get-tuple-element.15), channel_id=1, source_target_pairs={{8,0},{16,8},{24,16},{0,24},{9,1},{17,9},{25,17},{1,25},{10,2},{18... | collective-permute-start | bytes 55304 | tf_op jit(solution)/shard_map/ppermute | solution.py:13
  22.4 15.0 %collective-permute-start.1 = (f32[2,2353]{1,0:T(2,128)S(1)}, f32[2,2353]{1,0:T(2,128)S(1)}, u32[]{:S(2)}, u32[]{:S(2)}) collective-permute-start(f32[2,2353]{1,0:T(2,128)S(1)} %concatenate.244), channel_id=1, source_target_pairs={{24,0},{0,8},{8,16},{16,24},{25,1},{1,9},{9,17},{17,25},{26,2},{2,... | collective-permute-start | bytes 56480 | tf_op jit(solution)/shard_map/ppermute | solution.py:13
  22.4 15.1 %collective-permute-start = (f32[2,2353]{1,0:T(2,128)S(1)}, f32[2,2353]{1,0:T(2,128)S(1)}, u32[]{:S(2)}, u32[]{:S(2)}) collective-permute-start(f32[2,2353]{1,0:T(2,128)S(1)} %concatenate.243), channel_id=1, source_target_pairs={{7,0},{0,1},{1,2},{2,3},{3,4},{4,5},{5,6},{6,7},{15,8},{8,9},{9,10... | collective-permute-start | bytes 56480 | tf_op jit(solution)/shard_map/ppermute | solution.py:13
  23.1 13.3 %all-to-all-start = ((f32[32,1,12]{2,1,0:T(1,128)}), f32[32,1,12]{2,1,0:T(1,128)S(1)}, u32[]{:S(2)}, u32[]{:S(2)}) async-start(f32[32,1,12]{2,1,0:T(1,128)} %broadcast_in_dim.6), calls=%async_computation | async-start | bytes 32768 | tf_op jit(solution)/shard_map/all_to_all | solution.py:118
  47.1 9.7 %all-to-all-start.1 = ((f32[32,1,14]{2,1,0:T(1,128)}), f32[32,1,14]{2,1,0:T(1,128)S(1)}, u32[]{:S(2)}, u32[]{:S(2)}) async-start(f32[32,1,14]{2,1,0:T(1,128)} %broadcast_in_dim.7), calls=%async_computation.1 | async-start | bytes 32768 | tf_op jit(solution)/shard_map/all_to_all | solution.py:118
  49.7 10.6 %collective-permute-start.6 = (f32[2,2304]{1,0:T(2,128)S(1)}, f32[2,2304]{1,0:T(2,128)S(1)}, u32[]{:S(2)}, u32[]{:S(2)}) collective-permute-start(f32[2,2304]{1,0:T(2,128)S(1)} %get-tuple-element.18), channel_id=1, source_target_pairs={{7,0},{0,1},{1,2},{2,3},{3,4},{4,5},{5,6},{6,7},{15,8},{8,9},{9,10... | collective-permute-start | bytes 55304 | tf_op jit(solution)/shard_map/ppermute | solution.py:13
  49.8 10.4 %collective-permute-start.7 = (f32[2,2304]{1,0:T(2,128)S(1)}, f32[2,2304]{1,0:T(2,128)S(1)}, u32[]{:S(2)}, u32[]{:S(2)}) collective-permute-start(f32[2,2304]{1,0:T(2,128)S(1)} %get-tuple-element.19), channel_id=1, source_target_pairs={{24,0},{0,8},{8,16},{16,24},{25,1},{1,9},{9,17},{17,25},{26,2},{2,... | collective-permute-start | bytes 55304 | tf_op jit(solution)/shard_map/ppermute | solution.py:13
  51.5 8.5 %collective-permute-start.4 = (f32[2,2304]{1,0:T(2,128)S(1)}, f32[2,2304]{1,0:T(2,128)S(1)}, u32[]{:S(2)}, u32[]{:S(2)}) collective-permute-start(f32[2,2304]{1,0:T(2,128)S(1)} %get-tuple-element.16), channel_id=1, source_target_pairs={{1,0},{2,1},{3,2},{4,3},{5,4},{6,5},{7,6},{0,7},{9,8},{10,9},{11,1... | collective-permute-start | bytes 55304 | tf_op jit(solution)/shard_map/ppermute | solution.py:13
  54.6 5.4 %collective-permute-start.5 = (f32[2,2304]{1,0:T(2,128)S(1)}, f32[2,2304]{1,0:T(2,128)S(1)}, u32[]{:S(2)}, u32[]{:S(2)}) collective-permute-start(f32[2,2304]{1,0:T(2,128)S(1)} %get-tuple-element.17), channel_id=1, source_target_pairs={{8,0},{16,8},{24,16},{0,24},{9,1},{17,9},{25,17},{1,25},{10,2},{18... | collective-permute-start | bytes 55304 | tf_op jit(solution)/shard_map/ppermute | solution.py:13
  68.7 9.6 %all-to-all-start.2 = ((f32[32,1,4]{2,1,0:T(1,128)}), f32[32,1,4]{2,1,0:T(1,128)S(1)}, u32[]{:S(2)}, u32[]{:S(2)}) async-start(f32[32,1,4]{2,1,0:T(1,128)} %broadcast_in_dim.8), calls=%async_computation.2 | async-start | bytes 32768 | tf_op jit(solution)/shard_map/all_to_all | solution.py:118
  71.3 12.1 %collective-permute-start.8 = (f32[2,2304]{1,0:T(2,128)S(1)}, f32[2,2304]{1,0:T(2,128)S(1)}, u32[]{:S(2)}, u32[]{:S(2)}) collective-permute-start(f32[2,2304]{1,0:T(2,128)S(1)} %get-tuple-element.20), channel_id=1, source_target_pairs={{1,0},{2,1},{3,2},{4,3},{5,4},{6,5},{7,6},{0,7},{9,8},{10,9},{11,1... | collective-permute-start | bytes 55304 | tf_op jit(solution)/shard_map/ppermute | solution.py:13
  74.7 8.7 %collective-permute-start.9 = (f32[2,2304]{1,0:T(2,128)S(1)}, f32[2,2304]{1,0:T(2,128)S(1)}, u32[]{:S(2)}, u32[]{:S(2)}) collective-permute-start(f32[2,2304]{1,0:T(2,128)S(1)} %get-tuple-element.21), channel_id=1, source_target_pairs={{8,0},{16,8},{24,16},{0,24},{9,1},{17,9},{25,17},{1,25},{10,2},{18... | collective-permute-start | bytes 55304 | tf_op jit(solution)/shard_map/ppermute | solution.py:13

commit v6 on v3

--- a/solution.py
+++ b/solution.py
@@ -64,6 +64,55 @@
     return trace_solved(
         one_transform, one_inverse * face_spectrum(one_transform, low_side, high_side)
     )
+
+
+def side_by_side(blocks):
+    return jnp.concatenate([blocks[0], blocks[1]], axis=-1)
+
+
+def solve_pair(transforms, wide_inverse, low_side, high_side):
+    slots, points = transforms.shape[0], transforms.shape[1]
+    planes = jnp.stack([low_side, high_side], axis=1).reshape(slots, 2, 3, points, points)
+    hats = jnp.einsum(
+        "sbj,sedbc,sck->sedjk", transforms, planes, transforms, precision=FAST
+    )
+    ends = jnp.stack([transforms[:, 0], transforms[:, points - 1]], axis=1)
+    wide_rows = [
+        side_by_side(jnp.broadcast_to(ends[:, e, :, None], (slots, points, points)))
+        for e in range(2)
+    ]
+    wide_cols = [side_by_side(ends[:, e]) for e in range(2)]
+    lane = lax.broadcasted_iota(jnp.int32, (1, 1, slots * points), 2)
+    result = 0.0
+    for e in range(2):
+        result = result + wide_rows[e][:, None, :] * side_by_side(hats[:, e, 0])[None, :, :]
+        result = result + wide_rows[e][None, :, :] * side_by_side(hats[:, e, 1])[:, None, :]
+        third = jnp.where(lane < points, hats[0, e, 2][:, :, None], hats[1, e, 2][:, :, None])
+        result = result + wide_cols[e][None, None, :] * third
+    solved = wide_inverse * result
+    along_a = [jnp.sum(wide_rows[e][:, None, :] * solved, axis=0) for e in range(2)]
+    along_b = [jnp.sum(wide_rows[e][None, :, :] * solved, axis=1) for e in range(2)]
+    weighted = [wide_cols[e][None, None, :] * solved for e in range(2)]
+    along_c = [
+        [jnp.sum(weighted[e][:, :, :points], axis=2), jnp.sum(weighted[e][:, :, points:], axis=2)]
+        for e in range(2)
+    ]
+    out = []
+    for slot in range(slots):
+        cut = slice(slot * points, (slot + 1) * points)
+        out.append(
+            jnp.stack(
+                [
+                    jnp.stack([along_a[e][:, cut], along_b[e][:, cut], along_c[e][slot]])
+                    for e in range(2)
+                ]
+            )
+        )
+    planes_out = jnp.stack(out)
+    traces = jnp.einsum(
+        "sbj,sedjk,sck->sedbc", transforms, planes_out, transforms, precision=FAST
+    )
+    return traces.reshape(slots, 2, 3, points * points)
 
 
 def slot_before(vector):
@@ -110,7 +159,7 @@
     )
 
     inverses = jax.vmap(inverse_diagonal)(diagonals)
-    solver = jax.vmap(apply_one)
+    wide_inverse = side_by_side(inverses)
 
     def gather_all(payload):
         count = groups * owners
@@ -172,7 +221,7 @@
 
     def solve(v_own, v_in):
         preceding = jnp.stack([v_in[:, 0], v_in[:, 1], slot_before(v_own[:, 2])], axis=1)
-        return solver(transforms, inverses, -preceding, v_own)
+        return solve_pair(transforms, wide_inverse, -preceding, v_own)
 
     def split_terms(v_own, v_in, traces_now):
         low_side = traces_now[:, 0]

time: 85.3 us -> 129 us (1.51); the launches traced: 84.9 us -> 127 us
  local copies, waits for them, and re-layouts: 12.9 us -> 39.5 us
  other arithmetic: 15.7 us -> 27.9 us
  starting transfers between devices: 30.3 us -> 36 us
  waiting for transfers between devices: 7.45 us -> 1.91 us
  matrix products: 11.3 us -> 13.6 us
    unnamed x15 -> x163, local copies, waits for them, and re-layouts: 1.42 us -> 14.2 us
    reduce_sum x0 -> x6, other arithmetic: none -> 7.85 us  [the longest x4 4.61 us: solve_pair(): jnp.sum(weighted[e][:, :, :points], axis=2)]
    all_to_all x3, starting transfers between devices: 11.3 us -> 18.5 us  [gather_all(): got = lax.all_to_all(spread, ('grp', 'dev'), 0, 0, tiled=True)]
    slice x1 -> x9, local copies, waits for them, and re-layouts: 0.01 us -> 6.27 us  [the longest x4 3.15 us: solve_pair(): along_b[e][:, cut]]
    all_to_all x3, waiting for transfers between devices: 7.42 us -> 1.89 us  [gather_all(): got = lax.all_to_all(spread, ('grp', 'dev'), 0, 0, tiled=True)]
    reduce_sum x3 -> x1, other arithmetic: 6.94 us -> 2.3 us  [trace_solved(): along_a = jnp.sum(end_rows[:, :, None, None] * solved[None], axis=1)]
    reduce_sum x0 -> x8, local copies, waits for them, and re-layouts: none -> 3.3 us  [the longest x4 1.65 us: solve_pair(): jnp.sum(weighted[e][:, :, :points], axis=2)]
    another operation x1 -> x12, other arithmetic: 0.09 us -> 3.2 us  [the longest x8 3.15 us: solve_pair(): jnp.stack([jnp.stack([along_a[e][:, cut], along_b[e][:, cut], along_c[e][...]
  transfers between devices with their start and end apart: 13 -> 13, of which waited for: 3 -> 2; matrix products, arithmetic and copies ran while one was open for 8% -> 12% of each run, Pallas kernels for 0% -> 0%
where the time goes in v6:
time: 129 us; the launch traced here: 127 us
  local copies, waits for them, and re-layouts  39.5 us (31%)
  starting transfers between devices  36 us (28%)
  other arithmetic  27.9 us (22%)
  matrix products  13.6 us (11%)
  between operations  8.45 us (7%)
  waiting for transfers between devices  1.91 us (1%)
    all_to_all x3, starting transfers between devices, gather_all(): got = lax.all_to_all(spread, ('grp', 'dev'), 0, 0, tiled=True)  18.5 us
    ppermute x10, starting transfers between devices, shifted(): return lax.ppermute(block, axis, route)  17.4 us
    unnamed x163, local copies, waits for them, and re-layouts  14.2 us
    mul x2, other arithmetic, solve_pair(): weighted = [wide_cols[e][None, None, :] * solved for e in range(2)]  5.85 us
    reduce_sum x4, other arithmetic, solve_pair(): jnp.sum(weighted[e][:, :, :points], axis=2)  4.61 us
    reshape x1, local copies, waits for them, and re-layouts, spectral(): spatial = patch_load.astype(jnp.float32).reshape(points, points, points)  3.4 us
    reduce_sum x2, other arithmetic, solve_pair(): jnp.sum(wide_rows[e][:, None, :] * solved, axis=0)  3.25 us
    slice x4, local copies, waits for them, and re-layouts, solve_pair(): along_b[e][:, cut]  3.15 us
  transfers between devices with their start and end apart: 13, of which 2 were waited for; matrix products, arithmetic and copies ran while one was open for 12% of the time, Pallas kernels for 0%

profile of v6, /device:TPU:0, one launch (start us, length us, event | category | flops | bytes accessed | tf_op | source)
XLA Modules:
  0.0 127.2 jit_solution(7637120230703784203)
XLA Ops:
  2.3 3.4 %reshape.1172 = bf16[2,48,48,48]{3,2,1,0:T(8,128)(2,1)} reshape(bf16[1,1,2,48,2304]{4,3,2,1,0:T(8,128)(2,1)} %param.6) | data formatting | bytes 884736 | tf_op jit(solution)/shard_map/vmap()/reshape | solution.py:22
  5.7 2.1 %fusion.7 = f32[2,48,48,48]{3,1,2,0:T(8,128)S(1)} fusion(bf16[2,48,48,48]{3,2,1,0:T(8,128)(2,1)} %reshape.1172, f32[1,1,2,48,48]{4,3,2,1,0:T(8,128)S(1)} %copy-done), kind=kOutput, calls=%fused_computation.20 | convolution fusion | flops 63700992 | bytes 1345536 | tf_op jit(solution)/shard_map/vmap(ai,abc->ibc)/dot_general | solution.py:23
  7.8 2.2 %fusion.2 = f32[2,48,48,48]{3,2,1,0:T(8,128)S(1)} fusion(f32[2,48,48,48]{3,1,2,0:T(8,128)S(1)} %fusion.7, f32[1,1,2,48,48]{4,3,2,1,0:T(8,128)S(1)} %copy-done), kind=kOutput, calls=%fused_computation.5 | convolution fusion | flops 63700992 | bytes 1787904 | tf_op jit(solution)/shard_map/vmap(bj,ibc->ijc)/dot_general | solution.py:24
  10.0 2.5 %fusion.4 = f32[2,48,48,48]{3,2,1,0:T(8,128)S(1)} fusion(f32[2,48,48,48]{3,2,1,0:T(8,128)S(1)} %fusion.2, f32[2,48]{1,0:T(2,128)S(1)} %bitcast.501, f32[2,48,48]{2,1,0:T(8,128)S(1)} %broadcast_add_fusion, f32[1,1,2,48,48]{4,3,2,1,0:T(8,128)S(1)} %copy-done), kind=kOutput, calls=%fused_computation.8 | convolution fusion | flops 64364544 | bytes 1806720 | tf_op jit(solution)/shard_map/vmap(ck,ijc->ijk)/dot_general | solution.py:25
  12.5 2.3 %multiply_reduce_fusion.2 = (f32[2,2,48,48]{3,2,1,0:T(8,128)S(1)}, f32[2,2,48,48]{3,2,1,0:T(8,128)S(1)}, f32[2,2,48,48]{3,2,1,0:T(8,128)S(1)}) fusion(f32[2,48,48,48]{3,2,1,0:T(8,128)S(1)} %fusion.4, f32[2,2,48]{2,1,0:T(2,128)S(1)} %copy.425), kind=kLoop, calls=%fused_computation.2 | loop fusion | flops 2626560 | bytes 996096 | tf_op jit(solution)/shard_map/vmap()/reduce_sum | solution.py:51
  16.9 7.3 %all-to-all-start = ((f32[32,1,12]{2,1,0:T(1,128)}), f32[32,1,12]{2,1,0:T(1,128)S(1)}, u32[]{:S(2)}, u32[]{:S(2)}) async-start(f32[32,1,12]{2,1,0:T(1,128)} %broadcast_in_dim.195), calls=%async_computation | async-start | bytes 32768 | tf_op jit(solution)/shard_map/all_to_all | solution.py:167
  24.9 3.4 %collective-permute-start.2 = (f32[2,2304]{1,0:T(2,128)S(1)}, f32[2,2304]{1,0:T(2,128)S(1)}, u32[]{:S(2)}, u32[]{:S(2)}) collective-permute-start(f32[2,2304]{1,0:T(2,128)S(1)} %get-tuple-element.14), channel_id=1, source_target_pairs={{1,0},{2,1},{3,2},{4,3},{5,4},{6,5},{7,6},{0,7},{9,8},{10,9},{11,1... | collective-permute-start | bytes 55304 | tf_op jit(solution)/shard_map/ppermute | solution.py:13
  28.2 2.4 %collective-permute-start.3 = (f32[2,2304]{1,0:T(2,128)S(1)}, f32[2,2304]{1,0:T(2,128)S(1)}, u32[]{:S(2)}, u32[]{:S(2)}) collective-permute-start(f32[2,2304]{1,0:T(2,128)S(1)} %get-tuple-element.15), channel_id=1, source_target_pairs={{8,0},{16,8},{24,16},{0,24},{9,1},{17,9},{25,17},{1,25},{10,2},{18... | collective-permute-start | bytes 55304 | tf_op jit(solution)/shard_map/ppermute | solution.py:13
  30.8 1.8 %add_divide_fusion = f32[2,48,48,48]{3,2,1,0:T(8,128)} fusion(f32[2,48]{1,0:T(2,128)S(1)} %bitcast.502, f32[2,48,48]{2,1,0:T(8,128)S(1)} %broadcast_add_fusion), kind=kLoop, calls=%fused_computation.7 | loop fusion | flops 442368 | bytes 903552 | tf_op jit(solution)/shard_map/vmap()/div | solution.py:17
  34.0 1.8 %slice_bitcast_fusion.1 = (f32[48,48,48]{2,1,0:T(8,128)S(1)}, f32[48,48,48]{2,1,0:T(8,128)S(1)}) fusion(f32[2,48,48,48]{3,2,1,0:T(8,128)} %add_divide_fusion), kind=kLoop, calls=%fused_computation.18 | loop fusion | bytes 1769472 | tf_op jit(solution)/shard_map/squeeze | solution.py:70
  43.7 2.9 %broadcast_multiply_fusion.3 = (f32[48,48,96]{2,1,0:T(8,128)S(1)}, f32[48,48,96]{2,1,0:T(8,128)}) fusion(f32[96]{0:T(128)S(1)} %get-tuple-element.185, f32[48,48]{1,0:T(8,128)S(1)} %get-tuple-element.93, f32[48,48]{1,0:T(8,128)S(1)} %get-tuple-element.94, f32[96]{0:T(128)S(1)} %get-tuple-element.186, f32[48,96]{1,0:T(8,128)S(1)} %pad_maximum_fusion.7, ...), kind=kLoop, calls=%fused_computation.39 | loop fusion | flops 3538944 | bytes 2802528 | tf_op jit(solution)/shard_map/mul | solution.py:95
  49.0 2.6 %multiply_reduce_fusion.10 = (f32[48,96]{1,0:T(8,128)S(1)}, f32[48,96]{1,0:T(8,128)}, f32[48,96]{1,0:T(8,128)}, f32[48,96]{1,0:T(8,128)}, f32[48,48,96]{2,1,0:T(8,128)S(1)}) fusion(f32[48,48,96]{2,1,0:T(8,128)} %get-tuple-element.73, f32[48,96]{1,0:T(8,128)} %copy-done.3, f32[48,96]{1,0:T(8,128)} %copy-done.5, f32[96]{0:T(128)} %copy-done.45), kind=kLoop, calls=%fused_computation.30 | loop fusion | flops 1972224 | bytes 1880448 | tf_op jit(solution)/shard_map/reduce_sum | solution.py:93
  55.2 1.5 %fusion.117 = (f32[48,48]{1,0:T(8,128)}, f32[48,48]{1,0:T(8,128)}) fusion(f32[48,96]{1,0:T(8,128)} %get-tuple-element.42), kind=kLoop, calls=%fused_computation.315 | loop fusion | bytes 36864 | tf_op jit(solution)/shard_map/slice | solution.py:106
  56.6 1.4 %copy.563 = f32[48,48]{0,1:T(8,128)} copy(f32[48,48]{1,0:T(8,128)} %get-tuple-element.145) | data formatting | bytes 18432
  59.5 1.5 %fusion.119 = (f32[48,48]{1,0:T(8,128)}, f32[48,48]{1,0:T(8,128)}) fusion(f32[48,96]{1,0:T(8,128)} %get-tuple-element.55), kind=kLoop, calls=%fused_computation.317 | loop fusion | bytes 36864 | tf_op jit(solution)/shard_map/slice | solution.py:106
  63.8 1.5 %fusion.118 = (f32[48,48]{1,0:T(8,128)}, f32[48,48]{1,0:T(8,128)}) fusion(f32[48,96]{1,0:T(8,128)} %get-tuple-element.56), kind=kLoop, calls=%fused_computation.316 | loop fusion | bytes 36864 | tf_op jit(solution)/shard_map/slice | solution.py:106
  68.2 1.6 %slice_reduce_fusion.6 = (f32[48,48]{1,0:T(8,128)}, f32[48,48]{1,0:T(8,128)}) fusion(f32[48,48,96]{2,1,0:T(8,128)S(1)} %get-tuple-element.79), kind=kLoop, calls=%fused_computation.15 | loop fusion | flops 216576 | bytes 903168 | tf_op jit(solution)/shard_map/reduce_sum | solution.py:97
  77.4 6.0 %all-to-all-start.1 = ((f32[32,1,14]{2,1,0:T(1,128)}), f32[32,1,14]{2,1,0:T(1,128)S(1)}, u32[]{:S(2)}, u32[]{:S(2)}) async-start(f32[32,1,14]{2,1,0:T(1,128)} %broadcast_in_dim.209), calls=%async_computation.1 | async-start | bytes 32768 | tf_op jit(solution)/shard_map/all_to_all | solution.py:167
  84.0 3.4 %collective-permute-start.4 = (f32[2,2304]{1,0:T(2,128)S(1)}, f32[2,2304]{1,0:T(2,128)S(1)}, u32[]{:S(2)}, u32[]{:S(2)}) collective-permute-start(f32[2,2304]{1,0:T(2,128)S(1)} %get-tuple-element.16), channel_id=1, source_target_pairs={{1,0},{2,1},{3,2},{4,3},{5,4},{6,5},{7,6},{0,7},{9,8},{10,9},{11,1... | collective-permute-start | bytes 55304 | tf_op jit(solution)/shard_map/ppermute | solution.py:13
  87.4 2.4 %collective-permute-start.5 = (f32[2,2304]{1,0:T(2,128)S(1)}, f32[2,2304]{1,0:T(2,128)S(1)}, u32[]{:S(2)}, u32[]{:S(2)}) collective-permute-start(f32[2,2304]{1,0:T(2,128)S(1)} %get-tuple-element.17), channel_id=1, source_target_pairs={{8,0},{16,8},{24,16},{0,24},{9,1},{17,9},{25,17},{1,25},{10,2},{18... | collective-permute-start | bytes 55304 | tf_op jit(solution)/shard_map/ppermute | solution.py:13
  97.8 2.9 %broadcast_multiply_fusion.2 = (f32[48,48,96]{2,1,0:T(8,128)S(1)}, f32[48,48,96]{2,1,0:T(8,128)}) fusion(f32[96]{0:T(128)S(1)} %copy-done.55, f32[48,48]{1,0:T(8,128)S(1)} %get-tuple-element.81, f32[48,48]{1,0:T(8,128)S(1)} %get-tuple-element.82, f32[96]{0:T(128)S(1)} %copy-done.46, f32[48,96]{1,0:T(8,128)S(1)} %pad_maximum_fusion.11, ...), kind=kLoop, calls=%fused_computation.38 | loop fusion | flops 3538944 | bytes 2802528 | tf_op jit(solution)/shard_map/mul | solution.py:95
  107.6 5.3 %all-to-all-start.2 = ((f32[32,1,4]{2,1,0:T(1,128)}), f32[32,1,4]{2,1,0:T(1,128)S(1)}, u32[]{:S(2)}, u32[]{:S(2)}) async-start(f32[32,1,4]{2,1,0:T(1,128)} %broadcast_in_dim.218), calls=%async_computation.2 | async-start | bytes 32768 | tf_op jit(solution)/shard_map/all_to_all | solution.py:167
  113.0 3.4 %collective-permute-start.8 = (f32[2,2304]{1,0:T(2,128)S(1)}, f32[2,2304]{1,0:T(2,128)S(1)}, u32[]{:S(2)}, u32[]{:S(2)}) collective-permute-start(f32[2,2304]{1,0:T(2,128)S(1)} %get-tuple-element.20), channel_id=1, source_target_pairs={{1,0},{2,1},{3,2},{4,3},{5,4},{6,5},{7,6},{0,7},{9,8},{10,9},{11,1... | collective-permute-start | bytes 55304 | tf_op jit(solution)/shard_map/ppermute | solution.py:13
  116.4 2.4 %collective-permute-start.9 = (f32[2,2304]{1,0:T(2,128)S(1)}, f32[2,2304]{1,0:T(2,128)S(1)}, u32[]{:S(2)}, u32[]{:S(2)}) collective-permute-start(f32[2,2304]{1,0:T(2,128)S(1)} %get-tuple-element.21), channel_id=1, source_target_pairs={{8,0},{16,8},{24,16},{0,24},{9,1},{17,9},{25,17},{1,25},{10,2},{18... | collective-permute-start | bytes 55304 | tf_op jit(solution)/shard_map/ppermute | solution.py:13
  (391 shorter events, 50.8 us)
Async XLA Ops:
  16.9 20.0 %all-to-all-start = ((f32[32,1,12]{2,1,0:T(1,128)}), f32[32,1,12]{2,1,0:T(1,128)S(1)}, u32[]{:S(2)}, u32[]{:S(2)}) async-start(f32[32,1,12]{2,1,0:T(1,128)} %broadcast_in_dim.195), calls=%async_computation | async-start | bytes 32768 | tf_op jit(solution)/shard_map/all_to_all | solution.py:167
  24.9 13.2 %collective-permute-start.2 = (f32[2,2304]{1,0:T(2,128)S(1)}, f32[2,2304]{1,0:T(2,128)S(1)}, u32[]{:S(2)}, u32[]{:S(2)}) collective-permute-start(f32[2,2304]{1,0:T(2,128)S(1)} %get-tuple-element.14), channel_id=1, source_target_pairs={{1,0},{2,1},{3,2},{4,3},{5,4},{6,5},{7,6},{0,7},{9,8},{10,9},{11,1... | collective-permute-start | bytes 55304 | tf_op jit(solution)/shard_map/ppermute | solution.py:13
  28.2 9.9 %collective-permute-start.3 = (f32[2,2304]{1,0:T(2,128)S(1)}, f32[2,2304]{1,0:T(2,128)S(1)}, u32[]{:S(2)}, u32[]{:S(2)}) collective-permute-start(f32[2,2304]{1,0:T(2,128)S(1)} %get-tuple-element.15), channel_id=1, source_target_pairs={{8,0},{16,8},{24,16},{0,24},{9,1},{17,9},{25,17},{1,25},{10,2},{18... | collective-permute-start | bytes 55304 | tf_op jit(solution)/shard_map/ppermute | solution.py:13
  30.7 10.2 %collective-permute-start = (f32[2,2353]{1,0:T(2,128)S(1)}, f32[2,2353]{1,0:T(2,128)S(1)}, u32[]{:S(2)}, u32[]{:S(2)}) collective-permute-start(f32[2,2353]{1,0:T(2,128)S(1)} %concatenate.279), channel_id=1, source_target_pairs={{7,0},{0,1},{1,2},{2,3},{3,4},{4,5},{5,6},{6,7},{15,8},{8,9},{9,10... | collective-permute-start | bytes 56480 | tf_op jit(solution)/shard_map/ppermute | solution.py:13
  30.7 10.3 %collective-permute-start.1 = (f32[2,2353]{1,0:T(2,128)S(1)}, f32[2,2353]{1,0:T(2,128)S(1)}, u32[]{:S(2)}, u32[]{:S(2)}) collective-permute-start(f32[2,2353]{1,0:T(2,128)S(1)} %concatenate.280), channel_id=1, source_target_pairs={{24,0},{0,8},{8,16},{16,24},{25,1},{1,9},{9,17},{17,25},{26,2},{2,... | collective-permute-start | bytes 56480 | tf_op jit(solution)/shard_map/ppermute | solution.py:13
  75.7 19.6 %copy-start.13 = (f32[2,3,2304]{2,0,1:T(2,128)S(1)}, f32[2,3,2304]{2,0,1:T(2,128)}, u32[]{:S(2)}) copy-start(f32[2,3,2304]{2,0,1:T(2,128)} %copy-done.12) | copy-start | bytes 165892
  75.7 19.6 %copy-start.19 = (f32[2,2304]{1,0:T(2,128)S(1)}, f32[2,2304]{1,0:T(2,128)}, u32[]{:S(2)}) copy-start(f32[2,2304]{1,0:T(2,128)} %copy-done.18) | copy-start | bytes 55300
  75.7 19.6 %copy-start.21 = (f32[2,2304]{1,0:T(2,128)S(1)}, f32[2,2304]{1,0:T(2,128)}, u32[]{:S(2)}) copy-start(f32[2,2304]{1,0:T(2,128)} %copy-done.20) | copy-start | bytes 55300
  75.7 19.6 %copy-start.28 = (f32[2,1,2304]{2,0,1:T(2,128)S(1)}, f32[2,1,2304]{2,0,1:T(2,128)}, u32[]{:S(2)}) copy-start(f32[2,1,2304]{2,0,1:T(2,128)} %copy-done.27) | copy-start | bytes 55300
  76.0 19.5 %copy-start.24 = (f32[2,1,3,2304]{3,0,2,1:T(2,128)S(1)}, f32[2,1,3,2304]{3,0,2,1:T(2,128)}, u32[]{:S(2)}) copy-start(f32[2,1,3,2304]{3,0,2,1:T(2,128)} %get-tuple-element.75) | copy-start | bytes 165892
  77.4 13.1 %all-to-all-start.1 = ((f32[32,1,14]{2,1,0:T(1,128)}), f32[32,1,14]{2,1,0:T(1,128)S(1)}, u32[]{:S(2)}, u32[]{:S(2)}) async-start(f32[32,1,14]{2,1,0:T(1,128)} %broadcast_in_dim.209), calls=%async_computation.1 | async-start | bytes 32768 | tf_op jit(solution)/shard_map/all_to_all | solution.py:167
  84.0 11.2 %collective-permute-start.4 = (f32[2,2304]{1,0:T(2,128)S(1)}, f32[2,2304]{1,0:T(2,128)S(1)}, u32[]{:S(2)}, u32[]{:S(2)}) collective-permute-start(f32[2,2304]{1,0:T(2,128)S(1)} %get-tuple-element.16), channel_id=1, source_target_pairs={{1,0},{2,1},{3,2},{4,3},{5,4},{6,5},{7,6},{0,7},{9,8},{10,9},{11,1... | collective-permute-start | bytes 55304 | tf_op jit(solution)/shard_map/ppermute | solution.py:13
  87.4 7.9 %collective-permute-start.5 = (f32[2,2304]{1,0:T(2,128)S(1)}, f32[2,2304]{1,0:T(2,128)S(1)}, u32[]{:S(2)}, u32[]{:S(2)}) collective-permute-start(f32[2,2304]{1,0:T(2,128)S(1)} %get-tuple-element.17), channel_id=1, source_target_pairs={{8,0},{16,8},{24,16},{0,24},{9,1},{17,9},{25,17},{1,25},{10,2},{18... | collective-permute-start | bytes 55304 | tf_op jit(solution)/shard_map/ppermute | solution.py:13
  89.8 6.2 %collective-permute-start.6 = (f32[2,2304]{1,0:T(2,128)}, f32[2,2304]{1,0:T(2,128)S(1)}, u32[]{:S(2)}, u32[]{:S(2)}) collective-permute-start(f32[2,2304]{1,0:T(2,128)} %get-tuple-element.18), channel_id=1, source_target_pairs={{7,0},{0,1},{1,2},{2,3},{3,4},{4,5},{5,6},{6,7},{15,8},{8,9},{9,10... | collective-permute-start | bytes 55304 | tf_op jit(solution)/shard_map/ppermute | solution.py:13
  89.8 6.2 %collective-permute-start.7 = (f32[2,2304]{1,0:T(2,128)}, f32[2,2304]{1,0:T(2,128)S(1)}, u32[]{:S(2)}, u32[]{:S(2)}) collective-permute-start(f32[2,2304]{1,0:T(2,128)} %get-tuple-element.19), channel_id=1, source_target_pairs={{24,0},{0,8},{8,16},{16,24},{25,1},{1,9},{9,17},{17,25},{26,2},{2,... | collective-permute-start | bytes 55304 | tf_op jit(solution)/shard_map/ppermute | solution.py:13
  105.8 19.6 %copy-start.8 = (f32[2,1,3,2304]{3,2,1,0:T(4,128)S(1)}, f32[2,1,3,2304]{3,2,1,0:T(4,128)}, u32[]{:S(2)}) copy-start(f32[2,1,3,2304]{3,2,1,0:T(4,128)} %copy-done.7) | copy-start | bytes 165892
  105.8 19.6 %copy-start.23 = (f32[1,1,2,3,2304]{4,2,3,1,0:T(2,128)S(1)}, f32[1,1,2,3,2304]{4,2,3,1,0:T(2,128)}, u32[]{:S(2)}) copy-start(f32[1,1,2,3,2304]{4,2,3,1,0:T(2,128)} %pad_maximum_fusion.1) | copy-start | bytes 165892
  105.8 19.6 %copy-start.36 = (f32[2,3]{1,0:T(2,128)S(1)}, f32[2,3]{1,0:T(2,128)}, u32[]{:S(2)}) copy-start(f32[2,3]{1,0:T(2,128)} %copy-done.34) | copy-start | bytes 76
  106.2 20.1 %copy-start.44 = (f32[1,1,2,3]{3,2,1,0:T(2,128)S(1)}, f32[1,1,2,3]{3,2,1,0:T(2,128)}, u32[]{:S(2)}) copy-start(f32[1,1,2,3]{3,2,1,0:T(2,128)} %param.9) | copy-start | bytes 76
  106.2 20.1 %copy-start.49 = (f32[2,3]{1,0:T(2,128)S(1)}, f32[2,3]{1,0:T(2,128)}, u32[]{:S(2)}) copy-start(f32[2,3]{1,0:T(2,128)} %copy-done.48) | copy-start | bytes 76
  106.2 20.1 %copy-start.51 = (f32[2,3]{1,0:T(2,128)S(1)}, f32[2,3]{1,0:T(2,128)}, u32[]{:S(2)}) copy-start(f32[2,3]{1,0:T(2,128)} %copy-done.50) | copy-start | bytes 76
  107.6 12.3 %all-to-all-start.2 = ((f32[32,1,4]{2,1,0:T(1,128)}), f32[32,1,4]{2,1,0:T(1,128)S(1)}, u32[]{:S(2)}, u32[]{:S(2)}) async-start(f32[32,1,4]{2,1,0:T(1,128)} %broadcast_in_dim.218), calls=%async_computation.2 | async-start | bytes 32768 | tf_op jit(solution)/shard_map/all_to_all | solution.py:167
  113.0 12.3 %collective-permute-start.8 = (f32[2,2304]{1,0:T(2,128)S(1)}, f32[2,2304]{1,0:T(2,128)S(1)}, u32[]{:S(2)}, u32[]{:S(2)}) collective-permute-start(f32[2,2304]{1,0:T(2,128)S(1)} %get-tuple-element.20), channel_id=1, source_target_pairs={{1,0},{2,1},{3,2},{4,3},{5,4},{6,5},{7,6},{0,7},{9,8},{10,9},{11,1... | collective-permute-start | bytes 55304 | tf_op jit(solution)/shard_map/ppermute | solution.py:13
  116.4 8.8 %collective-permute-start.9 = (f32[2,2304]{1,0:T(2,128)S(1)}, f32[2,2304]{1,0:T(2,128)S(1)}, u32[]{:S(2)}, u32[]{:S(2)}) collective-permute-start(f32[2,2304]{1,0:T(2,128)S(1)} %get-tuple-element.21), channel_id=1, source_target_pairs={{8,0},{16,8},{24,16},{0,24},{9,1},{17,9},{25,17},{1,25},{10,2},{18... | collective-permute-start | bytes 55304 | tf_op jit(solution)/shard_map/ppermute | solution.py:13
  (60 other events, 364.2 us)

commit v7 on v3

--- a/solution.py
+++ b/solution.py
@@ -143,7 +143,7 @@
         second = jnp.dot(rows_in[:, 1], before, precision=PRECISE)
         return own, jnp.stack([first, second], axis=1)
 
-    def jumps(traces_now, both, extra=None):
+    def jumps(traces_now, both, extra=None, after=None):
         low_side = traces_now[:, 0]
         high_side = traces_now[:, 1]
         face_size = high_side.shape[-1]
@@ -153,7 +153,7 @@
                 jnp.concatenate([high_side[:, 0], extra[0]], axis=1),
                 jnp.concatenate([high_side[:, 1], extra[1]], axis=1),
             ]
-        sends = lax.optimization_barrier(sends)
+        sends, after = lax.optimization_barrier((sends, after))
         low_next_owner = shifted(sends[0], "dev", -1)
         low_next_group = shifted(sends[1], "grp", -1)
         following = jnp.stack(
@@ -168,7 +168,8 @@
             [high_prev_owner[:, :face_size], high_prev_group[:, :face_size]], axis=1
         )
         incoming = live_in[..., None] * (leading - low_side[:, :2])
-        return own, incoming, (high_prev_owner[:, face_size:], high_prev_group[:, face_size:])
+        tail = (high_prev_owner[:, face_size:], high_prev_group[:, face_size:])
+        return own, incoming, tail, after
 
     def solve(v_own, v_in):
         preceding = jnp.stack([v_in[:, 0], v_in[:, 1], slot_before(v_own[:, 2])], axis=1)
@@ -196,7 +197,9 @@
 
     start_traces = jax.vmap(setup_one)(patch_loads, transforms, inverses)
     gathered = gather_all(face_means(start_traces))
-    res_own, res_in, received = jumps(start_traces, True, (extra_owner, extra_group))
+    res_own, res_in, received, gathered = jumps(
+        start_traces, True, (extra_owner, extra_group), gathered
+    )
     rows_in = jnp.stack([received[0][:, :coarse_size], received[1][:, :coarse_size]], axis=1)
     weights_in = jnp.stack([received[0][:, coarse_size], received[1][:, coarse_size]], axis=1)
     c_own, c_in = coarse(interface_means(gathered))
@@ -204,7 +207,7 @@
     traces_one = solve(dir_own, dir_in)
     parts = partial_sums([res_own * dir_own, split_terms(dir_own, dir_in, traces_one)])
     gathered = gather_all(jnp.concatenate([face_means(traces_one), parts]))
-    img_own, img_in, _ = jumps(traces_one, True, (extra_owner[:, :0], extra_group[:, :0]))
+    img_own, img_in, _, _ = jumps(traces_one, True, (extra_owner[:, :0], extra_group[:, :0]))
     totals = jnp.sum(gathered[:, :, slot_count * 6 :], axis=(0, 1))
     product = totals[0:1]
     curve = totals[1:2]

time: 85.3 us -> 83.9 us (0.984)
  starting transfers between devices: 30.3 us -> 27.3 us
  waiting for transfers between devices: 7.45 us -> 9.16 us
    ppermute x10, starting transfers between devices: 19 us -> 14.4 us  [shifted(): return lax.ppermute(block, axis, route)]
    ppermute x10, waiting for transfers between devices: 0.03 us -> 2.22 us  [shifted(): return lax.ppermute(block, axis, route)]
    all_to_all x3, starting transfers between devices: 11.3 us -> 12.9 us  [gather_all(): got = lax.all_to_all(spread, ('grp', 'dev'), 0, 0, tiled=True)]
  transfers between devices with their start and end apart: 13 -> 13, of which waited for: 3 -> 5; matrix products, arithmetic and copies ran while one was open for 8% -> 8% of each run, Pallas kernels for 0% -> 0%
where the time goes in v7:
time: 83.9 us; the launch traced here: 83.6 us
  starting transfers between devices  27.3 us (33%)
  other arithmetic  15.6 us (19%)
  local copies, waits for them, and re-layouts  12.9 us (15%)
  matrix products  11.3 us (13%)
  waiting for transfers between devices  9.16 us (11%)
  between operations  7.26 us (9%)
    ppermute x10, starting transfers between devices, shifted(): return lax.ppermute(block, axis, route)  14.4 us
    all_to_all x3, starting transfers between devices, gather_all(): got = lax.all_to_all(spread, ('grp', 'dev'), 0, 0, tiled=True)  12.9 us
    all_to_all x3, waiting for transfers between devices, gather_all(): got = lax.all_to_all(spread, ('grp', 'dev'), 0, 0, tiled=True)  6.94 us
    reduce_sum x3, other arithmetic, trace_solved(): along_a = jnp.sum(end_rows[:, :, None, None] * solved[None], axis=1)  6.94 us
    mul x2, other arithmetic, apply_one(): one_inverse * face_spectrum(one_transform, low_side, high_side)  4.56 us
    dot_general x6, matrix products, trace_solved(): jnp.einsum('bj,edjk,ck->edbc', transform, planes, transform, precision=FAST)  2.84 us
    reshape x1, local copies, waits for them, and re-layouts, spectral(): spatial = patch_load.astype(jnp.float32).reshape(points, points, points)  2.66 us
    dot_general x1, matrix products, spectral(): return jnp.einsum('ck,ijc->ijk', transform, moved, precision=FAST)  2.59 us
  transfers between devices with their start and end apart: 13, of which 5 were waited for; matrix products, arithmetic and copies ran while one was open for 8% of the time, Pallas kernels for 0%

profile of v7, /device:TPU:0, one launch (start us, length us, event | category | flops | bytes accessed | tf_op | source)
XLA Modules:
  0.0 83.6 jit_solution(7607299342184557761)
XLA Ops:
  0.6 0.8 broadcast_add_fusion
  1.5 2.7 %reshape.1199 = bf16[2,48,48,48]{3,2,1,0:T(8,128)(2,1)S(1)} reshape(bf16[1,1,2,48,2304]{4,3,2,1,0:T(8,128)(2,1)} %param.6) | data formatting | bytes 884736 | tf_op jit(solution)/shard_map/vmap()/reshape | solution.py:22
  4.1 1.6 %fusion.7 = f32[2,48,48,48]{3,1,2,0:T(8,128)S(1)} fusion(bf16[2,48,48,48]{3,2,1,0:T(8,128)(2,1)S(1)} %reshape.1199, f32[1,1,2,48,48]{4,3,2,1,0:T(8,128)} %param.7), kind=kOutput, calls=%fused_computation.17 | convolution fusion | flops 63700992 | bytes 1345536 | tf_op jit(solution)/shard_map/vmap(ai,abc->ibc)/dot_general | solution.py:23
  5.8 2.2 %fusion.2 = f32[2,48,48,48]{3,2,1,0:T(8,128)S(1)} fusion(f32[2,48,48,48]{3,1,2,0:T(8,128)S(1)} %fusion.7, f32[1,1,2,48,48]{4,3,2,1,0:T(8,128)S(1)} %copy-done), kind=kOutput, calls=%fused_computation.11 | convolution fusion | flops 63700992 | bytes 1787904 | tf_op jit(solution)/shard_map/vmap(bj,ibc->ijc)/dot_general | solution.py:24
  8.1 2.6 %fusion.4 = f32[2,48,48,48]{3,2,1,0:T(8,128)S(1)} fusion(f32[2,48,48,48]{3,2,1,0:T(8,128)S(1)} %fusion.2, f32[2,48]{1,0:T(2,128)S(1)} %bitcast.404, f32[2,48,48]{2,1,0:T(8,128)S(1)} %broadcast_add_fusion, f32[1,1,2,48,48]{4,3,2,1,0:T(8,128)S(1)} %copy-done), kind=kOutput, calls=%fused_computation.16 | convolution fusion | flops 64364544 | bytes 1806720 | tf_op jit(solution)/shard_map/vmap(ck,ijc->ijk)/dot_general | solution.py:25
  10.7 2.3 %multiply_reduce_fusion.8 = (f32[2,2,48,48]{3,2,1,0:T(8,128)S(1)}, f32[2,2,48,48]{3,2,1,0:T(8,128)S(1)}, f32[2,2,48,48]{3,2,1,0:T(8,128)S(1)}) fusion(f32[2,48,48,48]{3,2,1,0:T(8,128)S(1)} %fusion.4, f32[2,2,48]{2,1,0:T(2,128)S(1)} %copy.344), kind=kLoop, calls=%fused_computation.8 | loop fusion | flops 2626560 | bytes 996096 | tf_op jit(solution)/shard_map/vmap()/reduce_sum | solution.py:51
  15.0 7.3 %all-to-all-start = ((f32[32,1,12]{2,1,0:T(1,128)}), f32[32,1,12]{2,1,0:T(1,128)S(1)}, u32[]{:S(2)}, u32[]{:S(2)}) async-start(f32[32,1,12]{2,1,0:T(1,128)} %broadcast_in_dim.6), calls=%async_computation | async-start | bytes 32768 | tf_op jit(solution)/shard_map/all_to_all | solution.py:118
  24.4 4.9 %all-to-all-done = f32[32,1,12]{2,1,0:T(1,128)S(1)} async-done(((f32[32,1,12]{2,1,0:T(1,128)}), f32[32,1,12]{2,1,0:T(1,128)S(1)}, u32[]{:S(2)}, u32[]{:S(2)}) %all-to-all-start) | async-done | bytes 1568 | tf_op jit(solution)/shard_map/all_to_all | solution.py:118
  29.6 0.8 %collective-permute-start.3 = (f32[2,2304]{1,0:T(2,128)S(1)}, f32[2,2304]{1,0:T(2,128)S(1)}, u32[]{:S(2)}, u32[]{:S(2)}) collective-permute-start(f32[2,2304]{1,0:T(2,128)S(1)} %get-tuple-element.17), channel_id=1, source_target_pairs={{8,0},{16,8},{24,16},{0,24},{9,1},{17,9},{25,17},{1,25},{10,2},{18... | collective-permute-start | bytes 55304 | tf_op jit(solution)/shard_map/ppermute | solution.py:13
  30.4 1.4 %collective-permute-start.1 = (f32[2,2353]{1,0:T(2,128)S(1)}, f32[2,2353]{1,0:T(2,128)S(1)}, u32[]{:S(2)}, u32[]{:S(2)}) collective-permute-start(f32[2,2353]{1,0:T(2,128)S(1)} %concatenate.240), channel_id=1, source_target_pairs={{24,0},{0,8},{8,16},{16,24},{25,1},{1,9},{9,17},{17,25},{26,2},{2,... | collective-permute-start | bytes 56480 | tf_op jit(solution)/shard_map/ppermute | solution.py:13
  33.8 1.6 %collective-permute-done = f32[2,2353]{1,0:T(2,128)S(1)} collective-permute-done((f32[2,2353]{1,0:T(2,128)S(1)}, f32[2,2353]{1,0:T(2,128)S(1)}, u32[]{:S(2)}, u32[]{:S(2)}) %collective-permute-start) | collective-permute-done | bytes 18856 | tf_op jit(solution)/shard_map/ppermute | solution.py:13
  37.1 2.3 %add_multiply_fusion.1 = f32[2,48,48,48]{3,2,1,0:T(8,128)S(1)} fusion(f32[2,48,48]{2,1,0:T(8,128)S(1)} %get-tuple-element.68, f32[2,48]{1,0:T(2,128)S(1)} %bitcast.394, f32[2,48,48]{2,1,0:T(8,128)S(1)} %get-tuple-element.69, f32[2,48]{1,0:T(2,128)S(1)} %bitcast.391, f32[2,48,48]{2,1,0:T(8,128)S(1)} %get-tuple-element.70, ...), kind=kLoop, calls=%fused_computation.14 | loop fusion | flops 3096576 | bytes 1014912 | tf_op jit(solution)/shard_map/vmap()/mul | solution.py:65
  39.4 2.3 %multiply_reduce_fusion.5 = (f32[2,2,48,48]{3,2,1,0:T(8,128)S(1)}, f32[2,2,48,48]{3,2,1,0:T(8,128)S(1)}, f32[2,2,48,48]{3,2,1,0:T(8,128)S(1)}) fusion(f32[2,48,48,48]{3,2,1,0:T(8,128)S(1)} %add_multiply_fusion.1, f32[2,2,48]{2,1,0:T(2,128)S(1)} %copy.344), kind=kLoop, calls=%fused_computation.5 | loop fusion | flops 2626560 | bytes 996096 | tf_op jit(solution)/shard_map/vmap()/reduce_sum | solution.py:51
  44.6 3.1 %all-to-all-start.1 = ((f32[32,1,14]{2,1,0:T(1,128)}), f32[32,1,14]{2,1,0:T(1,128)S(1)}, u32[]{:S(2)}, u32[]{:S(2)}) async-start(f32[32,1,14]{2,1,0:T(1,128)} %broadcast_in_dim.7), calls=%async_computation.1 | async-start | bytes 32768 | tf_op jit(solution)/shard_map/all_to_all | solution.py:118
  47.9 1.7 %collective-permute-start.7 = (f32[2,2304]{1,0:T(2,128)S(1)}, f32[2,2304]{1,0:T(2,128)S(1)}, u32[]{:S(2)}, u32[]{:S(2)}) collective-permute-start(f32[2,2304]{1,0:T(2,128)S(1)} %get-tuple-element.21), channel_id=1, source_target_pairs={{24,0},{0,8},{8,16},{16,24},{25,1},{1,9},{9,17},{17,25},{26,2},{2,... | collective-permute-start | bytes 55304 | tf_op jit(solution)/shard_map/ppermute | solution.py:13
  49.6 3.1 %collective-permute-start.4 = (f32[2,2304]{1,0:T(2,128)S(1)}, f32[2,2304]{1,0:T(2,128)S(1)}, u32[]{:S(2)}, u32[]{:S(2)}) collective-permute-start(f32[2,2304]{1,0:T(2,128)S(1)} %get-tuple-element.18), channel_id=1, source_target_pairs={{1,0},{2,1},{3,2},{4,3},{5,4},{6,5},{7,6},{0,7},{9,8},{10,9},{11,1... | collective-permute-start | bytes 55304 | tf_op jit(solution)/shard_map/ppermute | solution.py:13
  52.7 1.2 %collective-permute-start.5 = (f32[2,2304]{1,0:T(2,128)S(1)}, f32[2,2304]{1,0:T(2,128)S(1)}, u32[]{:S(2)}, u32[]{:S(2)}) collective-permute-start(f32[2,2304]{1,0:T(2,128)S(1)} %get-tuple-element.19), channel_id=1, source_target_pairs={{8,0},{16,8},{24,16},{0,24},{9,1},{17,9},{25,17},{1,25},{10,2},{18... | collective-permute-start | bytes 55304 | tf_op jit(solution)/shard_map/ppermute | solution.py:13
  53.9 0.8 %all-to-all-done.1 = f32[32,1,14]{2,1,0:T(1,128)S(1)} async-done(((f32[32,1,14]{2,1,0:T(1,128)}), f32[32,1,14]{2,1,0:T(1,128)S(1)}, u32[]{:S(2)}, u32[]{:S(2)}) %all-to-all-start.1) | async-done | bytes 1824 | tf_op jit(solution)/shard_map/all_to_all | solution.py:118
  59.5 2.3 %add_multiply_fusion = f32[2,48,48,48]{3,2,1,0:T(8,128)S(1)} fusion(f32[2,48,48]{2,1,0:T(8,128)S(1)} %get-tuple-element.62, f32[2,48,48]{2,1,0:T(8,128)S(1)} %get-tuple-element.63, f32[2,48,48]{2,1,0:T(8,128)S(1)} %get-tuple-element.64, f32[2,48,48]{2,1,0:T(8,128)S(1)} %get-tuple-element.65, f32[2,48,48]{2,1,0:T(8,128)S(1)} %get-tuple-element.66, ...), kind=kLoop, calls=%fused_computation.13 | loop fusion | flops 3096576 | bytes 1014912 | tf_op jit(solution)/shard_map/vmap()/mul | solution.py:65
  61.8 2.3 %multiply_reduce_fusion.2 = (f32[2,2,48,48]{3,2,1,0:T(8,128)S(1)}, f32[2,2,48,48]{3,2,1,0:T(8,128)S(1)}, f32[2,2,48,48]{3,2,1,0:T(8,128)S(1)}) fusion(f32[2,48,48,48]{3,2,1,0:T(8,128)S(1)} %add_multiply_fusion, f32[2,2,48]{2,1,0:T(2,128)S(1)} %copy.344), kind=kLoop, calls=%fused_computation.2 | loop fusion | flops 2626560 | bytes 996096 | tf_op jit(solution)/shard_map/vmap()/reduce_sum | solution.py:51
  66.9 2.5 %all-to-all-start.2 = ((f32[32,1,4]{2,1,0:T(1,128)}), f32[32,1,4]{2,1,0:T(1,128)S(1)}, u32[]{:S(2)}, u32[]{:S(2)}) async-start(f32[32,1,4]{2,1,0:T(1,128)} %broadcast_in_dim.8), calls=%async_computation.2 | async-start | bytes 32768 | tf_op jit(solution)/shard_map/all_to_all | solution.py:118
  69.4 3.4 %collective-permute-start.8 = (f32[2,2304]{1,0:T(2,128)S(1)}, f32[2,2304]{1,0:T(2,128)S(1)}, u32[]{:S(2)}, u32[]{:S(2)}) collective-permute-start(f32[2,2304]{1,0:T(2,128)S(1)} %get-tuple-element.22), channel_id=1, source_target_pairs={{1,0},{2,1},{3,2},{4,3},{5,4},{6,5},{7,6},{0,7},{9,8},{10,9},{11,1... | collective-permute-start | bytes 55304 | tf_op jit(solution)/shard_map/ppermute | solution.py:13
  72.9 2.4 %collective-permute-start.9 = (f32[2,2304]{1,0:T(2,128)S(1)}, f32[2,2304]{1,0:T(2,128)S(1)}, u32[]{:S(2)}, u32[]{:S(2)}) collective-permute-start(f32[2,2304]{1,0:T(2,128)S(1)} %get-tuple-element.23), channel_id=1, source_target_pairs={{8,0},{16,8},{24,16},{0,24},{9,1},{17,9},{25,17},{1,25},{10,2},{18... | collective-permute-start | bytes 55304 | tf_op jit(solution)/shard_map/ppermute | solution.py:13
  75.3 1.2 %all-to-all-done.2 = f32[32,1,4]{2,1,0:T(1,128)S(1)} async-done(((f32[32,1,4]{2,1,0:T(1,128)}), f32[32,1,4]{2,1,0:T(1,128)S(1)}, u32[]{:S(2)}, u32[]{:S(2)}) %all-to-all-start.2) | async-done | bytes 544 | tf_op jit(solution)/shard_map/all_to_all | solution.py:118
  (190 shorter events, 19.3 us)
Async XLA Ops:
  1.5 4.3 %copy-start = (f32[1,1,2,48,48]{4,3,2,1,0:T(8,128)S(1)}, f32[1,1,2,48,48]{4,3,2,1,0:T(8,128)}, u32[]{:S(2)}) copy-start(f32[1,1,2,48,48]{4,3,2,1,0:T(8,128)} %param.7) | copy-start | bytes 55300
  5.8 2.3 %copy-start.2 = (f32[1,1,2,48]{3,2,1,0:T(2,128)S(1)}, f32[1,1,2,48]{3,2,1,0:T(2,128)}, u32[]{:S(2)}) copy-start(f32[1,1,2,48]{3,2,1,0:T(2,128)} %param.8) | copy-start | bytes 1156
  10.7 12.0 %copy-start.1 = (s32[4,8]{1,0:T(4,128)S(1)}, s32[4,8]{1,0:T(4,128)}, u32[]{:S(2)}) copy-start(s32[4,8]{1,0:T(4,128)} %param.10) | copy-start | bytes 388
  10.7 12.1 %copy-start.4 = (f32[1,1,6,48]{3,1,2,0:T(1,128)S(1)}, f32[1,1,6,48]{3,1,2,0:T(1,128)}, u32[]{:S(2)}) copy-start(f32[1,1,6,48]{3,1,2,0:T(1,128)} %param.11) | copy-start | bytes 3460
  10.7 12.2 %copy-start.3 = (f32[1,1,2,3]{3,2,1,0:T(2,128)S(1)}, f32[1,1,2,3]{3,2,1,0:T(2,128)}, u32[]{:S(2)}) copy-start(f32[1,1,2,3]{3,2,1,0:T(2,128)} %param.9) | copy-start | bytes 76
  15.0 14.4 %all-to-all-start = ((f32[32,1,12]{2,1,0:T(1,128)}), f32[32,1,12]{2,1,0:T(1,128)S(1)}, u32[]{:S(2)}, u32[]{:S(2)}) async-start(f32[32,1,12]{2,1,0:T(1,128)} %broadcast_in_dim.6), calls=%async_computation | async-start | bytes 32768 | tf_op jit(solution)/shard_map/all_to_all | solution.py:118
  29.5 3.3 %collective-permute-start.2 = (f32[2,2304]{1,0:T(2,128)S(1)}, f32[2,2304]{1,0:T(2,128)S(1)}, u32[]{:S(2)}, u32[]{:S(2)}) collective-permute-start(f32[2,2304]{1,0:T(2,128)S(1)} %get-tuple-element.16), channel_id=1, source_target_pairs={{1,0},{2,1},{3,2},{4,3},{5,4},{6,5},{7,6},{0,7},{9,8},{10,9},{11,1... | collective-permute-start | bytes 55304 | tf_op jit(solution)/shard_map/ppermute | solution.py:13
  29.6 3.8 %collective-permute-start.3 = (f32[2,2304]{1,0:T(2,128)S(1)}, f32[2,2304]{1,0:T(2,128)S(1)}, u32[]{:S(2)}, u32[]{:S(2)}) collective-permute-start(f32[2,2304]{1,0:T(2,128)S(1)} %get-tuple-element.17), channel_id=1, source_target_pairs={{8,0},{16,8},{24,16},{0,24},{9,1},{17,9},{25,17},{1,25},{10,2},{18... | collective-permute-start | bytes 55304 | tf_op jit(solution)/shard_map/ppermute | solution.py:13
  30.4 5.0 %collective-permute-start = (f32[2,2353]{1,0:T(2,128)S(1)}, f32[2,2353]{1,0:T(2,128)S(1)}, u32[]{:S(2)}, u32[]{:S(2)}) collective-permute-start(f32[2,2353]{1,0:T(2,128)S(1)} %concatenate.239), channel_id=1, source_target_pairs={{7,0},{0,1},{1,2},{2,3},{3,4},{4,5},{5,6},{6,7},{15,8},{8,9},{9,10... | collective-permute-start | bytes 56480 | tf_op jit(solution)/shard_map/ppermute | solution.py:13
  30.4 5.1 %collective-permute-start.1 = (f32[2,2353]{1,0:T(2,128)S(1)}, f32[2,2353]{1,0:T(2,128)S(1)}, u32[]{:S(2)}, u32[]{:S(2)}) collective-permute-start(f32[2,2353]{1,0:T(2,128)S(1)} %concatenate.240), channel_id=1, source_target_pairs={{24,0},{0,8},{8,16},{16,24},{25,1},{1,9},{9,17},{17,25},{26,2},{2,... | collective-permute-start | bytes 56480 | tf_op jit(solution)/shard_map/ppermute | solution.py:13
  44.6 10.2 %all-to-all-start.1 = ((f32[32,1,14]{2,1,0:T(1,128)}), f32[32,1,14]{2,1,0:T(1,128)S(1)}, u32[]{:S(2)}, u32[]{:S(2)}) async-start(f32[32,1,14]{2,1,0:T(1,128)} %broadcast_in_dim.7), calls=%async_computation.1 | async-start | bytes 32768 | tf_op jit(solution)/shard_map/all_to_all | solution.py:118
  47.6 10.7 %collective-permute-start.6 = (f32[2,2304]{1,0:T(2,128)S(1)}, f32[2,2304]{1,0:T(2,128)S(1)}, u32[]{:S(2)}, u32[]{:S(2)}) collective-permute-start(f32[2,2304]{1,0:T(2,128)S(1)} %get-tuple-element.20), channel_id=1, source_target_pairs={{7,0},{0,1},{1,2},{2,3},{3,4},{4,5},{5,6},{6,7},{15,8},{8,9},{9,10... | collective-permute-start | bytes 55304 | tf_op jit(solution)/shard_map/ppermute | solution.py:13
  47.9 10.4 %collective-permute-start.7 = (f32[2,2304]{1,0:T(2,128)S(1)}, f32[2,2304]{1,0:T(2,128)S(1)}, u32[]{:S(2)}, u32[]{:S(2)}) collective-permute-start(f32[2,2304]{1,0:T(2,128)S(1)} %get-tuple-element.21), channel_id=1, source_target_pairs={{24,0},{0,8},{8,16},{16,24},{25,1},{1,9},{9,17},{17,25},{26,2},{2,... | collective-permute-start | bytes 55304 | tf_op jit(solution)/shard_map/ppermute | solution.py:13
  49.6 8.5 %collective-permute-start.4 = (f32[2,2304]{1,0:T(2,128)S(1)}, f32[2,2304]{1,0:T(2,128)S(1)}, u32[]{:S(2)}, u32[]{:S(2)}) collective-permute-start(f32[2,2304]{1,0:T(2,128)S(1)} %get-tuple-element.18), channel_id=1, source_target_pairs={{1,0},{2,1},{3,2},{4,3},{5,4},{6,5},{7,6},{0,7},{9,8},{10,9},{11,1... | collective-permute-start | bytes 55304 | tf_op jit(solution)/shard_map/ppermute | solution.py:13
  52.7 5.4 %collective-permute-start.5 = (f32[2,2304]{1,0:T(2,128)S(1)}, f32[2,2304]{1,0:T(2,128)S(1)}, u32[]{:S(2)}, u32[]{:S(2)}) collective-permute-start(f32[2,2304]{1,0:T(2,128)S(1)} %get-tuple-element.19), channel_id=1, source_target_pairs={{8,0},{16,8},{24,16},{0,24},{9,1},{17,9},{25,17},{1,25},{10,2},{18... | collective-permute-start | bytes 55304 | tf_op jit(solution)/shard_map/ppermute | solution.py:13
  66.9 9.6 %all-to-all-start.2 = ((f32[32,1,4]{2,1,0:T(1,128)}), f32[32,1,4]{2,1,0:T(1,128)S(1)}, u32[]{:S(2)}, u32[]{:S(2)}) async-start(f32[32,1,4]{2,1,0:T(1,128)} %broadcast_in_dim.8), calls=%async_computation.2 | async-start | bytes 32768 | tf_op jit(solution)/shard_map/all_to_all | solution.py:118
  69.4 12.1 %collective-permute-start.8 = (f32[2,2304]{1,0:T(2,128)S(1)}, f32[2,2304]{1,0:T(2,128)S(1)}, u32[]{:S(2)}, u32[]{:S(2)}) collective-permute-start(f32[2,2304]{1,0:T(2,128)S(1)} %get-tuple-element.22), channel_id=1, source_target_pairs={{1,0},{2,1},{3,2},{4,3},{5,4},{6,5},{7,6},{0,7},{9,8},{10,9},{11,1... | collective-permute-start | bytes 55304 | tf_op jit(solution)/shard_map/ppermute | solution.py:13
  72.9 8.7 %collective-permute-start.9 = (f32[2,2304]{1,0:T(2,128)S(1)}, f32[2,2304]{1,0:T(2,128)S(1)}, u32[]{:S(2)}, u32[]{:S(2)}) collective-permute-start(f32[2,2304]{1,0:T(2,128)S(1)} %get-tuple-element.23), channel_id=1, source_target_pairs={{8,0},{16,8},{24,16},{0,24},{9,1},{17,9},{25,17},{1,25},{10,2},{18... | collective-permute-start | bytes 55304 | tf_op jit(solution)/shard_map/ppermute | solution.py:13

commit v8 on v7

--- a/solution.py
+++ b/solution.py
@@ -161,7 +161,7 @@
         )
         own = live_own[..., None] * (high_side - following)
         if not both:
-            return own
+            return own, after
         high_prev_owner = shifted(sends[2], "dev", 1)
         high_prev_group = shifted(sends[3], "grp", 1)
         leading = jnp.stack(
@@ -207,7 +207,9 @@
     traces_one = solve(dir_own, dir_in)
     parts = partial_sums([res_own * dir_own, split_terms(dir_own, dir_in, traces_one)])
     gathered = gather_all(jnp.concatenate([face_means(traces_one), parts]))
-    img_own, img_in, _, _ = jumps(traces_one, True, (extra_owner[:, :0], extra_group[:, :0]))
+    img_own, img_in, _, gathered = jumps(
+        traces_one, True, (extra_owner[:, :0], extra_group[:, :0]), gathered
+    )
     totals = jnp.sum(gathered[:, :, slot_count * 6 :], axis=(0, 1))
     product = totals[0:1]
     curve = totals[1:2]
@@ -230,7 +232,7 @@
         ]
     )
     gathered = gather_all(parts)
-    fz_own = jumps(traces_two, False)
+    fz_own, gathered = jumps(traces_two, False, None, gathered)
     totals = jnp.sum(gathered, axis=(0, 1))
     new_product = totals[0:1]
     ratio = new_product / product

time: 83.9 us -> 91.7 us (1.093)
  waiting for transfers between devices: 9.16 us -> 21.2 us
  starting transfers between devices: 27.3 us -> 22.9 us
    all_to_all x3, waiting for transfers between devices: 6.94 us -> 19 us  [gather_all(): got = lax.all_to_all(spread, ('grp', 'dev'), 0, 0, tiled=True)]
    ppermute x10, starting transfers between devices: 14.4 us -> 9.19 us  [shifted(): return lax.ppermute(block, axis, route)]
  transfers between devices with their start and end apart: 13 -> 13, of which waited for: 5 -> 5; matrix products, arithmetic and copies ran while one was open for 8% -> 5% of each run, Pallas kernels for 0% -> 0%
where the time goes in v8:
time: 91.7 us; the launch traced here: 91.3 us
  starting transfers between devices  22.9 us (25%)
  waiting for transfers between devices  21.2 us (23%)
  other arithmetic  15.7 us (17%)
  local copies, waits for them, and re-layouts  13 us (14%)
  matrix products  11.3 us (12%)
  between operations  7.22 us (8%)
    all_to_all x3, waiting for transfers between devices, gather_all(): got = lax.all_to_all(spread, ('grp', 'dev'), 0, 0, tiled=True)  19 us
    all_to_all x3, starting transfers between devices, gather_all(): got = lax.all_to_all(spread, ('grp', 'dev'), 0, 0, tiled=True)  13.7 us
    ppermute x10, starting transfers between devices, shifted(): return lax.ppermute(block, axis, route)  9.19 us
    reduce_sum x3, other arithmetic, trace_solved(): along_a = jnp.sum(end_rows[:, :, None, None] * solved[None], axis=1)  6.94 us
    mul x2, other arithmetic, apply_one(): one_inverse * face_spectrum(one_transform, low_side, high_side)  4.56 us
    dot_general x6, matrix products, trace_solved(): jnp.einsum('bj,edjk,ck->edbc', transform, planes, transform, precision=FAST)  2.84 us
    reshape x1, local copies, waits for them, and re-layouts, spectral(): spatial = patch_load.astype(jnp.float32).reshape(points, points, points)  2.66 us
    dot_general x1, matrix products, spectral(): return jnp.einsum('ck,ijc->ijk', transform, moved, precision=FAST)  2.59 us
  transfers between devices with their start and end apart: 13, of which 5 were waited for; matrix products, arithmetic and copies ran while one was open for 5% of the time, Pallas kernels for 0%

profile of v8, /device:TPU:0, one launch (start us, length us, event | category | flops | bytes accessed | tf_op | source)
XLA Modules:
  0.0 91.3 jit_solution(18055987769222909545)
XLA Ops:
  0.6 0.8 broadcast_add_fusion
  1.5 2.7 %reshape.1202 = bf16[2,48,48,48]{3,2,1,0:T(8,128)(2,1)S(1)} reshape(bf16[1,1,2,48,2304]{4,3,2,1,0:T(8,128)(2,1)} %param.6) | data formatting | bytes 884736 | tf_op jit(solution)/shard_map/vmap()/reshape | solution.py:22
  4.1 1.6 %fusion.7 = f32[2,48,48,48]{3,1,2,0:T(8,128)S(1)} fusion(bf16[2,48,48,48]{3,2,1,0:T(8,128)(2,1)S(1)} %reshape.1202, f32[1,1,2,48,48]{4,3,2,1,0:T(8,128)} %param.7), kind=kOutput, calls=%fused_computation.17 | convolution fusion | flops 63700992 | bytes 1345536 | tf_op jit(solution)/shard_map/vmap(ai,abc->ibc)/dot_general | solution.py:23
  5.8 2.2 %fusion.2 = f32[2,48,48,48]{3,2,1,0:T(8,128)S(1)} fusion(f32[2,48,48,48]{3,1,2,0:T(8,128)S(1)} %fusion.7, f32[1,1,2,48,48]{4,3,2,1,0:T(8,128)S(1)} %copy-done), kind=kOutput, calls=%fused_computation.11 | convolution fusion | flops 63700992 | bytes 1787904 | tf_op jit(solution)/shard_map/vmap(bj,ibc->ijc)/dot_general | solution.py:24
  8.1 2.6 %fusion.4 = f32[2,48,48,48]{3,2,1,0:T(8,128)S(1)} fusion(f32[2,48,48,48]{3,2,1,0:T(8,128)S(1)} %fusion.2, f32[2,48]{1,0:T(2,128)S(1)} %bitcast.406, f32[2,48,48]{2,1,0:T(8,128)S(1)} %broadcast_add_fusion, f32[1,1,2,48,48]{4,3,2,1,0:T(8,128)S(1)} %copy-done), kind=kOutput, calls=%fused_computation.16 | convolution fusion | flops 64364544 | bytes 1806720 | tf_op jit(solution)/shard_map/vmap(ck,ijc->ijk)/dot_general | solution.py:25
  10.7 2.3 %multiply_reduce_fusion.8 = (f32[2,2,48,48]{3,2,1,0:T(8,128)S(1)}, f32[2,2,48,48]{3,2,1,0:T(8,128)S(1)}, f32[2,2,48,48]{3,2,1,0:T(8,128)S(1)}) fusion(f32[2,48,48,48]{3,2,1,0:T(8,128)S(1)} %fusion.4, f32[2,2,48]{2,1,0:T(2,128)S(1)} %copy.273), kind=kLoop, calls=%fused_computation.8 | loop fusion | flops 2626560 | bytes 996096 | tf_op jit(solution)/shard_map/vmap()/reduce_sum | solution.py:51
  15.0 7.3 %all-to-all-start = ((f32[32,1,12]{2,1,0:T(1,128)}), f32[32,1,12]{2,1,0:T(1,128)S(1)}, u32[]{:S(2)}, u32[]{:S(2)}) async-start(f32[32,1,12]{2,1,0:T(1,128)} %broadcast_in_dim.6), calls=%async_computation | async-start | bytes 32768 | tf_op jit(solution)/shard_map/all_to_all | solution.py:118
  24.4 4.9 %all-to-all-done = f32[32,1,12]{2,1,0:T(1,128)S(1)} async-done(((f32[32,1,12]{2,1,0:T(1,128)}), f32[32,1,12]{2,1,0:T(1,128)S(1)}, u32[]{:S(2)}, u32[]{:S(2)}) %all-to-all-start) | async-done | bytes 1568 | tf_op jit(solution)/shard_map/all_to_all | solution.py:118
  29.6 0.8 collective-permute-start.3
  30.4 1.4 %collective-permute-start.1 = (f32[2,2353]{1,0:T(2,128)S(1)}, f32[2,2353]{1,0:T(2,128)S(1)}, u32[]{:S(2)}, u32[]{:S(2)}) collective-permute-start(f32[2,2353]{1,0:T(2,128)S(1)} %concatenate.240), channel_id=1, source_target_pairs={{24,0},{0,8},{8,16},{16,24},{25,1},{1,9},{9,17},{17,25},{26,2},{2,... | collective-permute-start | bytes 56480 | tf_op jit(solution)/shard_map/ppermute | solution.py:13
  33.8 1.6 %collective-permute-done = f32[2,2353]{1,0:T(2,128)S(1)} collective-permute-done((f32[2,2353]{1,0:T(2,128)S(1)}, f32[2,2353]{1,0:T(2,128)S(1)}, u32[]{:S(2)}, u32[]{:S(2)}) %collective-permute-start) | collective-permute-done | bytes 18856 | tf_op jit(solution)/shard_map/ppermute | solution.py:13
  37.1 2.3 %add_multiply_fusion.1 = f32[2,48,48,48]{3,2,1,0:T(8,128)S(1)} fusion(f32[2,48,48]{2,1,0:T(8,128)S(1)} %get-tuple-element.70, f32[2,48]{1,0:T(2,128)S(1)} %bitcast.395, f32[2,48,48]{2,1,0:T(8,128)S(1)} %get-tuple-element.71, f32[2,48]{1,0:T(2,128)S(1)} %bitcast.392, f32[2,48,48]{2,1,0:T(8,128)S(1)} %get-tuple-element.72, ...), kind=kLoop, calls=%fused_computation.14 | loop fusion | flops 3096576 | bytes 1014912 | tf_op jit(solution)/shard_map/vmap()/mul | solution.py:65
  39.4 2.3 %multiply_reduce_fusion.5 = (f32[2,2,48,48]{3,2,1,0:T(8,128)S(1)}, f32[2,2,48,48]{3,2,1,0:T(8,128)S(1)}, f32[2,2,48,48]{3,2,1,0:T(8,128)S(1)}) fusion(f32[2,48,48,48]{3,2,1,0:T(8,128)S(1)} %add_multiply_fusion.1, f32[2,2,48]{2,1,0:T(2,128)S(1)} %copy.273), kind=kLoop, calls=%fused_computation.5 | loop fusion | flops 2626560 | bytes 996096 | tf_op jit(solution)/shard_map/vmap()/reduce_sum | solution.py:51
  44.6 3.1 %all-to-all-start.1 = ((f32[32,1,14]{2,1,0:T(1,128)}), f32[32,1,14]{2,1,0:T(1,128)S(1)}, u32[]{:S(2)}, u32[]{:S(2)}) async-start(f32[32,1,14]{2,1,0:T(1,128)} %broadcast_in_dim.7), calls=%async_computation.1 | async-start | bytes 32768 | tf_op jit(solution)/shard_map/all_to_all | solution.py:118
  47.7 7.0 %all-to-all-done.1 = f32[32,1,14]{2,1,0:T(1,128)S(1)} async-done(((f32[32,1,14]{2,1,0:T(1,128)}), f32[32,1,14]{2,1,0:T(1,128)S(1)}, u32[]{:S(2)}, u32[]{:S(2)}) %all-to-all-start.1) | async-done | bytes 1824 | tf_op jit(solution)/shard_map/all_to_all | solution.py:118
  57.0 3.3 %collective-permute-start.6 = (f32[2,2304]{1,0:T(2,128)S(1)}, f32[2,2304]{1,0:T(2,128)S(1)}, u32[]{:S(2)}, u32[]{:S(2)}) collective-permute-start(f32[2,2304]{1,0:T(2,128)S(1)} %get-tuple-element.23), channel_id=1, source_target_pairs={{1,0},{2,1},{3,2},{4,3},{5,4},{6,5},{7,6},{0,7},{9,8},{10,9},{11,1... | collective-permute-start | bytes 55304 | tf_op jit(solution)/shard_map/ppermute | solution.py:13
  60.3 2.3 %collective-permute-start.7 = (f32[2,2304]{1,0:T(2,128)S(1)}, f32[2,2304]{1,0:T(2,128)S(1)}, u32[]{:S(2)}, u32[]{:S(2)}) collective-permute-start(f32[2,2304]{1,0:T(2,128)S(1)} %get-tuple-element.24), channel_id=1, source_target_pairs={{8,0},{16,8},{24,16},{0,24},{9,1},{17,9},{25,17},{1,25},{10,2},{18... | collective-permute-start | bytes 55304 | tf_op jit(solution)/shard_map/ppermute | solution.py:13
  65.6 2.3 %add_multiply_fusion = f32[2,48,48,48]{3,2,1,0:T(8,128)S(1)} fusion(f32[2,48,48]{2,1,0:T(8,128)S(1)} %get-tuple-element.64, f32[2,48,48]{2,1,0:T(8,128)S(1)} %get-tuple-element.65, f32[2,48,48]{2,1,0:T(8,128)S(1)} %get-tuple-element.66, f32[2,48,48]{2,1,0:T(8,128)S(1)} %get-tuple-element.67, f32[2,48,48]{2,1,0:T(8,128)S(1)} %get-tuple-element.68, ...), kind=kLoop, calls=%fused_computation.13 | loop fusion | flops 3096576 | bytes 1014912 | tf_op jit(solution)/shard_map/vmap()/mul | solution.py:65
  67.9 2.3 %multiply_reduce_fusion.2 = (f32[2,2,48,48]{3,2,1,0:T(8,128)S(1)}, f32[2,2,48,48]{3,2,1,0:T(8,128)S(1)}, f32[2,2,48,48]{3,2,1,0:T(8,128)S(1)}) fusion(f32[2,48,48,48]{3,2,1,0:T(8,128)S(1)} %add_multiply_fusion, f32[2,2,48]{2,1,0:T(2,128)S(1)} %copy.273), kind=kLoop, calls=%fused_computation.2 | loop fusion | flops 2626560 | bytes 996096 | tf_op jit(solution)/shard_map/vmap()/reduce_sum | solution.py:51
  73.0 3.4 %all-to-all-start.2 = ((f32[32,1,4]{2,1,0:T(1,128)}), f32[32,1,4]{2,1,0:T(1,128)S(1)}, u32[]{:S(2)}, u32[]{:S(2)}) async-start(f32[32,1,4]{2,1,0:T(1,128)} %broadcast_in_dim.8), calls=%async_computation.2 | async-start | bytes 32768 | tf_op jit(solution)/shard_map/all_to_all | solution.py:118
  76.4 7.0 %all-to-all-done.2 = f32[32,1,4]{2,1,0:T(1,128)S(1)} async-done(((f32[32,1,4]{2,1,0:T(1,128)}), f32[32,1,4]{2,1,0:T(1,128)S(1)}, u32[]{:S(2)}, u32[]{:S(2)}) %all-to-all-start.2) | async-done | bytes 544 | tf_op jit(solution)/shard_map/all_to_all | solution.py:118
  84.3 0.7 fusion.108
  90.0 0.7 copy.344
  90.7 0.7 copy.345
  (191 shorter events, 18.5 us)
Async XLA Ops:
  1.5 4.3 %copy-start = (f32[1,1,2,48,48]{4,3,2,1,0:T(8,128)S(1)}, f32[1,1,2,48,48]{4,3,2,1,0:T(8,128)}, u32[]{:S(2)}) copy-start(f32[1,1,2,48,48]{4,3,2,1,0:T(8,128)} %param.7) | copy-start | bytes 55300
  5.8 2.3 %copy-start.2 = (f32[1,1,2,48]{3,2,1,0:T(2,128)S(1)}, f32[1,1,2,48]{3,2,1,0:T(2,128)}, u32[]{:S(2)}) copy-start(f32[1,1,2,48]{3,2,1,0:T(2,128)} %param.8) | copy-start | bytes 1156
  10.7 12.0 %copy-start.1 = (s32[4,8]{1,0:T(4,128)S(1)}, s32[4,8]{1,0:T(4,128)}, u32[]{:S(2)}) copy-start(s32[4,8]{1,0:T(4,128)} %param.10) | copy-start | bytes 388
  10.7 12.1 %copy-start.4 = (f32[1,1,6,48]{3,1,2,0:T(1,128)S(1)}, f32[1,1,6,48]{3,1,2,0:T(1,128)}, u32[]{:S(2)}) copy-start(f32[1,1,6,48]{3,1,2,0:T(1,128)} %param.11) | copy-start | bytes 3460
  10.7 12.2 %copy-start.3 = (f32[1,1,2,3]{3,2,1,0:T(2,128)S(1)}, f32[1,1,2,3]{3,2,1,0:T(2,128)}, u32[]{:S(2)}) copy-start(f32[1,1,2,3]{3,2,1,0:T(2,128)} %param.9) | copy-start | bytes 76
  15.0 14.4 %all-to-all-start = ((f32[32,1,12]{2,1,0:T(1,128)}), f32[32,1,12]{2,1,0:T(1,128)S(1)}, u32[]{:S(2)}, u32[]{:S(2)}) async-start(f32[32,1,12]{2,1,0:T(1,128)} %broadcast_in_dim.6), calls=%async_computation | async-start | bytes 32768 | tf_op jit(solution)/shard_map/all_to_all | solution.py:118
  29.5 3.3 %collective-permute-start.2 = (f32[2,2304]{1,0:T(2,128)S(1)}, f32[2,2304]{1,0:T(2,128)S(1)}, u32[]{:S(2)}, u32[]{:S(2)}) collective-permute-start(f32[2,2304]{1,0:T(2,128)S(1)} %get-tuple-element.18), channel_id=1, source_target_pairs={{1,0},{2,1},{3,2},{4,3},{5,4},{6,5},{7,6},{0,7},{9,8},{10,9},{11,1... | collective-permute-start | bytes 55304 | tf_op jit(solution)/shard_map/ppermute | solution.py:13
  29.6 3.8 %collective-permute-start.3 = (f32[2,2304]{1,0:T(2,128)S(1)}, f32[2,2304]{1,0:T(2,128)S(1)}, u32[]{:S(2)}, u32[]{:S(2)}) collective-permute-start(f32[2,2304]{1,0:T(2,128)S(1)} %get-tuple-element.19), channel_id=1, source_target_pairs={{8,0},{16,8},{24,16},{0,24},{9,1},{17,9},{25,17},{1,25},{10,2},{18... | collective-permute-start | bytes 55304 | tf_op jit(solution)/shard_map/ppermute | solution.py:13
  30.4 5.0 %collective-permute-start = (f32[2,2353]{1,0:T(2,128)S(1)}, f32[2,2353]{1,0:T(2,128)S(1)}, u32[]{:S(2)}, u32[]{:S(2)}) collective-permute-start(f32[2,2353]{1,0:T(2,128)S(1)} %concatenate.239), channel_id=1, source_target_pairs={{7,0},{0,1},{1,2},{2,3},{3,4},{4,5},{5,6},{6,7},{15,8},{8,9},{9,10... | collective-permute-start | bytes 56480 | tf_op jit(solution)/shard_map/ppermute | solution.py:13
  30.4 5.1 %collective-permute-start.1 = (f32[2,2353]{1,0:T(2,128)S(1)}, f32[2,2353]{1,0:T(2,128)S(1)}, u32[]{:S(2)}, u32[]{:S(2)}) collective-permute-start(f32[2,2353]{1,0:T(2,128)S(1)} %concatenate.240), channel_id=1, source_target_pairs={{24,0},{0,8},{8,16},{16,24},{25,1},{1,9},{9,17},{17,25},{26,2},{2,... | collective-permute-start | bytes 56480 | tf_op jit(solution)/shard_map/ppermute | solution.py:13
  44.6 10.1 %all-to-all-start.1 = ((f32[32,1,14]{2,1,0:T(1,128)}), f32[32,1,14]{2,1,0:T(1,128)S(1)}, u32[]{:S(2)}, u32[]{:S(2)}) async-start(f32[32,1,14]{2,1,0:T(1,128)} %broadcast_in_dim.7), calls=%async_computation.1 | async-start | bytes 32768 | tf_op jit(solution)/shard_map/all_to_all | solution.py:118
  56.2 8.3 %collective-permute-start.4 = (f32[2,2304]{1,0:T(2,128)S(1)}, f32[2,2304]{1,0:T(2,128)S(1)}, u32[]{:S(2)}, u32[]{:S(2)}) collective-permute-start(f32[2,2304]{1,0:T(2,128)S(1)} %get-tuple-element.21), channel_id=1, source_target_pairs={{7,0},{0,1},{1,2},{2,3},{3,4},{4,5},{5,6},{6,7},{15,8},{8,9},{9,10... | collective-permute-start | bytes 55304 | tf_op jit(solution)/shard_map/ppermute | solution.py:13
  56.2 8.3 %collective-permute-start.5 = (f32[2,2304]{1,0:T(2,128)S(1)}, f32[2,2304]{1,0:T(2,128)S(1)}, u32[]{:S(2)}, u32[]{:S(2)}) collective-permute-start(f32[2,2304]{1,0:T(2,128)S(1)} %get-tuple-element.22), channel_id=1, source_target_pairs={{24,0},{0,8},{8,16},{16,24},{25,1},{1,9},{9,17},{17,25},{26,2},{2,... | collective-permute-start | bytes 55304 | tf_op jit(solution)/shard_map/ppermute | solution.py:13
  57.0 7.3 %collective-permute-start.6 = (f32[2,2304]{1,0:T(2,128)S(1)}, f32[2,2304]{1,0:T(2,128)S(1)}, u32[]{:S(2)}, u32[]{:S(2)}) collective-permute-start(f32[2,2304]{1,0:T(2,128)S(1)} %get-tuple-element.23), channel_id=1, source_target_pairs={{1,0},{2,1},{3,2},{4,3},{5,4},{6,5},{7,6},{0,7},{9,8},{10,9},{11,1... | collective-permute-start | bytes 55304 | tf_op jit(solution)/shard_map/ppermute | solution.py:13
  60.3 4.0 %collective-permute-start.7 = (f32[2,2304]{1,0:T(2,128)S(1)}, f32[2,2304]{1,0:T(2,128)S(1)}, u32[]{:S(2)}, u32[]{:S(2)}) collective-permute-start(f32[2,2304]{1,0:T(2,128)S(1)} %get-tuple-element.24), channel_id=1, source_target_pairs={{8,0},{16,8},{24,16},{0,24},{9,1},{17,9},{25,17},{1,25},{10,2},{18... | collective-permute-start | bytes 55304 | tf_op jit(solution)/shard_map/ppermute | solution.py:13
  73.0 10.4 %all-to-all-start.2 = ((f32[32,1,4]{2,1,0:T(1,128)}), f32[32,1,4]{2,1,0:T(1,128)S(1)}, u32[]{:S(2)}, u32[]{:S(2)}) async-start(f32[32,1,4]{2,1,0:T(1,128)} %broadcast_in_dim.8), calls=%async_computation.2 | async-start | bytes 32768 | tf_op jit(solution)/shard_map/all_to_all | solution.py:118
  83.5 5.8 %collective-permute-start.8 = (f32[2,2304]{1,0:T(2,128)S(1)}, f32[2,2304]{1,0:T(2,128)S(1)}, u32[]{:S(2)}, u32[]{:S(2)}) collective-permute-start(f32[2,2304]{1,0:T(2,128)S(1)} %get-tuple-element.26), channel_id=1, source_target_pairs={{1,0},{2,1},{3,2},{4,3},{5,4},{6,5},{7,6},{0,7},{9,8},{10,9},{11,1... | collective-permute-start | bytes 55304 | tf_op jit(solution)/shard_map/ppermute | solution.py:13
  83.5 5.8 %collective-permute-start.9 = (f32[2,2304]{1,0:T(2,128)S(1)}, f32[2,2304]{1,0:T(2,128)S(1)}, u32[]{:S(2)}, u32[]{:S(2)}) collective-permute-start(f32[2,2304]{1,0:T(2,128)S(1)} %get-tuple-element.27), channel_id=1, source_target_pairs={{8,0},{16,8},{24,16},{0,24},{9,1},{17,9},{25,17},{1,25},{10,2},{18... | collective-permute-start | bytes 55304 | tf_op jit(solution)/shard_map/ppermute | solution.py:13

commit v9 on v7

--- a/solution.py
+++ b/solution.py
@@ -56,8 +56,20 @@
     return traces.reshape(2, 3, points * points)
 
 
+def plane_means(transform, solved):
+    points = transform.shape[0]
+    end_rows = jnp.stack([transform[0], transform[points - 1]])
+    spread = jnp.mean(transform, axis=0)
+    along_a = jnp.sum(end_rows[:, :, None, None] * solved[None], axis=1)
+    along_b = jnp.sum(end_rows[:, None, :, None] * solved[None], axis=2)
+    along_c = jnp.sum(end_rows[:, None, None, :] * solved[None], axis=3)
+    planes = jnp.stack([along_a, along_b, along_c], axis=1)
+    return jnp.sum(planes * spread[:, None] * spread[None, :], axis=(2, 3))
+
+
 def setup_one(patch_load, one_transform, one_inverse):
-    return trace_solved(one_transform, one_inverse * spectral(patch_load, one_transform))
+    solved = one_inverse * spectral(patch_load, one_transform)
+    return trace_solved(one_transform, solved), plane_means(one_transform, solved)
 
 
 def apply_one(one_transform, one_inverse, low_side, high_side):
@@ -195,8 +207,8 @@
         z_in = weights_in[..., None] * res_in + live_in[..., None] * c_in[..., None]
         return z_own, z_in
 
-    start_traces = jax.vmap(setup_one)(patch_loads, transforms, inverses)
-    gathered = gather_all(face_means(start_traces))
+    start_traces, start_means = jax.vmap(setup_one)(patch_loads, transforms, inverses)
+    gathered = gather_all(start_means.reshape(-1))
     res_own, res_in, received, gathered = jumps(
         start_traces, True, (extra_owner, extra_group), gathered
     )

time: 83.9 us -> 83.7 us (level)
    all_to_all x3, waiting for transfers between devices: 6.94 us -> 5.97 us  [gather_all(): got = lax.all_to_all(spread, ('grp', 'dev'), 0, 0, tiled=True)]
    ppermute x10, waiting for transfers between devices: 2.22 us -> 3.18 us  [shifted(): return lax.ppermute(block, axis, route)]
    broadcast_in_dim x3 -> x4, local copies, waits for them, and re-layouts: 1.86 us -> 1.94 us  [gather_all(): spread = jnp.broadcast_to(payload[None], (count,) + payload.shape)]
  transfers between devices with their start and end apart: 13 -> 13, of which waited for: 5 -> 5; matrix products, arithmetic and copies ran while one was open for 8% -> 9% of each run, Pallas kernels for 0% -> 0%
where the time goes in v9:
time: 83.7 us; the launch traced here: 83.3 us
  starting transfers between devices  26.8 us (32%)
  other arithmetic  16 us (19%)
  local copies, waits for them, and re-layouts  12.9 us (15%)
  matrix products  11.2 us (13%)
  waiting for transfers between devices  9.15 us (11%)
  between operations  7.27 us (9%)
    ppermute x10, starting transfers between devices, shifted(): return lax.ppermute(block, axis, route)  14.4 us
    all_to_all x3, starting transfers between devices, gather_all(): got = lax.all_to_all(spread, ('grp', 'dev'), 0, 0, tiled=True)  12.4 us
    reduce_sum x3, other arithmetic, trace_solved(): along_a = jnp.sum(end_rows[:, :, None, None] * solved[None], axis=1)  6.94 us
    all_to_all x3, waiting for transfers between devices, gather_all(): got = lax.all_to_all(spread, ('grp', 'dev'), 0, 0, tiled=True)  5.97 us
    mul x2, other arithmetic, apply_one(): one_inverse * face_spectrum(one_transform, low_side, high_side)  4.6 us
    ppermute x10, waiting for transfers between devices, shifted(): return lax.ppermute(block, axis, route)  3.18 us
    dot_general x6, matrix products, trace_solved(): jnp.einsum('bj,edjk,ck->edbc', transform, planes, transform, precision=FAST)  2.74 us
    reshape x1, local copies, waits for them, and re-layouts, spectral(): spatial = patch_load.astype(jnp.float32).reshape(points, points, points)  2.66 us
  transfers between devices with their start and end apart: 13, of which 5 were waited for; matrix products, arithmetic and copies ran while one was open for 9% of the time, Pallas kernels for 0%

profile of v9, /device:TPU:0, one launch (start us, length us, event | category | flops | bytes accessed | tf_op | source)
XLA Modules:
  0.0 83.3 jit_solution(9634679277315268682)
XLA Ops:
  0.6 0.8 broadcast_add_fusion
  1.5 2.7 %reshape.1200 = bf16[2,48,48,48]{3,2,1,0:T(8,128)(2,1)S(1)} reshape(bf16[1,1,2,48,2304]{4,3,2,1,0:T(8,128)(2,1)} %param.6) | data formatting | bytes 884736 | tf_op jit(solution)/shard_map/vmap()/reshape | solution.py:22
  4.1 1.6 %fusion.7 = f32[2,48,48,48]{3,1,2,0:T(8,128)S(1)} fusion(bf16[2,48,48,48]{3,2,1,0:T(8,128)(2,1)S(1)} %reshape.1200, f32[1,1,2,48,48]{4,3,2,1,0:T(8,128)} %param.7), kind=kOutput, calls=%fused_computation.17 | convolution fusion | flops 63700992 | bytes 1345536 | tf_op jit(solution)/shard_map/vmap(ai,abc->ibc)/dot_general | solution.py:23
  5.8 2.2 %fusion.2 = f32[2,48,48,48]{3,2,1,0:T(8,128)S(1)} fusion(f32[2,48,48,48]{3,1,2,0:T(8,128)S(1)} %fusion.7, f32[1,1,2,48,48]{4,3,2,1,0:T(8,128)S(1)} %copy-done), kind=kOutput, calls=%fused_computation.11 | convolution fusion | flops 63700992 | bytes 1787904 | tf_op jit(solution)/shard_map/vmap(bj,ibc->ijc)/dot_general | solution.py:24
  8.1 2.6 %fusion.4 = f32[2,48,48,48]{3,2,1,0:T(8,128)S(1)} fusion(f32[2,48,48,48]{3,2,1,0:T(8,128)S(1)} %fusion.2, f32[2,48]{1,0:T(2,128)S(1)} %bitcast.413, f32[2,48,48]{2,1,0:T(8,128)S(1)} %broadcast_add_fusion, f32[1,1,2,48,48]{4,3,2,1,0:T(8,128)S(1)} %copy-done), kind=kOutput, calls=%fused_computation.16 | convolution fusion | flops 64364544 | bytes 1806720 | tf_op jit(solution)/shard_map/vmap(ck,ijc->ijk)/dot_general | solution.py:25
  10.7 2.3 %multiply_reduce_fusion.8 = (f32[2,2,48,48]{3,2,1,0:T(8,128)S(1)}, f32[2,2,48,48]{3,2,1,0:T(8,128)S(1)}, f32[2,2,48,48]{3,2,1,0:T(8,128)S(1)}) fusion(f32[2,48,48,48]{3,2,1,0:T(8,128)S(1)} %fusion.4, f32[2,2,48]{2,1,0:T(2,128)S(1)} %copy.344), kind=kLoop, calls=%fused_computation.8 | loop fusion | flops 2626560 | bytes 996096 | tf_op jit(solution)/shard_map/vmap()/reduce_sum | solution.py:51
  14.3 7.3 %all-to-all-start = ((f32[32,1,12]{2,1,0:T(1,128)}), f32[32,1,12]{2,1,0:T(1,128)S(1)}, u32[]{:S(2)}, u32[]{:S(2)}) async-start(f32[32,1,12]{2,1,0:T(1,128)} %broadcast_in_dim.9), calls=%async_computation | async-start | bytes 32768 | tf_op jit(solution)/shard_map/all_to_all | solution.py:130
  24.7 4.0 %all-to-all-done = f32[32,1,12]{2,1,0:T(1,128)S(1)} async-done(((f32[32,1,12]{2,1,0:T(1,128)}), f32[32,1,12]{2,1,0:T(1,128)S(1)}, u32[]{:S(2)}, u32[]{:S(2)}) %all-to-all-start) | async-done | bytes 1568 | tf_op jit(solution)/shard_map/all_to_all | solution.py:130
  28.8 1.8 %collective-permute-start.3 = (f32[2,2304]{1,0:T(2,128)S(1)}, f32[2,2304]{1,0:T(2,128)S(1)}, u32[]{:S(2)}, u32[]{:S(2)}) collective-permute-start(f32[2,2304]{1,0:T(2,128)S(1)} %get-tuple-element.17), channel_id=1, source_target_pairs={{8,0},{16,8},{24,16},{0,24},{9,1},{17,9},{25,17},{1,25},{10,2},{18... | collective-permute-start | bytes 55304 | tf_op jit(solution)/shard_map/ppermute | solution.py:13
  33.0 2.6 %collective-permute-done = f32[2,2353]{1,0:T(2,128)S(1)} collective-permute-done((f32[2,2353]{1,0:T(2,128)S(1)}, f32[2,2353]{1,0:T(2,128)S(1)}, u32[]{:S(2)}, u32[]{:S(2)}) %collective-permute-start) | collective-permute-done | bytes 18856 | tf_op jit(solution)/shard_map/ppermute | solution.py:13
  37.3 2.3 %add_multiply_fusion.1 = f32[2,48,48,48]{3,2,1,0:T(8,128)S(1)} fusion(f32[2,48,48]{2,1,0:T(8,128)S(1)} %get-tuple-element.67, f32[2,48]{1,0:T(2,128)S(1)} %bitcast.403, f32[2,48,48]{2,1,0:T(8,128)S(1)} %get-tuple-element.68, f32[2,48]{1,0:T(2,128)S(1)} %bitcast.400, f32[2,48,48]{2,1,0:T(8,128)S(1)} %get-tuple-element.69, ...), kind=kLoop, calls=%fused_computation.14 | loop fusion | flops 3096576 | bytes 1014912 | tf_op jit(solution)/shard_map/vmap()/mul | solution.py:77
  39.6 2.3 %multiply_reduce_fusion.5 = (f32[2,2,48,48]{3,2,1,0:T(8,128)S(1)}, f32[2,2,48,48]{3,2,1,0:T(8,128)S(1)}, f32[2,2,48,48]{3,2,1,0:T(8,128)S(1)}) fusion(f32[2,48,48,48]{3,2,1,0:T(8,128)S(1)} %add_multiply_fusion.1, f32[2,2,48]{2,1,0:T(2,128)S(1)} %copy.344), kind=kLoop, calls=%fused_computation.5 | loop fusion | flops 2626560 | bytes 996096 | tf_op jit(solution)/shard_map/vmap()/reduce_sum | solution.py:51
  44.8 2.5 %all-to-all-start.1 = ((f32[32,1,14]{2,1,0:T(1,128)}), f32[32,1,14]{2,1,0:T(1,128)S(1)}, u32[]{:S(2)}, u32[]{:S(2)}) async-start(f32[32,1,14]{2,1,0:T(1,128)} %broadcast_in_dim.10), calls=%async_computation.1 | async-start | bytes 32768 | tf_op jit(solution)/shard_map/all_to_all | solution.py:130
  47.5 1.7 %collective-permute-start.7 = (f32[2,2304]{1,0:T(2,128)S(1)}, f32[2,2304]{1,0:T(2,128)S(1)}, u32[]{:S(2)}, u32[]{:S(2)}) collective-permute-start(f32[2,2304]{1,0:T(2,128)S(1)} %get-tuple-element.21), channel_id=1, source_target_pairs={{24,0},{0,8},{8,16},{16,24},{25,1},{1,9},{9,17},{17,25},{26,2},{2,... | collective-permute-start | bytes 55304 | tf_op jit(solution)/shard_map/ppermute | solution.py:13
  49.2 3.1 %collective-permute-start.4 = (f32[2,2304]{1,0:T(2,128)S(1)}, f32[2,2304]{1,0:T(2,128)S(1)}, u32[]{:S(2)}, u32[]{:S(2)}) collective-permute-start(f32[2,2304]{1,0:T(2,128)S(1)} %get-tuple-element.18), channel_id=1, source_target_pairs={{1,0},{2,1},{3,2},{4,3},{5,4},{6,5},{7,6},{0,7},{9,8},{10,9},{11,1... | collective-permute-start | bytes 55304 | tf_op jit(solution)/shard_map/ppermute | solution.py:13
  52.3 1.3 %collective-permute-start.5 = (f32[2,2304]{1,0:T(2,128)S(1)}, f32[2,2304]{1,0:T(2,128)S(1)}, u32[]{:S(2)}, u32[]{:S(2)}) collective-permute-start(f32[2,2304]{1,0:T(2,128)S(1)} %get-tuple-element.19), channel_id=1, source_target_pairs={{8,0},{16,8},{24,16},{0,24},{9,1},{17,9},{25,17},{1,25},{10,2},{18... | collective-permute-start | bytes 55304 | tf_op jit(solution)/shard_map/ppermute | solution.py:13
  53.6 0.8 all-to-all-done.1
  59.2 2.3 %add_multiply_fusion = f32[2,48,48,48]{3,2,1,0:T(8,128)S(1)} fusion(f32[2,48,48]{2,1,0:T(8,128)S(1)} %get-tuple-element.61, f32[2,48,48]{2,1,0:T(8,128)S(1)} %get-tuple-element.62, f32[2,48,48]{2,1,0:T(8,128)S(1)} %get-tuple-element.63, f32[2,48,48]{2,1,0:T(8,128)S(1)} %get-tuple-element.64, f32[2,48,48]{2,1,0:T(8,128)S(1)} %get-tuple-element.65, ...), kind=kLoop, calls=%fused_computation.13 | loop fusion | flops 3096576 | bytes 1014912 | tf_op jit(solution)/shard_map/vmap()/mul | solution.py:77
  61.5 2.3 %multiply_reduce_fusion.2 = (f32[2,2,48,48]{3,2,1,0:T(8,128)S(1)}, f32[2,2,48,48]{3,2,1,0:T(8,128)S(1)}, f32[2,2,48,48]{3,2,1,0:T(8,128)S(1)}) fusion(f32[2,48,48,48]{3,2,1,0:T(8,128)S(1)} %add_multiply_fusion, f32[2,2,48]{2,1,0:T(2,128)S(1)} %copy.344), kind=kLoop, calls=%fused_computation.2 | loop fusion | flops 2626560 | bytes 996096 | tf_op jit(solution)/shard_map/vmap()/reduce_sum | solution.py:51
  66.6 2.5 %all-to-all-start.2 = ((f32[32,1,4]{2,1,0:T(1,128)}), f32[32,1,4]{2,1,0:T(1,128)S(1)}, u32[]{:S(2)}, u32[]{:S(2)}) async-start(f32[32,1,4]{2,1,0:T(1,128)} %broadcast_in_dim.11), calls=%async_computation.2 | async-start | bytes 32768 | tf_op jit(solution)/shard_map/all_to_all | solution.py:130
  69.2 3.4 %collective-permute-start.8 = (f32[2,2304]{1,0:T(2,128)S(1)}, f32[2,2304]{1,0:T(2,128)S(1)}, u32[]{:S(2)}, u32[]{:S(2)}) collective-permute-start(f32[2,2304]{1,0:T(2,128)S(1)} %get-tuple-element.22), channel_id=1, source_target_pairs={{1,0},{2,1},{3,2},{4,3},{5,4},{6,5},{7,6},{0,7},{9,8},{10,9},{11,1... | collective-permute-start | bytes 55304 | tf_op jit(solution)/shard_map/ppermute | solution.py:13
  72.6 2.4 %collective-permute-start.9 = (f32[2,2304]{1,0:T(2,128)S(1)}, f32[2,2304]{1,0:T(2,128)S(1)}, u32[]{:S(2)}, u32[]{:S(2)}) collective-permute-start(f32[2,2304]{1,0:T(2,128)S(1)} %get-tuple-element.23), channel_id=1, source_target_pairs={{8,0},{16,8},{24,16},{0,24},{9,1},{17,9},{25,17},{1,25},{10,2},{18... | collective-permute-start | bytes 55304 | tf_op jit(solution)/shard_map/ppermute | solution.py:13
  75.0 1.2 %all-to-all-done.2 = f32[32,1,4]{2,1,0:T(1,128)S(1)} async-done(((f32[32,1,4]{2,1,0:T(1,128)}), f32[32,1,4]{2,1,0:T(1,128)S(1)}, u32[]{:S(2)}, u32[]{:S(2)}) %all-to-all-start.2) | async-done | bytes 544 | tf_op jit(solution)/shard_map/all_to_all | solution.py:130
  82.0 0.7 copy.415
  (192 shorter events, 19.3 us)
Async XLA Ops:
  1.5 4.3 %copy-start = (f32[1,1,2,48,48]{4,3,2,1,0:T(8,128)S(1)}, f32[1,1,2,48,48]{4,3,2,1,0:T(8,128)}, u32[]{:S(2)}) copy-start(f32[1,1,2,48,48]{4,3,2,1,0:T(8,128)} %param.7) | copy-start | bytes 55300
  5.8 2.3 %copy-start.2 = (f32[1,1,2,48]{3,2,1,0:T(2,128)S(1)}, f32[1,1,2,48]{3,2,1,0:T(2,128)}, u32[]{:S(2)}) copy-start(f32[1,1,2,48]{3,2,1,0:T(2,128)} %param.8) | copy-start | bytes 1156
  10.7 12.2 %copy-start.1 = (s32[4,8]{1,0:T(4,128)S(1)}, s32[4,8]{1,0:T(4,128)}, u32[]{:S(2)}) copy-start(s32[4,8]{1,0:T(4,128)} %param.10) | copy-start | bytes 388
  10.7 12.3 %copy-start.4 = (f32[1,1,6,48]{3,1,2,0:T(1,128)S(1)}, f32[1,1,6,48]{3,1,2,0:T(1,128)}, u32[]{:S(2)}) copy-start(f32[1,1,6,48]{3,1,2,0:T(1,128)} %param.11) | copy-start | bytes 3460
  10.7 12.4 %copy-start.3 = (f32[1,1,2,3]{3,2,1,0:T(2,128)S(1)}, f32[1,1,2,3]{3,2,1,0:T(2,128)}, u32[]{:S(2)}) copy-start(f32[1,1,2,3]{3,2,1,0:T(2,128)} %param.9) | copy-start | bytes 76
  14.3 14.4 %all-to-all-start = ((f32[32,1,12]{2,1,0:T(1,128)}), f32[32,1,12]{2,1,0:T(1,128)S(1)}, u32[]{:S(2)}, u32[]{:S(2)}) async-start(f32[32,1,12]{2,1,0:T(1,128)} %broadcast_in_dim.9), calls=%async_computation | async-start | bytes 32768 | tf_op jit(solution)/shard_map/all_to_all | solution.py:130
  28.8 3.3 %collective-permute-start.2 = (f32[2,2304]{1,0:T(2,128)S(1)}, f32[2,2304]{1,0:T(2,128)S(1)}, u32[]{:S(2)}, u32[]{:S(2)}) collective-permute-start(f32[2,2304]{1,0:T(2,128)S(1)} %get-tuple-element.16), channel_id=1, source_target_pairs={{1,0},{2,1},{3,2},{4,3},{5,4},{6,5},{7,6},{0,7},{9,8},{10,9},{11,1... | collective-permute-start | bytes 55304 | tf_op jit(solution)/shard_map/ppermute | solution.py:13
  28.8 3.8 %collective-permute-start.3 = (f32[2,2304]{1,0:T(2,128)S(1)}, f32[2,2304]{1,0:T(2,128)S(1)}, u32[]{:S(2)}, u32[]{:S(2)}) collective-permute-start(f32[2,2304]{1,0:T(2,128)S(1)} %get-tuple-element.17), channel_id=1, source_target_pairs={{8,0},{16,8},{24,16},{0,24},{9,1},{17,9},{25,17},{1,25},{10,2},{18... | collective-permute-start | bytes 55304 | tf_op jit(solution)/shard_map/ppermute | solution.py:13
  30.6 5.0 %collective-permute-start = (f32[2,2353]{1,0:T(2,128)S(1)}, f32[2,2353]{1,0:T(2,128)S(1)}, u32[]{:S(2)}, u32[]{:S(2)}) collective-permute-start(f32[2,2353]{1,0:T(2,128)S(1)} %concatenate.239), channel_id=1, source_target_pairs={{7,0},{0,1},{1,2},{2,3},{3,4},{4,5},{5,6},{6,7},{15,8},{8,9},{9,10... | collective-permute-start | bytes 56480 | tf_op jit(solution)/shard_map/ppermute | solution.py:13
  30.6 5.1 %collective-permute-start.1 = (f32[2,2353]{1,0:T(2,128)S(1)}, f32[2,2353]{1,0:T(2,128)S(1)}, u32[]{:S(2)}, u32[]{:S(2)}) collective-permute-start(f32[2,2353]{1,0:T(2,128)S(1)} %concatenate.240), channel_id=1, source_target_pairs={{24,0},{0,8},{8,16},{16,24},{25,1},{1,9},{9,17},{17,25},{26,2},{2,... | collective-permute-start | bytes 56480 | tf_op jit(solution)/shard_map/ppermute | solution.py:13
  44.8 9.7 %all-to-all-start.1 = ((f32[32,1,14]{2,1,0:T(1,128)}), f32[32,1,14]{2,1,0:T(1,128)S(1)}, u32[]{:S(2)}, u32[]{:S(2)}) async-start(f32[32,1,14]{2,1,0:T(1,128)} %broadcast_in_dim.10), calls=%async_computation.1 | async-start | bytes 32768 | tf_op jit(solution)/shard_map/all_to_all | solution.py:130
  47.3 10.7 %collective-permute-start.6 = (f32[2,2304]{1,0:T(2,128)S(1)}, f32[2,2304]{1,0:T(2,128)S(1)}, u32[]{:S(2)}, u32[]{:S(2)}) collective-permute-start(f32[2,2304]{1,0:T(2,128)S(1)} %get-tuple-element.20), channel_id=1, source_target_pairs={{7,0},{0,1},{1,2},{2,3},{3,4},{4,5},{5,6},{6,7},{15,8},{8,9},{9,10... | collective-permute-start | bytes 55304 | tf_op jit(solution)/shard_map/ppermute | solution.py:13
  47.5 10.5 %collective-permute-start.7 = (f32[2,2304]{1,0:T(2,128)S(1)}, f32[2,2304]{1,0:T(2,128)S(1)}, u32[]{:S(2)}, u32[]{:S(2)}) collective-permute-start(f32[2,2304]{1,0:T(2,128)S(1)} %get-tuple-element.21), channel_id=1, source_target_pairs={{24,0},{0,8},{8,16},{16,24},{25,1},{1,9},{9,17},{17,25},{26,2},{2,... | collective-permute-start | bytes 55304 | tf_op jit(solution)/shard_map/ppermute | solution.py:13
  49.2 8.6 %collective-permute-start.4 = (f32[2,2304]{1,0:T(2,128)S(1)}, f32[2,2304]{1,0:T(2,128)S(1)}, u32[]{:S(2)}, u32[]{:S(2)}) collective-permute-start(f32[2,2304]{1,0:T(2,128)S(1)} %get-tuple-element.18), channel_id=1, source_target_pairs={{1,0},{2,1},{3,2},{4,3},{5,4},{6,5},{7,6},{0,7},{9,8},{10,9},{11,1... | collective-permute-start | bytes 55304 | tf_op jit(solution)/shard_map/ppermute | solution.py:13
  52.3 5.5 %collective-permute-start.5 = (f32[2,2304]{1,0:T(2,128)S(1)}, f32[2,2304]{1,0:T(2,128)S(1)}, u32[]{:S(2)}, u32[]{:S(2)}) collective-permute-start(f32[2,2304]{1,0:T(2,128)S(1)} %get-tuple-element.19), channel_id=1, source_target_pairs={{8,0},{16,8},{24,16},{0,24},{9,1},{17,9},{25,17},{1,25},{10,2},{18... | collective-permute-start | bytes 55304 | tf_op jit(solution)/shard_map/ppermute | solution.py:13
  66.6 9.6 %all-to-all-start.2 = ((f32[32,1,4]{2,1,0:T(1,128)}), f32[32,1,4]{2,1,0:T(1,128)S(1)}, u32[]{:S(2)}, u32[]{:S(2)}) async-start(f32[32,1,4]{2,1,0:T(1,128)} %broadcast_in_dim.11), calls=%async_computation.2 | async-start | bytes 32768 | tf_op jit(solution)/shard_map/all_to_all | solution.py:130
  69.2 12.1 %collective-permute-start.8 = (f32[2,2304]{1,0:T(2,128)S(1)}, f32[2,2304]{1,0:T(2,128)S(1)}, u32[]{:S(2)}, u32[]{:S(2)}) collective-permute-start(f32[2,2304]{1,0:T(2,128)S(1)} %get-tuple-element.22), channel_id=1, source_target_pairs={{1,0},{2,1},{3,2},{4,3},{5,4},{6,5},{7,6},{0,7},{9,8},{10,9},{11,1... | collective-permute-start | bytes 55304 | tf_op jit(solution)/shard_map/ppermute | solution.py:13
  72.6 8.7 %collective-permute-start.9 = (f32[2,2304]{1,0:T(2,128)S(1)}, f32[2,2304]{1,0:T(2,128)S(1)}, u32[]{:S(2)}, u32[]{:S(2)}) collective-permute-start(f32[2,2304]{1,0:T(2,128)S(1)} %get-tuple-element.23), channel_id=1, source_target_pairs={{8,0},{16,8},{24,16},{0,24},{9,1},{17,9},{25,17},{1,25},{10,2},{18... | collective-permute-start | bytes 55304 | tf_op jit(solution)/shard_map/ppermute | solution.py:13

commit v10 on v9

--- a/solution.py
+++ b/solution.py
@@ -253,6 +253,7 @@
     applied = fz_own + ratio * img_own
     multiplier = multiplier + step_two * direction
     residual = res_own - step_two * applied
+    multiplier, residual = lax.optimization_barrier((multiplier, residual))
     return (multiplier[None, None], residual[None, None])
 
 

time: 83.7 us -> 86.9 us (1.038)
  starting transfers between devices: 26.8 us -> 31.8 us
  waiting for transfers between devices: 9.15 us -> 7.2 us
  local copies, waits for them, and re-layouts: 12.9 us -> 11.7 us
  other arithmetic: 16 us -> 17.2 us
    ppermute x10, starting transfers between devices: 14.4 us -> 18.4 us  [shifted(): return lax.ppermute(block, axis, route)]
    ppermute x10, waiting for transfers between devices: 3.18 us -> 1.16 us  [shifted(): return lax.ppermute(block, axis, route)]
    unnamed x15 -> x13, local copies, waits for them, and re-layouts: 1.42 us -> 0.12 us
    all_to_all x3, starting transfers between devices: 12.4 us -> 13.4 us  [gather_all(): got = lax.all_to_all(spread, ('grp', 'dev'), 0, 0, tiled=True)]
  transfers between devices with their start and end apart: 13 -> 13, of which waited for: 5 -> 4; matrix products, arithmetic and copies ran while one was open for 9% -> 9% of each run, Pallas kernels for 0% -> 0%
where the time goes in v10:
time: 86.9 us; the launch traced here: 86.5 us
  starting transfers between devices  31.8 us (37%)
  other arithmetic  17.2 us (20%)
  local copies, waits for them, and re-layouts  11.7 us (13%)
  matrix products  11.2 us (13%)
  between operations  7.47 us (9%)
  waiting for transfers between devices  7.2 us (8%)
    ppermute x10, starting transfers between devices, shifted(): return lax.ppermute(block, axis, route)  18.4 us
    all_to_all x3, starting transfers between devices, gather_all(): got = lax.all_to_all(spread, ('grp', 'dev'), 0, 0, tiled=True)  13.4 us
    reduce_sum x3, other arithmetic, trace_solved(): along_a = jnp.sum(end_rows[:, :, None, None] * solved[None], axis=1)  6.94 us
    all_to_all x3, waiting for transfers between devices, gather_all(): got = lax.all_to_all(spread, ('grp', 'dev'), 0, 0, tiled=True)  6.04 us
    mul x2, other arithmetic, apply_one(): one_inverse * face_spectrum(one_transform, low_side, high_side)  4.6 us
    dot_general x6, matrix products, trace_solved(): jnp.einsum('bj,edjk,ck->edbc', transform, planes, transform, precision=FAST)  2.75 us
    reshape x1, local copies, waits for them, and re-layouts, spectral(): spatial = patch_load.astype(jnp.float32).reshape(points, points, points)  2.66 us
    dot_general x1, matrix products, spectral(): return jnp.einsum('ck,ijc->ijk', transform, moved, precision=FAST)  2.59 us
  transfers between devices with their start and end apart: 13, of which 4 were waited for; matrix products, arithmetic and copies ran while one was open for 9% of the time, Pallas kernels for 0%

profile of v10, /device:TPU:0, one launch (start us, length us, event | category | flops | bytes accessed | tf_op | source)
XLA Modules:
  0.0 86.5 jit_solution(11516664950849804513)
XLA Ops:
  0.6 0.8 broadcast_add_fusion
  1.5 2.7 %reshape.934 = bf16[2,48,48,48]{3,2,1,0:T(8,128)(2,1)S(1)} reshape(bf16[1,1,2,48,2304]{4,3,2,1,0:T(8,128)(2,1)} %param.6) | data formatting | bytes 884736 | tf_op jit(solution)/shard_map/vmap()/reshape | solution.py:22
  4.1 1.6 %fusion.7 = f32[2,48,48,48]{3,1,2,0:T(8,128)S(1)} fusion(bf16[2,48,48,48]{3,2,1,0:T(8,128)(2,1)S(1)} %reshape.934, f32[1,1,2,48,48]{4,3,2,1,0:T(8,128)} %param.7), kind=kOutput, calls=%fused_computation.17 | convolution fusion | flops 63700992 | bytes 1345536 | tf_op jit(solution)/shard_map/vmap(ai,abc->ibc)/dot_general | solution.py:23
  5.8 2.2 %fusion.2 = f32[2,48,48,48]{3,2,1,0:T(8,128)S(1)} fusion(f32[2,48,48,48]{3,1,2,0:T(8,128)S(1)} %fusion.7, f32[1,1,2,48,48]{4,3,2,1,0:T(8,128)S(1)} %copy-done), kind=kOutput, calls=%fused_computation.11 | convolution fusion | flops 63700992 | bytes 1787904 | tf_op jit(solution)/shard_map/vmap(bj,ibc->ijc)/dot_general | solution.py:24
  8.1 2.6 %fusion.4 = f32[2,48,48,48]{3,2,1,0:T(8,128)S(1)} fusion(f32[2,48,48,48]{3,2,1,0:T(8,128)S(1)} %fusion.2, f32[2,48]{1,0:T(2,128)S(1)} %bitcast.393, f32[2,48,48]{2,1,0:T(8,128)S(1)} %broadcast_add_fusion, f32[1,1,2,48,48]{4,3,2,1,0:T(8,128)S(1)} %copy-done), kind=kOutput, calls=%fused_computation.16 | convolution fusion | flops 64364544 | bytes 1806720 | tf_op jit(solution)/shard_map/vmap(ck,ijc->ijk)/dot_general | solution.py:25
  10.7 2.3 %multiply_reduce_fusion.8 = (f32[2,2,48,48]{3,2,1,0:T(8,128)S(1)}, f32[2,2,48,48]{3,2,1,0:T(8,128)S(1)}, f32[2,2,48,48]{3,2,1,0:T(8,128)S(1)}) fusion(f32[2,48,48,48]{3,2,1,0:T(8,128)S(1)} %fusion.4, f32[2,2,48]{2,1,0:T(2,128)S(1)} %copy.341), kind=kLoop, calls=%fused_computation.8 | loop fusion | flops 2626560 | bytes 996096 | tf_op jit(solution)/shard_map/vmap()/reduce_sum | solution.py:51
  14.3 7.3 %all-to-all-start = ((f32[32,1,12]{2,1,0:T(1,128)}), f32[32,1,12]{2,1,0:T(1,128)S(1)}, u32[]{:S(2)}, u32[]{:S(2)}) async-start(f32[32,1,12]{2,1,0:T(1,128)} %broadcast_in_dim.13), calls=%async_computation | async-start | bytes 32768 | tf_op jit(solution)/shard_map/all_to_all | solution.py:130
  24.7 4.0 %all-to-all-done = f32[32,1,12]{2,1,0:T(1,128)S(1)} async-done(((f32[32,1,12]{2,1,0:T(1,128)}), f32[32,1,12]{2,1,0:T(1,128)S(1)}, u32[]{:S(2)}, u32[]{:S(2)}) %all-to-all-start) | async-done | bytes 1568 | tf_op jit(solution)/shard_map/all_to_all | solution.py:130
  30.1 3.3 %collective-permute-start.2 = (f32[2,2304]{1,0:T(2,128)S(1)}, f32[2,2304]{1,0:T(2,128)S(1)}, u32[]{:S(2)}, u32[]{:S(2)}) collective-permute-start(f32[2,2304]{1,0:T(2,128)S(1)} %get-tuple-element.18), channel_id=1, source_target_pairs={{1,0},{2,1},{3,2},{4,3},{5,4},{6,5},{7,6},{0,7},{9,8},{10,9},{11,1... | collective-permute-start | bytes 55304 | tf_op jit(solution)/shard_map/ppermute | solution.py:13
  33.4 2.3 %collective-permute-start.3 = (f32[2,2304]{1,0:T(2,128)S(1)}, f32[2,2304]{1,0:T(2,128)S(1)}, u32[]{:S(2)}, u32[]{:S(2)}) collective-permute-start(f32[2,2304]{1,0:T(2,128)S(1)} %get-tuple-element.19), channel_id=1, source_target_pairs={{8,0},{16,8},{24,16},{0,24},{9,1},{17,9},{25,17},{1,25},{10,2},{18... | collective-permute-start | bytes 55304 | tf_op jit(solution)/shard_map/ppermute | solution.py:13
  36.1 1.1 %collective-permute-done.3 = f32[2,2304]{1,0:T(2,128)S(1)} collective-permute-done((f32[2,2304]{1,0:T(2,128)S(1)}, f32[2,2304]{1,0:T(2,128)S(1)}, u32[]{:S(2)}, u32[]{:S(2)}) %collective-permute-start.3) | collective-permute-done | bytes 18464 | tf_op jit(solution)/shard_map/ppermute | solution.py:13
  39.3 2.3 %add_multiply_fusion.1 = f32[2,48,48,48]{3,2,1,0:T(8,128)S(1)} fusion(f32[2,48,48]{2,1,0:T(8,128)S(1)} %get-tuple-element.58, f32[2,48]{1,0:T(2,128)S(1)} %bitcast.381, f32[2,48,48]{2,1,0:T(8,128)S(1)} %get-tuple-element.59, f32[2,48]{1,0:T(2,128)S(1)} %bitcast.378, f32[2,48,48]{2,1,0:T(8,128)S(1)} %get-tuple-element.60, ...), kind=kLoop, calls=%fused_computation.14 | loop fusion | flops 3096576 | bytes 1014912 | tf_op jit(solution)/shard_map/vmap()/mul | solution.py:77
  41.6 2.3 %multiply_reduce_fusion.5 = (f32[2,2,48,48]{3,2,1,0:T(8,128)S(1)}, f32[2,2,48,48]{3,2,1,0:T(8,128)S(1)}, f32[2,2,48,48]{3,2,1,0:T(8,128)S(1)}) fusion(f32[2,48,48,48]{3,2,1,0:T(8,128)S(1)} %add_multiply_fusion.1, f32[2,2,48]{2,1,0:T(2,128)S(1)} %copy.341), kind=kLoop, calls=%fused_computation.5 | loop fusion | flops 2626560 | bytes 996096 | tf_op jit(solution)/shard_map/vmap()/reduce_sum | solution.py:51
  46.8 3.6 %all-to-all-start.1 = ((f32[32,1,14]{2,1,0:T(1,128)}), f32[32,1,14]{2,1,0:T(1,128)S(1)}, u32[]{:S(2)}, u32[]{:S(2)}) async-start(f32[32,1,14]{2,1,0:T(1,128)} %broadcast_in_dim.14), calls=%async_computation.1 | async-start | bytes 32768 | tf_op jit(solution)/shard_map/all_to_all | solution.py:130
  50.7 1.7 %collective-permute-start.7 = (f32[2,2304]{1,0:T(2,128)S(1)}, f32[2,2304]{1,0:T(2,128)S(1)}, u32[]{:S(2)}, u32[]{:S(2)}) collective-permute-start(f32[2,2304]{1,0:T(2,128)S(1)} %get-tuple-element.23), channel_id=1, source_target_pairs={{24,0},{0,8},{8,16},{16,24},{25,1},{1,9},{9,17},{17,25},{26,2},{2,... | collective-permute-start | bytes 55304 | tf_op jit(solution)/shard_map/ppermute | solution.py:13
  52.3 3.1 %collective-permute-start.4 = (f32[2,2304]{1,0:T(2,128)S(1)}, f32[2,2304]{1,0:T(2,128)S(1)}, u32[]{:S(2)}, u32[]{:S(2)}) collective-permute-start(f32[2,2304]{1,0:T(2,128)S(1)} %get-tuple-element.20), channel_id=1, source_target_pairs={{1,0},{2,1},{3,2},{4,3},{5,4},{6,5},{7,6},{0,7},{9,8},{10,9},{11,1... | collective-permute-start | bytes 55304 | tf_op jit(solution)/shard_map/ppermute | solution.py:13
  55.5 1.2 %collective-permute-start.5 = (f32[2,2304]{1,0:T(2,128)S(1)}, f32[2,2304]{1,0:T(2,128)S(1)}, u32[]{:S(2)}, u32[]{:S(2)}) collective-permute-start(f32[2,2304]{1,0:T(2,128)S(1)} %get-tuple-element.21), channel_id=1, source_target_pairs={{8,0},{16,8},{24,16},{0,24},{9,1},{17,9},{25,17},{1,25},{10,2},{18... | collective-permute-start | bytes 55304 | tf_op jit(solution)/shard_map/ppermute | solution.py:13
  56.6 0.9 all-to-all-done.1
  62.5 2.3 %add_multiply_fusion = f32[2,48,48,48]{3,2,1,0:T(8,128)S(1)} fusion(f32[2,48,48]{2,1,0:T(8,128)S(1)} %get-tuple-element.52, f32[2,48,48]{2,1,0:T(8,128)S(1)} %get-tuple-element.53, f32[2,48,48]{2,1,0:T(8,128)S(1)} %get-tuple-element.54, f32[2,48,48]{2,1,0:T(8,128)S(1)} %get-tuple-element.55, f32[2,48,48]{2,1,0:T(8,128)S(1)} %get-tuple-element.56, ...), kind=kLoop, calls=%fused_computation.13 | loop fusion | flops 3096576 | bytes 1014912 | tf_op jit(solution)/shard_map/vmap()/mul | solution.py:77
  64.8 2.3 %multiply_reduce_fusion.2 = (f32[2,2,48,48]{3,2,1,0:T(8,128)S(1)}, f32[2,2,48,48]{3,2,1,0:T(8,128)S(1)}, f32[2,2,48,48]{3,2,1,0:T(8,128)S(1)}) fusion(f32[2,48,48,48]{3,2,1,0:T(8,128)S(1)} %add_multiply_fusion, f32[2,2,48]{2,1,0:T(2,128)S(1)} %copy.341), kind=kLoop, calls=%fused_computation.2 | loop fusion | flops 2626560 | bytes 996096 | tf_op jit(solution)/shard_map/vmap()/reduce_sum | solution.py:51
  70.3 2.5 %all-to-all-start.2 = ((f32[32,1,4]{2,1,0:T(1,128)}), f32[32,1,4]{2,1,0:T(1,128)S(1)}, u32[]{:S(2)}, u32[]{:S(2)}) async-start(f32[32,1,4]{2,1,0:T(1,128)} %broadcast_in_dim.15), calls=%async_computation.2 | async-start | bytes 32768 | tf_op jit(solution)/shard_map/all_to_all | solution.py:130
  72.9 3.4 %collective-permute-start.8 = (f32[2,2304]{1,0:T(2,128)S(1)}, f32[2,2304]{1,0:T(2,128)S(1)}, u32[]{:S(2)}, u32[]{:S(2)}) collective-permute-start(f32[2,2304]{1,0:T(2,128)S(1)} %get-tuple-element.24), channel_id=1, source_target_pairs={{1,0},{2,1},{3,2},{4,3},{5,4},{6,5},{7,6},{0,7},{9,8},{10,9},{11,1... | collective-permute-start | bytes 55304 | tf_op jit(solution)/shard_map/ppermute | solution.py:13
  76.3 2.4 %collective-permute-start.9 = (f32[2,2304]{1,0:T(2,128)S(1)}, f32[2,2304]{1,0:T(2,128)S(1)}, u32[]{:S(2)}, u32[]{:S(2)}) collective-permute-start(f32[2,2304]{1,0:T(2,128)S(1)} %get-tuple-element.25), channel_id=1, source_target_pairs={{8,0},{16,8},{24,16},{0,24},{9,1},{17,9},{25,17},{1,25},{10,2},{18... | collective-permute-start | bytes 55304 | tf_op jit(solution)/shard_map/ppermute | solution.py:13
  78.7 1.2 %all-to-all-done.2 = f32[32,1,4]{2,1,0:T(1,128)S(1)} async-done(((f32[32,1,4]{2,1,0:T(1,128)}), f32[32,1,4]{2,1,0:T(1,128)S(1)}, u32[]{:S(2)}, u32[]{:S(2)}) %all-to-all-start.2) | async-done | bytes 544 | tf_op jit(solution)/shard_map/all_to_all | solution.py:130
  (194 shorter events, 19.6 us)
Async XLA Ops:
  1.5 4.3 %copy-start = (f32[1,1,2,48,48]{4,3,2,1,0:T(8,128)S(1)}, f32[1,1,2,48,48]{4,3,2,1,0:T(8,128)}, u32[]{:S(2)}) copy-start(f32[1,1,2,48,48]{4,3,2,1,0:T(8,128)} %param.7) | copy-start | bytes 55300
  5.8 2.3 %copy-start.2 = (f32[1,1,2,48]{3,2,1,0:T(2,128)S(1)}, f32[1,1,2,48]{3,2,1,0:T(2,128)}, u32[]{:S(2)}) copy-start(f32[1,1,2,48]{3,2,1,0:T(2,128)} %param.8) | copy-start | bytes 1156
  10.7 11.5 %copy-start.1 = (s32[4,8]{1,0:T(4,128)S(1)}, s32[4,8]{1,0:T(4,128)}, u32[]{:S(2)}) copy-start(s32[4,8]{1,0:T(4,128)} %param.10) | copy-start | bytes 388
  10.7 12.3 %copy-start.4 = (f32[1,1,6,48]{3,1,2,0:T(1,128)S(1)}, f32[1,1,6,48]{3,1,2,0:T(1,128)}, u32[]{:S(2)}) copy-start(f32[1,1,6,48]{3,1,2,0:T(1,128)} %param.11) | copy-start | bytes 3460
  10.7 12.4 %copy-start.3 = (f32[1,1,2,3]{3,2,1,0:T(2,128)S(1)}, f32[1,1,2,3]{3,2,1,0:T(2,128)}, u32[]{:S(2)}) copy-start(f32[1,1,2,3]{3,2,1,0:T(2,128)} %param.9) | copy-start | bytes 76
  14.3 14.4 %all-to-all-start = ((f32[32,1,12]{2,1,0:T(1,128)}), f32[32,1,12]{2,1,0:T(1,128)S(1)}, u32[]{:S(2)}, u32[]{:S(2)}) async-start(f32[32,1,12]{2,1,0:T(1,128)} %broadcast_in_dim.13), calls=%async_computation | async-start | bytes 32768 | tf_op jit(solution)/shard_map/all_to_all | solution.py:130
  28.8 8.8 %collective-permute-start = (f32[2,2353]{1,0:T(2,128)S(1)}, f32[2,2353]{1,0:T(2,128)S(1)}, u32[]{:S(2)}, u32[]{:S(2)}) collective-permute-start(f32[2,2353]{1,0:T(2,128)S(1)} %concatenate.210), channel_id=1, source_target_pairs={{7,0},{0,1},{1,2},{2,3},{3,4},{4,5},{5,6},{6,7},{15,8},{8,9},{9,10... | collective-permute-start | bytes 56480 | tf_op jit(solution)/shard_map/ppermute | solution.py:13
  28.8 8.9 %collective-permute-start.1 = (f32[2,2353]{1,0:T(2,128)S(1)}, f32[2,2353]{1,0:T(2,128)S(1)}, u32[]{:S(2)}, u32[]{:S(2)}) collective-permute-start(f32[2,2353]{1,0:T(2,128)S(1)} %concatenate.211), channel_id=1, source_target_pairs={{24,0},{0,8},{8,16},{16,24},{25,1},{1,9},{9,17},{17,25},{26,2},{2,... | collective-permute-start | bytes 56480 | tf_op jit(solution)/shard_map/ppermute | solution.py:13
  30.1 5.9 %collective-permute-start.2 = (f32[2,2304]{1,0:T(2,128)S(1)}, f32[2,2304]{1,0:T(2,128)S(1)}, u32[]{:S(2)}, u32[]{:S(2)}) collective-permute-start(f32[2,2304]{1,0:T(2,128)S(1)} %get-tuple-element.18), channel_id=1, source_target_pairs={{1,0},{2,1},{3,2},{4,3},{5,4},{6,5},{7,6},{0,7},{9,8},{10,9},{11,1... | collective-permute-start | bytes 55304 | tf_op jit(solution)/shard_map/ppermute | solution.py:13
  33.4 3.8 %collective-permute-start.3 = (f32[2,2304]{1,0:T(2,128)S(1)}, f32[2,2304]{1,0:T(2,128)S(1)}, u32[]{:S(2)}, u32[]{:S(2)}) collective-permute-start(f32[2,2304]{1,0:T(2,128)S(1)} %get-tuple-element.19), channel_id=1, source_target_pairs={{8,0},{16,8},{24,16},{0,24},{9,1},{17,9},{25,17},{1,25},{10,2},{18... | collective-permute-start | bytes 55304 | tf_op jit(solution)/shard_map/ppermute | solution.py:13
  46.8 10.7 %all-to-all-start.1 = ((f32[32,1,14]{2,1,0:T(1,128)}), f32[32,1,14]{2,1,0:T(1,128)S(1)}, u32[]{:S(2)}, u32[]{:S(2)}) async-start(f32[32,1,14]{2,1,0:T(1,128)} %broadcast_in_dim.14), calls=%async_computation.1 | async-start | bytes 32768 | tf_op jit(solution)/shard_map/all_to_all | solution.py:130
  50.4 11.1 %collective-permute-start.6 = (f32[2,2304]{1,0:T(2,128)S(1)}, f32[2,2304]{1,0:T(2,128)S(1)}, u32[]{:S(2)}, u32[]{:S(2)}) collective-permute-start(f32[2,2304]{1,0:T(2,128)S(1)} %get-tuple-element.22), channel_id=1, source_target_pairs={{7,0},{0,1},{1,2},{2,3},{3,4},{4,5},{5,6},{6,7},{15,8},{8,9},{9,10... | collective-permute-start | bytes 55304 | tf_op jit(solution)/shard_map/ppermute | solution.py:13
  50.7 10.8 %collective-permute-start.7 = (f32[2,2304]{1,0:T(2,128)S(1)}, f32[2,2304]{1,0:T(2,128)S(1)}, u32[]{:S(2)}, u32[]{:S(2)}) collective-permute-start(f32[2,2304]{1,0:T(2,128)S(1)} %get-tuple-element.23), channel_id=1, source_target_pairs={{24,0},{0,8},{8,16},{16,24},{25,1},{1,9},{9,17},{17,25},{26,2},{2,... | collective-permute-start | bytes 55304 | tf_op jit(solution)/shard_map/ppermute | solution.py:13
  52.3 8.6 %collective-permute-start.4 = (f32[2,2304]{1,0:T(2,128)S(1)}, f32[2,2304]{1,0:T(2,128)S(1)}, u32[]{:S(2)}, u32[]{:S(2)}) collective-permute-start(f32[2,2304]{1,0:T(2,128)S(1)} %get-tuple-element.20), channel_id=1, source_target_pairs={{1,0},{2,1},{3,2},{4,3},{5,4},{6,5},{7,6},{0,7},{9,8},{10,9},{11,1... | collective-permute-start | bytes 55304 | tf_op jit(solution)/shard_map/ppermute | solution.py:13
  55.5 5.5 %collective-permute-start.5 = (f32[2,2304]{1,0:T(2,128)S(1)}, f32[2,2304]{1,0:T(2,128)S(1)}, u32[]{:S(2)}, u32[]{:S(2)}) collective-permute-start(f32[2,2304]{1,0:T(2,128)S(1)} %get-tuple-element.21), channel_id=1, source_target_pairs={{8,0},{16,8},{24,16},{0,24},{9,1},{17,9},{25,17},{1,25},{10,2},{18... | collective-permute-start | bytes 55304 | tf_op jit(solution)/shard_map/ppermute | solution.py:13
  70.3 9.6 %all-to-all-start.2 = ((f32[32,1,4]{2,1,0:T(1,128)}), f32[32,1,4]{2,1,0:T(1,128)S(1)}, u32[]{:S(2)}, u32[]{:S(2)}) async-start(f32[32,1,4]{2,1,0:T(1,128)} %broadcast_in_dim.15), calls=%async_computation.2 | async-start | bytes 32768 | tf_op jit(solution)/shard_map/all_to_all | solution.py:130
  72.9 12.9 %collective-permute-start.8 = (f32[2,2304]{1,0:T(2,128)S(1)}, f32[2,2304]{1,0:T(2,128)S(1)}, u32[]{:S(2)}, u32[]{:S(2)}) collective-permute-start(f32[2,2304]{1,0:T(2,128)S(1)} %get-tuple-element.24), channel_id=1, source_target_pairs={{1,0},{2,1},{3,2},{4,3},{5,4},{6,5},{7,6},{0,7},{9,8},{10,9},{11,1... | collective-permute-start | bytes 55304 | tf_op jit(solution)/shard_map/ppermute | solution.py:13
  76.3 9.4 %collective-permute-start.9 = (f32[2,2304]{1,0:T(2,128)S(1)}, f32[2,2304]{1,0:T(2,128)S(1)}, u32[]{:S(2)}, u32[]{:S(2)}) collective-permute-start(f32[2,2304]{1,0:T(2,128)S(1)} %get-tuple-element.25), channel_id=1, source_target_pairs={{8,0},{16,8},{24,16},{0,24},{9,1},{17,9},{25,17},{1,25},{10,2},{18... | collective-permute-start | bytes 55304 | tf_op jit(solution)/shard_map/ppermute | solution.py:13

commit v11 on v9

--- a/solution.py
+++ b/solution.py
@@ -253,6 +253,7 @@
     applied = fz_own + ratio * img_own
     multiplier = multiplier + step_two * direction
     residual = res_own - step_two * applied
+    multiplier = lax.optimization_barrier(multiplier)
     return (multiplier[None, None], residual[None, None])
 
 

time: 83.7 us -> 83.4 us (level)
  transfers between devices with their start and end apart: 13 -> 13, of which waited for: 5 -> 5; matrix products, arithmetic and copies ran while one was open for 9% -> 10% of each run, Pallas kernels for 0% -> 0%
where the time goes in v11:
time: 83.4 us; the launch traced here: 83.1 us
  starting transfers between devices  26.8 us (32%)
  other arithmetic  16.4 us (20%)
  local copies, waits for them, and re-layouts  12.3 us (15%)
  matrix products  11.2 us (13%)
  waiting for transfers between devices  9.15 us (11%)
  between operations  7.25 us (9%)
    ppermute x10, starting transfers between devices, shifted(): return lax.ppermute(block, axis, route)  14.4 us
    all_to_all x3, starting transfers between devices, gather_all(): got = lax.all_to_all(spread, ('grp', 'dev'), 0, 0, tiled=True)  12.4 us
    reduce_sum x3, other arithmetic, trace_solved(): along_a = jnp.sum(end_rows[:, :, None, None] * solved[None], axis=1)  6.94 us
    all_to_all x3, waiting for transfers between devices, gather_all(): got = lax.all_to_all(spread, ('grp', 'dev'), 0, 0, tiled=True)  5.97 us
    mul x2, other arithmetic, apply_one(): one_inverse * face_spectrum(one_transform, low_side, high_side)  4.61 us
    ppermute x10, waiting for transfers between devices, shifted(): return lax.ppermute(block, axis, route)  3.18 us
    dot_general x6, matrix products, trace_solved(): jnp.einsum('bj,edjk,ck->edbc', transform, planes, transform, precision=FAST)  2.74 us
    reshape x1, local copies, waits for them, and re-layouts, spectral(): spatial = patch_load.astype(jnp.float32).reshape(points, points, points)  2.66 us
  transfers between devices with their start and end apart: 13, of which 5 were waited for; matrix products, arithmetic and copies ran while one was open for 10% of the time, Pallas kernels for 0%

profile of v11, /device:TPU:0, one launch (start us, length us, event | category | flops | bytes accessed | tf_op | source)
XLA Modules:
  0.0 83.1 jit_solution(9464552936187966032)
XLA Ops:
  0.6 0.8 broadcast_add_fusion
  1.5 2.7 %reshape.1117 = bf16[2,48,48,48]{3,2,1,0:T(8,128)(2,1)S(1)} reshape(bf16[1,1,2,48,2304]{4,3,2,1,0:T(8,128)(2,1)} %param.6) | data formatting | bytes 884736 | tf_op jit(solution)/shard_map/vmap()/reshape | solution.py:22
  4.1 1.6 %fusion.7 = f32[2,48,48,48]{3,1,2,0:T(8,128)S(1)} fusion(bf16[2,48,48,48]{3,2,1,0:T(8,128)(2,1)S(1)} %reshape.1117, f32[1,1,2,48,48]{4,3,2,1,0:T(8,128)} %param.7), kind=kOutput, calls=%fused_computation.17 | convolution fusion | flops 63700992 | bytes 1345536 | tf_op jit(solution)/shard_map/vmap(ai,abc->ibc)/dot_general | solution.py:23
  5.8 2.2 %fusion.2 = f32[2,48,48,48]{3,2,1,0:T(8,128)S(1)} fusion(f32[2,48,48,48]{3,1,2,0:T(8,128)S(1)} %fusion.7, f32[1,1,2,48,48]{4,3,2,1,0:T(8,128)S(1)} %copy-done), kind=kOutput, calls=%fused_computation.11 | convolution fusion | flops 63700992 | bytes 1787904 | tf_op jit(solution)/shard_map/vmap(bj,ibc->ijc)/dot_general | solution.py:24
  8.1 2.6 %fusion.4 = f32[2,48,48,48]{3,2,1,0:T(8,128)S(1)} fusion(f32[2,48,48,48]{3,2,1,0:T(8,128)S(1)} %fusion.2, f32[2,48]{1,0:T(2,128)S(1)} %bitcast.419, f32[2,48,48]{2,1,0:T(8,128)S(1)} %broadcast_add_fusion, f32[1,1,2,48,48]{4,3,2,1,0:T(8,128)S(1)} %copy-done), kind=kOutput, calls=%fused_computation.16 | convolution fusion | flops 64364544 | bytes 1806720 | tf_op jit(solution)/shard_map/vmap(ck,ijc->ijk)/dot_general | solution.py:25
  10.7 2.3 %multiply_reduce_fusion.8 = (f32[2,2,48,48]{3,2,1,0:T(8,128)S(1)}, f32[2,2,48,48]{3,2,1,0:T(8,128)S(1)}, f32[2,2,48,48]{3,2,1,0:T(8,128)S(1)}) fusion(f32[2,48,48,48]{3,2,1,0:T(8,128)S(1)} %fusion.4, f32[2,2,48]{2,1,0:T(2,128)S(1)} %copy.336), kind=kLoop, calls=%fused_computation.8 | loop fusion | flops 2626560 | bytes 996096 | tf_op jit(solution)/shard_map/vmap()/reduce_sum | solution.py:51
  14.3 7.3 %all-to-all-start = ((f32[32,1,12]{2,1,0:T(1,128)}), f32[32,1,12]{2,1,0:T(1,128)S(1)}, u32[]{:S(2)}, u32[]{:S(2)}) async-start(f32[32,1,12]{2,1,0:T(1,128)} %broadcast_in_dim.11), calls=%async_computation | async-start | bytes 32768 | tf_op jit(solution)/shard_map/all_to_all | solution.py:130
  24.7 4.0 %all-to-all-done = f32[32,1,12]{2,1,0:T(1,128)S(1)} async-done(((f32[32,1,12]{2,1,0:T(1,128)}), f32[32,1,12]{2,1,0:T(1,128)S(1)}, u32[]{:S(2)}, u32[]{:S(2)}) %all-to-all-start) | async-done | bytes 1568 | tf_op jit(solution)/shard_map/all_to_all | solution.py:130
  28.8 1.8 %collective-permute-start.3 = (f32[2,2304]{1,0:T(2,128)S(1)}, f32[2,2304]{1,0:T(2,128)S(1)}, u32[]{:S(2)}, u32[]{:S(2)}) collective-permute-start(f32[2,2304]{1,0:T(2,128)S(1)} %get-tuple-element.17), channel_id=1, source_target_pairs={{8,0},{16,8},{24,16},{0,24},{9,1},{17,9},{25,17},{1,25},{10,2},{18... | collective-permute-start | bytes 55304 | tf_op jit(solution)/shard_map/ppermute | solution.py:13
  33.0 2.6 %collective-permute-done = f32[2,2353]{1,0:T(2,128)S(1)} collective-permute-done((f32[2,2353]{1,0:T(2,128)S(1)}, f32[2,2353]{1,0:T(2,128)S(1)}, u32[]{:S(2)}, u32[]{:S(2)}) %collective-permute-start) | collective-permute-done | bytes 18856 | tf_op jit(solution)/shard_map/ppermute | solution.py:13
  37.3 2.3 %add_multiply_fusion.1 = f32[2,48,48,48]{3,2,1,0:T(8,128)S(1)} fusion(f32[2,48,48]{2,1,0:T(8,128)S(1)} %get-tuple-element.65, f32[2,48]{1,0:T(2,128)S(1)} %bitcast.408, f32[2,48,48]{2,1,0:T(8,128)S(1)} %get-tuple-element.66, f32[2,48]{1,0:T(2,128)S(1)} %bitcast.405, f32[2,48,48]{2,1,0:T(8,128)S(1)} %get-tuple-element.67, ...), kind=kLoop, calls=%fused_computation.14 | loop fusion | flops 3096576 | bytes 1014912 | tf_op jit(solution)/shard_map/vmap()/mul | solution.py:77
  39.6 2.3 %multiply_reduce_fusion.5 = (f32[2,2,48,48]{3,2,1,0:T(8,128)S(1)}, f32[2,2,48,48]{3,2,1,0:T(8,128)S(1)}, f32[2,2,48,48]{3,2,1,0:T(8,128)S(1)}) fusion(f32[2,48,48,48]{3,2,1,0:T(8,128)S(1)} %add_multiply_fusion.1, f32[2,2,48]{2,1,0:T(2,128)S(1)} %copy.336), kind=kLoop, calls=%fused_computation.5 | loop fusion | flops 2626560 | bytes 996096 | tf_op jit(solution)/shard_map/vmap()/reduce_sum | solution.py:51
  44.8 2.5 %all-to-all-start.1 = ((f32[32,1,14]{2,1,0:T(1,128)}), f32[32,1,14]{2,1,0:T(1,128)S(1)}, u32[]{:S(2)}, u32[]{:S(2)}) async-start(f32[32,1,14]{2,1,0:T(1,128)} %broadcast_in_dim.12), calls=%async_computation.1 | async-start | bytes 32768 | tf_op jit(solution)/shard_map/all_to_all | solution.py:130
  47.5 1.7 %collective-permute-start.7 = (f32[2,2304]{1,0:T(2,128)S(1)}, f32[2,2304]{1,0:T(2,128)S(1)}, u32[]{:S(2)}, u32[]{:S(2)}) collective-permute-start(f32[2,2304]{1,0:T(2,128)S(1)} %get-tuple-element.21), channel_id=1, source_target_pairs={{24,0},{0,8},{8,16},{16,24},{25,1},{1,9},{9,17},{17,25},{26,2},{2,... | collective-permute-start | bytes 55304 | tf_op jit(solution)/shard_map/ppermute | solution.py:13
  49.2 3.1 %collective-permute-start.4 = (f32[2,2304]{1,0:T(2,128)S(1)}, f32[2,2304]{1,0:T(2,128)S(1)}, u32[]{:S(2)}, u32[]{:S(2)}) collective-permute-start(f32[2,2304]{1,0:T(2,128)S(1)} %get-tuple-element.18), channel_id=1, source_target_pairs={{1,0},{2,1},{3,2},{4,3},{5,4},{6,5},{7,6},{0,7},{9,8},{10,9},{11,1... | collective-permute-start | bytes 55304 | tf_op jit(solution)/shard_map/ppermute | solution.py:13
  52.3 1.3 %collective-permute-start.5 = (f32[2,2304]{1,0:T(2,128)S(1)}, f32[2,2304]{1,0:T(2,128)S(1)}, u32[]{:S(2)}, u32[]{:S(2)}) collective-permute-start(f32[2,2304]{1,0:T(2,128)S(1)} %get-tuple-element.19), channel_id=1, source_target_pairs={{8,0},{16,8},{24,16},{0,24},{9,1},{17,9},{25,17},{1,25},{10,2},{18... | collective-permute-start | bytes 55304 | tf_op jit(solution)/shard_map/ppermute | solution.py:13
  53.6 0.8 all-to-all-done.1
  59.2 2.3 %add_multiply_fusion = f32[2,48,48,48]{3,2,1,0:T(8,128)S(1)} fusion(f32[2,48,48]{2,1,0:T(8,128)S(1)} %get-tuple-element.59, f32[2,48,48]{2,1,0:T(8,128)S(1)} %get-tuple-element.60, f32[2,48,48]{2,1,0:T(8,128)S(1)} %get-tuple-element.61, f32[2,48,48]{2,1,0:T(8,128)S(1)} %get-tuple-element.62, f32[2,48,48]{2,1,0:T(8,128)S(1)} %get-tuple-element.63, ...), kind=kLoop, calls=%fused_computation.13 | loop fusion | flops 3096576 | bytes 1014912 | tf_op jit(solution)/shard_map/vmap()/mul | solution.py:77
  61.5 2.3 %multiply_reduce_fusion.2 = (f32[2,2,48,48]{3,2,1,0:T(8,128)S(1)}, f32[2,2,48,48]{3,2,1,0:T(8,128)S(1)}, f32[2,2,48,48]{3,2,1,0:T(8,128)S(1)}) fusion(f32[2,48,48,48]{3,2,1,0:T(8,128)S(1)} %add_multiply_fusion, f32[2,2,48]{2,1,0:T(2,128)S(1)} %copy.336), kind=kLoop, calls=%fused_computation.2 | loop fusion | flops 2626560 | bytes 996096 | tf_op jit(solution)/shard_map/vmap()/reduce_sum | solution.py:51
  66.6 2.5 %all-to-all-start.2 = ((f32[32,1,4]{2,1,0:T(1,128)}), f32[32,1,4]{2,1,0:T(1,128)S(1)}, u32[]{:S(2)}, u32[]{:S(2)}) async-start(f32[32,1,4]{2,1,0:T(1,128)} %broadcast_in_dim.13), calls=%async_computation.2 | async-start | bytes 32768 | tf_op jit(solution)/shard_map/all_to_all | solution.py:130
  69.2 3.4 %collective-permute-start.8 = (f32[2,2304]{1,0:T(2,128)S(1)}, f32[2,2304]{1,0:T(2,128)S(1)}, u32[]{:S(2)}, u32[]{:S(2)}) collective-permute-start(f32[2,2304]{1,0:T(2,128)S(1)} %get-tuple-element.22), channel_id=1, source_target_pairs={{1,0},{2,1},{3,2},{4,3},{5,4},{6,5},{7,6},{0,7},{9,8},{10,9},{11,1... | collective-permute-start | bytes 55304 | tf_op jit(solution)/shard_map/ppermute | solution.py:13
  72.6 2.4 %collective-permute-start.9 = (f32[2,2304]{1,0:T(2,128)S(1)}, f32[2,2304]{1,0:T(2,128)S(1)}, u32[]{:S(2)}, u32[]{:S(2)}) collective-permute-start(f32[2,2304]{1,0:T(2,128)S(1)} %get-tuple-element.23), channel_id=1, source_target_pairs={{8,0},{16,8},{24,16},{0,24},{9,1},{17,9},{25,17},{1,25},{10,2},{18... | collective-permute-start | bytes 55304 | tf_op jit(solution)/shard_map/ppermute | solution.py:13
  75.0 1.2 %all-to-all-done.2 = f32[32,1,4]{2,1,0:T(1,128)S(1)} async-done(((f32[32,1,4]{2,1,0:T(1,128)}), f32[32,1,4]{2,1,0:T(1,128)S(1)}, u32[]{:S(2)}, u32[]{:S(2)}) %all-to-all-start.2) | async-done | bytes 544 | tf_op jit(solution)/shard_map/all_to_all | solution.py:130
  81.3 0.8 multiply_add_fusion
  (191 shorter events, 18.9 us)
Async XLA Ops:
  1.5 4.3 %copy-start = (f32[1,1,2,48,48]{4,3,2,1,0:T(8,128)S(1)}, f32[1,1,2,48,48]{4,3,2,1,0:T(8,128)}, u32[]{:S(2)}) copy-start(f32[1,1,2,48,48]{4,3,2,1,0:T(8,128)} %param.7) | copy-start | bytes 55300
  5.8 2.3 %copy-start.2 = (f32[1,1,2,48]{3,2,1,0:T(2,128)S(1)}, f32[1,1,2,48]{3,2,1,0:T(2,128)}, u32[]{:S(2)}) copy-start(f32[1,1,2,48]{3,2,1,0:T(2,128)} %param.8) | copy-start | bytes 1156
  10.7 12.2 %copy-start.1 = (s32[4,8]{1,0:T(4,128)S(1)}, s32[4,8]{1,0:T(4,128)}, u32[]{:S(2)}) copy-start(s32[4,8]{1,0:T(4,128)} %param.10) | copy-start | bytes 388
  10.7 12.3 %copy-start.4 = (f32[1,1,6,48]{3,1,2,0:T(1,128)S(1)}, f32[1,1,6,48]{3,1,2,0:T(1,128)}, u32[]{:S(2)}) copy-start(f32[1,1,6,48]{3,1,2,0:T(1,128)} %param.11) | copy-start | bytes 3460
  10.7 12.4 %copy-start.3 = (f32[1,1,2,3]{3,2,1,0:T(2,128)S(1)}, f32[1,1,2,3]{3,2,1,0:T(2,128)}, u32[]{:S(2)}) copy-start(f32[1,1,2,3]{3,2,1,0:T(2,128)} %param.9) | copy-start | bytes 76
  14.3 14.4 %all-to-all-start = ((f32[32,1,12]{2,1,0:T(1,128)}), f32[32,1,12]{2,1,0:T(1,128)S(1)}, u32[]{:S(2)}, u32[]{:S(2)}) async-start(f32[32,1,12]{2,1,0:T(1,128)} %broadcast_in_dim.11), calls=%async_computation | async-start | bytes 32768 | tf_op jit(solution)/shard_map/all_to_all | solution.py:130
  28.8 3.3 %collective-permute-start.2 = (f32[2,2304]{1,0:T(2,128)S(1)}, f32[2,2304]{1,0:T(2,128)S(1)}, u32[]{:S(2)}, u32[]{:S(2)}) collective-permute-start(f32[2,2304]{1,0:T(2,128)S(1)} %get-tuple-element.16), channel_id=1, source_target_pairs={{1,0},{2,1},{3,2},{4,3},{5,4},{6,5},{7,6},{0,7},{9,8},{10,9},{11,1... | collective-permute-start | bytes 55304 | tf_op jit(solution)/shard_map/ppermute | solution.py:13
  28.8 3.8 %collective-permute-start.3 = (f32[2,2304]{1,0:T(2,128)S(1)}, f32[2,2304]{1,0:T(2,128)S(1)}, u32[]{:S(2)}, u32[]{:S(2)}) collective-permute-start(f32[2,2304]{1,0:T(2,128)S(1)} %get-tuple-element.17), channel_id=1, source_target_pairs={{8,0},{16,8},{24,16},{0,24},{9,1},{17,9},{25,17},{1,25},{10,2},{18... | collective-permute-start | bytes 55304 | tf_op jit(solution)/shard_map/ppermute | solution.py:13
  30.6 5.0 %collective-permute-start = (f32[2,2353]{1,0:T(2,128)S(1)}, f32[2,2353]{1,0:T(2,128)S(1)}, u32[]{:S(2)}, u32[]{:S(2)}) collective-permute-start(f32[2,2353]{1,0:T(2,128)S(1)} %concatenate.231), channel_id=1, source_target_pairs={{7,0},{0,1},{1,2},{2,3},{3,4},{4,5},{5,6},{6,7},{15,8},{8,9},{9,10... | collective-permute-start | bytes 56480 | tf_op jit(solution)/shard_map/ppermute | solution.py:13
  30.6 5.1 %collective-permute-start.1 = (f32[2,2353]{1,0:T(2,128)S(1)}, f32[2,2353]{1,0:T(2,128)S(1)}, u32[]{:S(2)}, u32[]{:S(2)}) collective-permute-start(f32[2,2353]{1,0:T(2,128)S(1)} %concatenate.232), channel_id=1, source_target_pairs={{24,0},{0,8},{8,16},{16,24},{25,1},{1,9},{9,17},{17,25},{26,2},{2,... | collective-permute-start | bytes 56480 | tf_op jit(solution)/shard_map/ppermute | solution.py:13
  44.8 9.7 %all-to-all-start.1 = ((f32[32,1,14]{2,1,0:T(1,128)}), f32[32,1,14]{2,1,0:T(1,128)S(1)}, u32[]{:S(2)}, u32[]{:S(2)}) async-start(f32[32,1,14]{2,1,0:T(1,128)} %broadcast_in_dim.12), calls=%async_computation.1 | async-start | bytes 32768 | tf_op jit(solution)/shard_map/all_to_all | solution.py:130
  47.4 10.7 %collective-permute-start.6 = (f32[2,2304]{1,0:T(2,128)S(1)}, f32[2,2304]{1,0:T(2,128)S(1)}, u32[]{:S(2)}, u32[]{:S(2)}) collective-permute-start(f32[2,2304]{1,0:T(2,128)S(1)} %get-tuple-element.20), channel_id=1, source_target_pairs={{7,0},{0,1},{1,2},{2,3},{3,4},{4,5},{5,6},{6,7},{15,8},{8,9},{9,10... | collective-permute-start | bytes 55304 | tf_op jit(solution)/shard_map/ppermute | solution.py:13
  47.5 10.5 %collective-permute-start.7 = (f32[2,2304]{1,0:T(2,128)S(1)}, f32[2,2304]{1,0:T(2,128)S(1)}, u32[]{:S(2)}, u32[]{:S(2)}) collective-permute-start(f32[2,2304]{1,0:T(2,128)S(1)} %get-tuple-element.21), channel_id=1, source_target_pairs={{24,0},{0,8},{8,16},{16,24},{25,1},{1,9},{9,17},{17,25},{26,2},{2,... | collective-permute-start | bytes 55304 | tf_op jit(solution)/shard_map/ppermute | solution.py:13
  49.2 8.6 %collective-permute-start.4 = (f32[2,2304]{1,0:T(2,128)S(1)}, f32[2,2304]{1,0:T(2,128)S(1)}, u32[]{:S(2)}, u32[]{:S(2)}) collective-permute-start(f32[2,2304]{1,0:T(2,128)S(1)} %get-tuple-element.18), channel_id=1, source_target_pairs={{1,0},{2,1},{3,2},{4,3},{5,4},{6,5},{7,6},{0,7},{9,8},{10,9},{11,1... | collective-permute-start | bytes 55304 | tf_op jit(solution)/shard_map/ppermute | solution.py:13
  52.3 5.5 %collective-permute-start.5 = (f32[2,2304]{1,0:T(2,128)S(1)}, f32[2,2304]{1,0:T(2,128)S(1)}, u32[]{:S(2)}, u32[]{:S(2)}) collective-permute-start(f32[2,2304]{1,0:T(2,128)S(1)} %get-tuple-element.19), channel_id=1, source_target_pairs={{8,0},{16,8},{24,16},{0,24},{9,1},{17,9},{25,17},{1,25},{10,2},{18... | collective-permute-start | bytes 55304 | tf_op jit(solution)/shard_map/ppermute | solution.py:13
  66.6 9.6 %all-to-all-start.2 = ((f32[32,1,4]{2,1,0:T(1,128)}), f32[32,1,4]{2,1,0:T(1,128)S(1)}, u32[]{:S(2)}, u32[]{:S(2)}) async-start(f32[32,1,4]{2,1,0:T(1,128)} %broadcast_in_dim.13), calls=%async_computation.2 | async-start | bytes 32768 | tf_op jit(solution)/shard_map/all_to_all | solution.py:130
  69.2 12.9 %collective-permute-start.8 = (f32[2,2304]{1,0:T(2,128)S(1)}, f32[2,2304]{1,0:T(2,128)S(1)}, u32[]{:S(2)}, u32[]{:S(2)}) collective-permute-start(f32[2,2304]{1,0:T(2,128)S(1)} %get-tuple-element.22), channel_id=1, source_target_pairs={{1,0},{2,1},{3,2},{4,3},{5,4},{6,5},{7,6},{0,7},{9,8},{10,9},{11,1... | collective-permute-start | bytes 55304 | tf_op jit(solution)/shard_map/ppermute | solution.py:13
  72.6 9.5 %collective-permute-start.9 = (f32[2,2304]{1,0:T(2,128)S(1)}, f32[2,2304]{1,0:T(2,128)S(1)}, u32[]{:S(2)}, u32[]{:S(2)}) collective-permute-start(f32[2,2304]{1,0:T(2,128)S(1)} %get-tuple-element.23), channel_id=1, source_target_pairs={{8,0},{16,8},{24,16},{0,24},{9,1},{17,9},{25,17},{1,25},{10,2},{18... | collective-permute-start | bytes 55304 | tf_op jit(solution)/shard_map/ppermute | solution.py:13

commit v12 on v11

--- a/solution.py
+++ b/solution.py
@@ -150,10 +150,11 @@
     def coarse(means):
         here = means[group_index]
         before = means[prev_group]
-        own = jnp.dot(coarse_rows, here, precision=PRECISE).reshape(slot_count, 3)
-        first = jnp.dot(rows_in[:, 0], here, precision=PRECISE)
-        second = jnp.dot(rows_in[:, 1], before, precision=PRECISE)
-        return own, jnp.stack([first, second], axis=1)
+        near = jnp.concatenate([coarse_rows, rows_in[:, 0]], axis=0)
+        values = jnp.sum(near * here[None, :], axis=1)
+        second = jnp.sum(rows_in[:, 1] * before[None, :], axis=1)
+        own = values[: slot_count * 3].reshape(slot_count, 3)
+        return own, jnp.stack([values[slot_count * 3 :], second], axis=1)
 
     def jumps(traces_now, both, extra=None, after=None):
         low_side = traces_now[:, 0]

time: 83.4 us -> 83.9 us (level)
  matrix products: 11.2 us -> 10.3 us
    dot_general x6 -> x0, matrix products: 0.89 us -> none  [the longest x2 0.37 us: coarse(): own = jnp.dot(coarse_rows, here, precision=PRECISE).reshape(slot_count, 3)]
  transfers between devices with their start and end apart: 13 -> 13, of which waited for: 5 -> 5; matrix products, arithmetic and copies ran while one was open for 10% -> 9% of each run, Pallas kernels for 0% -> 0%
where the time goes in v12:
time: 83.9 us; the launch traced here: 83.5 us
  starting transfers between devices  26.8 us (32%)
  other arithmetic  16.8 us (20%)
  local copies, waits for them, and re-layouts  12.6 us (15%)
  matrix products  10.3 us (12%)
  waiting for transfers between devices  9.83 us (12%)
  between operations  7.19 us (9%)
    ppermute x10, starting transfers between devices, shifted(): return lax.ppermute(block, axis, route)  14.4 us
    all_to_all x3, starting transfers between devices, gather_all(): got = lax.all_to_all(spread, ('grp', 'dev'), 0, 0, tiled=True)  12.4 us
    reduce_sum x3, other arithmetic, trace_solved(): along_a = jnp.sum(end_rows[:, :, None, None] * solved[None], axis=1)  6.94 us
    all_to_all x3, waiting for transfers between devices, gather_all(): got = lax.all_to_all(spread, ('grp', 'dev'), 0, 0, tiled=True)  5.96 us
    mul x2, other arithmetic, apply_one(): one_inverse * face_spectrum(one_transform, low_side, high_side)  4.61 us
    ppermute x10, waiting for transfers between devices, shifted(): return lax.ppermute(block, axis, route)  3.87 us
    dot_general x6, matrix products, trace_solved(): jnp.einsum('bj,edjk,ck->edbc', transform, planes, transform, precision=FAST)  2.74 us
    reshape x1, local copies, waits for them, and re-layouts, spectral(): spatial = patch_load.astype(jnp.float32).reshape(points, points, points)  2.66 us
  transfers between devices with their start and end apart: 13, of which 5 were waited for; matrix products, arithmetic and copies ran while one was open for 9% of the time, Pallas kernels for 0%

profile of v12, /device:TPU:0, one launch (start us, length us, event | category | flops | bytes accessed | tf_op | source)
XLA Modules:
  0.0 83.5 jit_solution(7259381435445205820)
XLA Ops:
  0.6 0.8 broadcast_add_fusion
  1.5 2.7 %reshape.1120 = bf16[2,48,48,48]{3,2,1,0:T(8,128)(2,1)S(1)} reshape(bf16[1,1,2,48,2304]{4,3,2,1,0:T(8,128)(2,1)} %param.6) | data formatting | bytes 884736 | tf_op jit(solution)/shard_map/vmap()/reshape | solution.py:22
  4.1 1.6 %fusion.7 = f32[2,48,48,48]{3,1,2,0:T(8,128)S(1)} fusion(bf16[2,48,48,48]{3,2,1,0:T(8,128)(2,1)S(1)} %reshape.1120, f32[1,1,2,48,48]{4,3,2,1,0:T(8,128)} %param.7), kind=kOutput, calls=%fused_computation.17 | convolution fusion | flops 63700992 | bytes 1345536 | tf_op jit(solution)/shard_map/vmap(ai,abc->ibc)/dot_general | solution.py:23
  5.8 2.2 %fusion.2 = f32[2,48,48,48]{3,2,1,0:T(8,128)S(1)} fusion(f32[2,48,48,48]{3,1,2,0:T(8,128)S(1)} %fusion.7, f32[1,1,2,48,48]{4,3,2,1,0:T(8,128)S(1)} %copy-done), kind=kOutput, calls=%fused_computation.11 | convolution fusion | flops 63700992 | bytes 1787904 | tf_op jit(solution)/shard_map/vmap(bj,ibc->ijc)/dot_general | solution.py:24
  8.1 2.6 %fusion.4 = f32[2,48,48,48]{3,2,1,0:T(8,128)S(1)} fusion(f32[2,48,48,48]{3,2,1,0:T(8,128)S(1)} %fusion.2, f32[2,48]{1,0:T(2,128)S(1)} %bitcast.395, f32[2,48,48]{2,1,0:T(8,128)S(1)} %broadcast_add_fusion, f32[1,1,2,48,48]{4,3,2,1,0:T(8,128)S(1)} %copy-done), kind=kOutput, calls=%fused_computation.16 | convolution fusion | flops 64364544 | bytes 1806720 | tf_op jit(solution)/shard_map/vmap(ck,ijc->ijk)/dot_general | solution.py:25
  10.7 2.3 %multiply_reduce_fusion.8 = (f32[2,2,48,48]{3,2,1,0:T(8,128)S(1)}, f32[2,2,48,48]{3,2,1,0:T(8,128)S(1)}, f32[2,2,48,48]{3,2,1,0:T(8,128)S(1)}) fusion(f32[2,48,48,48]{3,2,1,0:T(8,128)S(1)} %fusion.4, f32[2,2,48]{2,1,0:T(2,128)S(1)} %copy.336), kind=kLoop, calls=%fused_computation.8 | loop fusion | flops 2626560 | bytes 996096 | tf_op jit(solution)/shard_map/vmap()/reduce_sum | solution.py:51
  14.3 7.3 %all-to-all-start = ((f32[32,1,12]{2,1,0:T(1,128)}), f32[32,1,12]{2,1,0:T(1,128)S(1)}, u32[]{:S(2)}, u32[]{:S(2)}) async-start(f32[32,1,12]{2,1,0:T(1,128)} %broadcast_in_dim.11), calls=%async_computation | async-start | bytes 32768 | tf_op jit(solution)/shard_map/all_to_all | solution.py:130
  24.7 4.0 %all-to-all-done = f32[32,1,12]{2,1,0:T(1,128)S(1)} async-done(((f32[32,1,12]{2,1,0:T(1,128)}), f32[32,1,12]{2,1,0:T(1,128)S(1)}, u32[]{:S(2)}, u32[]{:S(2)}) %all-to-all-start) | async-done | bytes 1568 | tf_op jit(solution)/shard_map/all_to_all | solution.py:130
  28.8 1.8 %collective-permute-start.3 = (f32[2,2304]{1,0:T(2,128)S(1)}, f32[2,2304]{1,0:T(2,128)S(1)}, u32[]{:S(2)}, u32[]{:S(2)}) collective-permute-start(f32[2,2304]{1,0:T(2,128)S(1)} %get-tuple-element.17), channel_id=1, source_target_pairs={{8,0},{16,8},{24,16},{0,24},{9,1},{17,9},{25,17},{1,25},{10,2},{18... | collective-permute-start | bytes 55304 | tf_op jit(solution)/shard_map/ppermute | solution.py:13
  31.8 0.9 %collective-permute-done.3 = f32[2,2304]{1,0:T(2,128)S(1)} collective-permute-done((f32[2,2304]{1,0:T(2,128)S(1)}, f32[2,2304]{1,0:T(2,128)S(1)}, u32[]{:S(2)}, u32[]{:S(2)}) %collective-permute-start.3) | collective-permute-done | bytes 18464 | tf_op jit(solution)/shard_map/ppermute | solution.py:13
  32.7 3.0 %collective-permute-done = f32[2,2353]{1,0:T(2,128)S(1)} collective-permute-done((f32[2,2353]{1,0:T(2,128)S(1)}, f32[2,2353]{1,0:T(2,128)S(1)}, u32[]{:S(2)}, u32[]{:S(2)}) %collective-permute-start) | collective-permute-done | bytes 18856 | tf_op jit(solution)/shard_map/ppermute | solution.py:13
  37.9 2.3 %add_multiply_fusion.1 = f32[2,48,48,48]{3,2,1,0:T(8,128)S(1)} fusion(f32[2,48,48]{2,1,0:T(8,128)S(1)} %get-tuple-element.65, f32[2,48]{1,0:T(2,128)S(1)} %bitcast.382, f32[2,48,48]{2,1,0:T(8,128)S(1)} %get-tuple-element.66, f32[2,48]{1,0:T(2,128)S(1)} %bitcast.379, f32[2,48,48]{2,1,0:T(8,128)S(1)} %get-tuple-element.67, ...), kind=kLoop, calls=%fused_computation.14 | loop fusion | flops 3096576 | bytes 1014912 | tf_op jit(solution)/shard_map/vmap()/mul | solution.py:77
  40.2 2.3 %multiply_reduce_fusion.5 = (f32[2,2,48,48]{3,2,1,0:T(8,128)S(1)}, f32[2,2,48,48]{3,2,1,0:T(8,128)S(1)}, f32[2,2,48,48]{3,2,1,0:T(8,128)S(1)}) fusion(f32[2,48,48,48]{3,2,1,0:T(8,128)S(1)} %add_multiply_fusion.1, f32[2,2,48]{2,1,0:T(2,128)S(1)} %copy.336), kind=kLoop, calls=%fused_computation.5 | loop fusion | flops 2626560 | bytes 996096 | tf_op jit(solution)/shard_map/vmap()/reduce_sum | solution.py:51
  45.4 2.5 %all-to-all-start.1 = ((f32[32,1,14]{2,1,0:T(1,128)}), f32[32,1,14]{2,1,0:T(1,128)S(1)}, u32[]{:S(2)}, u32[]{:S(2)}) async-start(f32[32,1,14]{2,1,0:T(1,128)} %broadcast_in_dim.12), calls=%async_computation.1 | async-start | bytes 32768 | tf_op jit(solution)/shard_map/all_to_all | solution.py:130
  48.1 1.7 %collective-permute-start.7 = (f32[2,2304]{1,0:T(2,128)S(1)}, f32[2,2304]{1,0:T(2,128)S(1)}, u32[]{:S(2)}, u32[]{:S(2)}) collective-permute-start(f32[2,2304]{1,0:T(2,128)S(1)} %get-tuple-element.21), channel_id=1, source_target_pairs={{24,0},{0,8},{8,16},{16,24},{25,1},{1,9},{9,17},{17,25},{26,2},{2,... | collective-permute-start | bytes 55304 | tf_op jit(solution)/shard_map/ppermute | solution.py:13
  49.8 3.1 %collective-permute-start.4 = (f32[2,2304]{1,0:T(2,128)S(1)}, f32[2,2304]{1,0:T(2,128)S(1)}, u32[]{:S(2)}, u32[]{:S(2)}) collective-permute-start(f32[2,2304]{1,0:T(2,128)S(1)} %get-tuple-element.18), channel_id=1, source_target_pairs={{1,0},{2,1},{3,2},{4,3},{5,4},{6,5},{7,6},{0,7},{9,8},{10,9},{11,1... | collective-permute-start | bytes 55304 | tf_op jit(solution)/shard_map/ppermute | solution.py:13
  52.9 1.3 %collective-permute-start.5 = (f32[2,2304]{1,0:T(2,128)S(1)}, f32[2,2304]{1,0:T(2,128)S(1)}, u32[]{:S(2)}, u32[]{:S(2)}) collective-permute-start(f32[2,2304]{1,0:T(2,128)S(1)} %get-tuple-element.19), channel_id=1, source_target_pairs={{8,0},{16,8},{24,16},{0,24},{9,1},{17,9},{25,17},{1,25},{10,2},{18... | collective-permute-start | bytes 55304 | tf_op jit(solution)/shard_map/ppermute | solution.py:13
  54.2 0.8 all-to-all-done.1
  59.7 2.3 %add_multiply_fusion = f32[2,48,48,48]{3,2,1,0:T(8,128)S(1)} fusion(f32[2,48,48]{2,1,0:T(8,128)S(1)} %get-tuple-element.59, f32[2,48,48]{2,1,0:T(8,128)S(1)} %get-tuple-element.60, f32[2,48,48]{2,1,0:T(8,128)S(1)} %get-tuple-element.61, f32[2,48,48]{2,1,0:T(8,128)S(1)} %get-tuple-element.62, f32[2,48,48]{2,1,0:T(8,128)S(1)} %get-tuple-element.63, ...), kind=kLoop, calls=%fused_computation.13 | loop fusion | flops 3096576 | bytes 1014912 | tf_op jit(solution)/shard_map/vmap()/mul | solution.py:77
  62.0 2.3 %multiply_reduce_fusion.2 = (f32[2,2,48,48]{3,2,1,0:T(8,128)S(1)}, f32[2,2,48,48]{3,2,1,0:T(8,128)S(1)}, f32[2,2,48,48]{3,2,1,0:T(8,128)S(1)}) fusion(f32[2,48,48,48]{3,2,1,0:T(8,128)S(1)} %add_multiply_fusion, f32[2,2,48]{2,1,0:T(2,128)S(1)} %copy.336), kind=kLoop, calls=%fused_computation.2 | loop fusion | flops 2626560 | bytes 996096 | tf_op jit(solution)/shard_map/vmap()/reduce_sum | solution.py:51
  67.1 2.5 %all-to-all-start.2 = ((f32[32,1,4]{2,1,0:T(1,128)}), f32[32,1,4]{2,1,0:T(1,128)S(1)}, u32[]{:S(2)}, u32[]{:S(2)}) async-start(f32[32,1,4]{2,1,0:T(1,128)} %broadcast_in_dim.13), calls=%async_computation.2 | async-start | bytes 32768 | tf_op jit(solution)/shard_map/all_to_all | solution.py:130
  69.6 3.4 %collective-permute-start.8 = (f32[2,2304]{1,0:T(2,128)S(1)}, f32[2,2304]{1,0:T(2,128)S(1)}, u32[]{:S(2)}, u32[]{:S(2)}) collective-permute-start(f32[2,2304]{1,0:T(2,128)S(1)} %get-tuple-element.22), channel_id=1, source_target_pairs={{1,0},{2,1},{3,2},{4,3},{5,4},{6,5},{7,6},{0,7},{9,8},{10,9},{11,1... | collective-permute-start | bytes 55304 | tf_op jit(solution)/shard_map/ppermute | solution.py:13
  73.1 2.4 %collective-permute-start.9 = (f32[2,2304]{1,0:T(2,128)S(1)}, f32[2,2304]{1,0:T(2,128)S(1)}, u32[]{:S(2)}, u32[]{:S(2)}) collective-permute-start(f32[2,2304]{1,0:T(2,128)S(1)} %get-tuple-element.23), channel_id=1, source_target_pairs={{8,0},{16,8},{24,16},{0,24},{9,1},{17,9},{25,17},{1,25},{10,2},{18... | collective-permute-start | bytes 55304 | tf_op jit(solution)/shard_map/ppermute | solution.py:13
  75.5 1.2 %all-to-all-done.2 = f32[32,1,4]{2,1,0:T(1,128)S(1)} async-done(((f32[32,1,4]{2,1,0:T(1,128)}), f32[32,1,4]{2,1,0:T(1,128)S(1)}, u32[]{:S(2)}, u32[]{:S(2)}) %all-to-all-start.2) | async-done | bytes 544 | tf_op jit(solution)/shard_map/all_to_all | solution.py:130
  (196 shorter events, 18.9 us)
Async XLA Ops:
  1.5 4.3 %copy-start = (f32[1,1,2,48,48]{4,3,2,1,0:T(8,128)S(1)}, f32[1,1,2,48,48]{4,3,2,1,0:T(8,128)}, u32[]{:S(2)}) copy-start(f32[1,1,2,48,48]{4,3,2,1,0:T(8,128)} %param.7) | copy-start | bytes 55300
  5.8 2.3 %copy-start.2 = (f32[1,1,2,48]{3,2,1,0:T(2,128)S(1)}, f32[1,1,2,48]{3,2,1,0:T(2,128)}, u32[]{:S(2)}) copy-start(f32[1,1,2,48]{3,2,1,0:T(2,128)} %param.8) | copy-start | bytes 1156
  10.7 12.2 %copy-start.1 = (s32[4,8]{1,0:T(4,128)S(1)}, s32[4,8]{1,0:T(4,128)}, u32[]{:S(2)}) copy-start(s32[4,8]{1,0:T(4,128)} %param.10) | copy-start | bytes 388
  10.7 12.3 %copy-start.4 = (f32[1,1,2,3]{3,2,1,0:T(2,128)S(1)}, f32[1,1,2,3]{3,2,1,0:T(2,128)}, u32[]{:S(2)}) copy-start(f32[1,1,2,3]{3,2,1,0:T(2,128)} %param.9) | copy-start | bytes 76
  10.7 12.4 %copy-start.3 = (f32[1,1,6,48]{3,1,2,0:T(1,128)S(1)}, f32[1,1,6,48]{3,1,2,0:T(1,128)}, u32[]{:S(2)}) copy-start(f32[1,1,6,48]{3,1,2,0:T(1,128)} %param.11) | copy-start | bytes 3460
  14.3 14.4 %all-to-all-start = ((f32[32,1,12]{2,1,0:T(1,128)}), f32[32,1,12]{2,1,0:T(1,128)S(1)}, u32[]{:S(2)}, u32[]{:S(2)}) async-start(f32[32,1,12]{2,1,0:T(1,128)} %broadcast_in_dim.11), calls=%async_computation | async-start | bytes 32768 | tf_op jit(solution)/shard_map/all_to_all | solution.py:130
  28.8 3.0 %collective-permute-start.2 = (f32[2,2304]{1,0:T(2,128)S(1)}, f32[2,2304]{1,0:T(2,128)S(1)}, u32[]{:S(2)}, u32[]{:S(2)}) collective-permute-start(f32[2,2304]{1,0:T(2,128)S(1)} %get-tuple-element.16), channel_id=1, source_target_pairs={{1,0},{2,1},{3,2},{4,3},{5,4},{6,5},{7,6},{0,7},{9,8},{10,9},{11,1... | collective-permute-start | bytes 55304 | tf_op jit(solution)/shard_map/ppermute | solution.py:13
  28.8 3.8 %collective-permute-start.3 = (f32[2,2304]{1,0:T(2,128)S(1)}, f32[2,2304]{1,0:T(2,128)S(1)}, u32[]{:S(2)}, u32[]{:S(2)}) collective-permute-start(f32[2,2304]{1,0:T(2,128)S(1)} %get-tuple-element.17), channel_id=1, source_target_pairs={{8,0},{16,8},{24,16},{0,24},{9,1},{17,9},{25,17},{1,25},{10,2},{18... | collective-permute-start | bytes 55304 | tf_op jit(solution)/shard_map/ppermute | solution.py:13
  30.6 5.0 %collective-permute-start = (f32[2,2353]{1,0:T(2,128)S(1)}, f32[2,2353]{1,0:T(2,128)S(1)}, u32[]{:S(2)}, u32[]{:S(2)}) collective-permute-start(f32[2,2353]{1,0:T(2,128)S(1)} %concatenate.235), channel_id=1, source_target_pairs={{7,0},{0,1},{1,2},{2,3},{3,4},{4,5},{5,6},{6,7},{15,8},{8,9},{9,10... | collective-permute-start | bytes 56480 | tf_op jit(solution)/shard_map/ppermute | solution.py:13
  30.6 5.1 %collective-permute-start.1 = (f32[2,2353]{1,0:T(2,128)S(1)}, f32[2,2353]{1,0:T(2,128)S(1)}, u32[]{:S(2)}, u32[]{:S(2)}) collective-permute-start(f32[2,2353]{1,0:T(2,128)S(1)} %concatenate.236), channel_id=1, source_target_pairs={{24,0},{0,8},{8,16},{16,24},{25,1},{1,9},{9,17},{17,25},{26,2},{2,... | collective-permute-start | bytes 56480 | tf_op jit(solution)/shard_map/ppermute | solution.py:13
  45.4 9.7 %all-to-all-start.1 = ((f32[32,1,14]{2,1,0:T(1,128)}), f32[32,1,14]{2,1,0:T(1,128)S(1)}, u32[]{:S(2)}, u32[]{:S(2)}) async-start(f32[32,1,14]{2,1,0:T(1,128)} %broadcast_in_dim.12), calls=%async_computation.1 | async-start | bytes 32768 | tf_op jit(solution)/shard_map/all_to_all | solution.py:130
  47.9 10.6 %collective-permute-start.6 = (f32[2,2304]{1,0:T(2,128)S(1)}, f32[2,2304]{1,0:T(2,128)S(1)}, u32[]{:S(2)}, u32[]{:S(2)}) collective-permute-start(f32[2,2304]{1,0:T(2,128)S(1)} %get-tuple-element.20), channel_id=1, source_target_pairs={{7,0},{0,1},{1,2},{2,3},{3,4},{4,5},{5,6},{6,7},{15,8},{8,9},{9,10... | collective-permute-start | bytes 55304 | tf_op jit(solution)/shard_map/ppermute | solution.py:13
  48.1 10.4 %collective-permute-start.7 = (f32[2,2304]{1,0:T(2,128)S(1)}, f32[2,2304]{1,0:T(2,128)S(1)}, u32[]{:S(2)}, u32[]{:S(2)}) collective-permute-start(f32[2,2304]{1,0:T(2,128)S(1)} %get-tuple-element.21), channel_id=1, source_target_pairs={{24,0},{0,8},{8,16},{16,24},{25,1},{1,9},{9,17},{17,25},{26,2},{2,... | collective-permute-start | bytes 55304 | tf_op jit(solution)/shard_map/ppermute | solution.py:13
  49.8 8.5 %collective-permute-start.4 = (f32[2,2304]{1,0:T(2,128)S(1)}, f32[2,2304]{1,0:T(2,128)S(1)}, u32[]{:S(2)}, u32[]{:S(2)}) collective-permute-start(f32[2,2304]{1,0:T(2,128)S(1)} %get-tuple-element.18), channel_id=1, source_target_pairs={{1,0},{2,1},{3,2},{4,3},{5,4},{6,5},{7,6},{0,7},{9,8},{10,9},{11,1... | collective-permute-start | bytes 55304 | tf_op jit(solution)/shard_map/ppermute | solution.py:13
  52.9 5.4 %collective-permute-start.5 = (f32[2,2304]{1,0:T(2,128)S(1)}, f32[2,2304]{1,0:T(2,128)S(1)}, u32[]{:S(2)}, u32[]{:S(2)}) collective-permute-start(f32[2,2304]{1,0:T(2,128)S(1)} %get-tuple-element.19), channel_id=1, source_target_pairs={{8,0},{16,8},{24,16},{0,24},{9,1},{17,9},{25,17},{1,25},{10,2},{18... | collective-permute-start | bytes 55304 | tf_op jit(solution)/shard_map/ppermute | solution.py:13
  67.1 9.6 %all-to-all-start.2 = ((f32[32,1,4]{2,1,0:T(1,128)}), f32[32,1,4]{2,1,0:T(1,128)S(1)}, u32[]{:S(2)}, u32[]{:S(2)}) async-start(f32[32,1,4]{2,1,0:T(1,128)} %broadcast_in_dim.13), calls=%async_computation.2 | async-start | bytes 32768 | tf_op jit(solution)/shard_map/all_to_all | solution.py:130
  69.6 12.9 %collective-permute-start.8 = (f32[2,2304]{1,0:T(2,128)S(1)}, f32[2,2304]{1,0:T(2,128)S(1)}, u32[]{:S(2)}, u32[]{:S(2)}) collective-permute-start(f32[2,2304]{1,0:T(2,128)S(1)} %get-tuple-element.22), channel_id=1, source_target_pairs={{1,0},{2,1},{3,2},{4,3},{5,4},{6,5},{7,6},{0,7},{9,8},{10,9},{11,1... | collective-permute-start | bytes 55304 | tf_op jit(solution)/shard_map/ppermute | solution.py:13
  73.1 9.5 %collective-permute-start.9 = (f32[2,2304]{1,0:T(2,128)S(1)}, f32[2,2304]{1,0:T(2,128)S(1)}, u32[]{:S(2)}, u32[]{:S(2)}) collective-permute-start(f32[2,2304]{1,0:T(2,128)S(1)} %get-tuple-element.23), channel_id=1, source_target_pairs={{8,0},{16,8},{24,16},{0,24},{9,1},{17,9},{25,17},{1,25},{10,2},{18... | collective-permute-start | bytes 55304 | tf_op jit(solution)/shard_map/ppermute | solution.py:13

commit v13 on v11

--- a/solution.py
+++ b/solution.py
@@ -165,7 +165,12 @@
                 jnp.concatenate([high_side[:, 0], extra[0]], axis=1),
                 jnp.concatenate([high_side[:, 1], extra[1]], axis=1),
             ]
-        sends, after = lax.optimization_barrier((sends, after))
+        if both and after is not None:
+            lows = lax.optimization_barrier(sends[:2])
+            highs, after = lax.optimization_barrier((sends[2:], after))
+            sends = list(lows) + list(highs)
+        else:
+            sends, after = lax.optimization_barrier((sends, after))
         low_next_owner = shifted(sends[0], "dev", -1)
         low_next_group = shifted(sends[1], "grp", -1)
         following = jnp.stack(

time: 83.4 us -> 84.1 us (level)
  starting transfers between devices: 26.8 us -> 30.6 us
  waiting for transfers between devices: 9.15 us -> 6.02 us
    all_to_all x3, waiting for transfers between devices: 5.97 us -> 1.99 us  [gather_all(): got = lax.all_to_all(spread, ('grp', 'dev'), 0, 0, tiled=True)]
    ppermute x10, starting transfers between devices: 14.4 us -> 18.2 us  [shifted(): return lax.ppermute(block, axis, route)]
    ppermute x10, waiting for transfers between devices: 3.18 us -> 4.03 us  [shifted(): return lax.ppermute(block, axis, route)]
  transfers between devices with their start and end apart: 13 -> 13, of which waited for: 5 -> 3; matrix products, arithmetic and copies ran while one was open for 10% -> 10% of each run, Pallas kernels for 0% -> 0%
where the time goes in v13:
time: 84.1 us; the launch traced here: 83.8 us
  starting transfers between devices  30.6 us (36%)
  other arithmetic  16.4 us (20%)
  local copies, waits for them, and re-layouts  12.3 us (15%)
  matrix products  11.2 us (13%)
  between operations  7.26 us (9%)
  waiting for transfers between devices  6.02 us (7%)
    ppermute x10, starting transfers between devices, shifted(): return lax.ppermute(block, axis, route)  18.2 us
    all_to_all x3, starting transfers between devices, gather_all(): got = lax.all_to_all(spread, ('grp', 'dev'), 0, 0, tiled=True)  12.4 us
    reduce_sum x3, other arithmetic, trace_solved(): along_a = jnp.sum(end_rows[:, :, None, None] * solved[None], axis=1)  6.94 us
    mul x2, other arithmetic, apply_one(): one_inverse * face_spectrum(one_transform, low_side, high_side)  4.61 us
    ppermute x10, waiting for transfers between devices, shifted(): return lax.ppermute(block, axis, route)  4.03 us
    dot_general x6, matrix products, trace_solved(): jnp.einsum('bj,edjk,ck->edbc', transform, planes, transform, precision=FAST)  2.74 us
    reshape x1, local copies, waits for them, and re-layouts, spectral(): spatial = patch_load.astype(jnp.float32).reshape(points, points, points)  2.66 us
    dot_general x1, matrix products, spectral(): return jnp.einsum('ck,ijc->ijk', transform, moved, precision=FAST)  2.59 us
  transfers between devices with their start and end apart: 13, of which 3 were waited for; matrix products, arithmetic and copies ran while one was open for 10% of the time, Pallas kernels for 0%

profile of v13, /device:TPU:0, one launch (start us, length us, event | category | flops | bytes accessed | tf_op | source)
XLA Modules:
  0.0 83.8 jit_solution(5952955058379575335)
XLA Ops:
  0.6 0.8 broadcast_add_fusion
  1.5 2.7 %reshape.1117 = bf16[2,48,48,48]{3,2,1,0:T(8,128)(2,1)S(1)} reshape(bf16[1,1,2,48,2304]{4,3,2,1,0:T(8,128)(2,1)} %param.6) | data formatting | bytes 884736 | tf_op jit(solution)/shard_map/vmap()/reshape | solution.py:22
  4.1 1.6 %fusion.7 = f32[2,48,48,48]{3,1,2,0:T(8,128)S(1)} fusion(bf16[2,48,48,48]{3,2,1,0:T(8,128)(2,1)S(1)} %reshape.1117, f32[1,1,2,48,48]{4,3,2,1,0:T(8,128)} %param.7), kind=kOutput, calls=%fused_computation.17 | convolution fusion | flops 63700992 | bytes 1345536 | tf_op jit(solution)/shard_map/vmap(ai,abc->ibc)/dot_general | solution.py:23
  5.8 2.2 %fusion.2 = f32[2,48,48,48]{3,2,1,0:T(8,128)S(1)} fusion(f32[2,48,48,48]{3,1,2,0:T(8,128)S(1)} %fusion.7, f32[1,1,2,48,48]{4,3,2,1,0:T(8,128)S(1)} %copy-done), kind=kOutput, calls=%fused_computation.11 | convolution fusion | flops 63700992 | bytes 1787904 | tf_op jit(solution)/shard_map/vmap(bj,ibc->ijc)/dot_general | solution.py:24
  8.1 2.6 %fusion.4 = f32[2,48,48,48]{3,2,1,0:T(8,128)S(1)} fusion(f32[2,48,48,48]{3,2,1,0:T(8,128)S(1)} %fusion.2, f32[2,48]{1,0:T(2,128)S(1)} %bitcast.424, f32[2,48,48]{2,1,0:T(8,128)S(1)} %broadcast_add_fusion, f32[1,1,2,48,48]{4,3,2,1,0:T(8,128)S(1)} %copy-done), kind=kOutput, calls=%fused_computation.16 | convolution fusion | flops 64364544 | bytes 1806720 | tf_op jit(solution)/shard_map/vmap(ck,ijc->ijk)/dot_general | solution.py:25
  10.7 2.3 %multiply_reduce_fusion.8 = (f32[2,2,48,48]{3,2,1,0:T(8,128)S(1)}, f32[2,2,48,48]{3,2,1,0:T(8,128)S(1)}, f32[2,2,48,48]{3,2,1,0:T(8,128)S(1)}) fusion(f32[2,48,48,48]{3,2,1,0:T(8,128)S(1)} %fusion.4, f32[2,2,48]{2,1,0:T(2,128)S(1)} %copy.328), kind=kLoop, calls=%fused_computation.8 | loop fusion | flops 2626560 | bytes 996096 | tf_op jit(solution)/shard_map/vmap()/reduce_sum | solution.py:51
  14.3 7.3 %all-to-all-start = ((f32[32,1,12]{2,1,0:T(1,128)}), f32[32,1,12]{2,1,0:T(1,128)S(1)}, u32[]{:S(2)}, u32[]{:S(2)}) async-start(f32[32,1,12]{2,1,0:T(1,128)} %broadcast_in_dim.11), calls=%async_computation | async-start | bytes 32768 | tf_op jit(solution)/shard_map/all_to_all | solution.py:130
  22.8 3.4 %collective-permute-start.2 = (f32[2,2304]{1,0:T(2,128)S(1)}, f32[2,2304]{1,0:T(2,128)S(1)}, u32[]{:S(2)}, u32[]{:S(2)}) collective-permute-start(f32[2,2304]{1,0:T(2,128)S(1)} %get-tuple-element.16), channel_id=1, source_target_pairs={{1,0},{2,1},{3,2},{4,3},{5,4},{6,5},{7,6},{0,7},{9,8},{10,9},{11,1... | collective-permute-start | bytes 55304 | tf_op jit(solution)/shard_map/ppermute | solution.py:13
  26.3 2.4 %collective-permute-start.3 = (f32[2,2304]{1,0:T(2,128)S(1)}, f32[2,2304]{1,0:T(2,128)S(1)}, u32[]{:S(2)}, u32[]{:S(2)}) collective-permute-start(f32[2,2304]{1,0:T(2,128)S(1)} %get-tuple-element.17), channel_id=1, source_target_pairs={{8,0},{16,8},{24,16},{0,24},{9,1},{17,9},{25,17},{1,25},{10,2},{18... | collective-permute-start | bytes 55304 | tf_op jit(solution)/shard_map/ppermute | solution.py:13
  32.3 4.0 %collective-permute-done = f32[2,2353]{1,0:T(2,128)S(1)} collective-permute-done((f32[2,2353]{1,0:T(2,128)S(1)}, f32[2,2353]{1,0:T(2,128)S(1)}, u32[]{:S(2)}, u32[]{:S(2)}) %collective-permute-start) | collective-permute-done | bytes 18856 | tf_op jit(solution)/shard_map/ppermute | solution.py:13
  38.0 2.3 %add_multiply_fusion.1 = f32[2,48,48,48]{3,2,1,0:T(8,128)S(1)} fusion(f32[2,48,48]{2,1,0:T(8,128)S(1)} %get-tuple-element.63, f32[2,48]{1,0:T(2,128)S(1)} %bitcast.413, f32[2,48,48]{2,1,0:T(8,128)S(1)} %get-tuple-element.64, f32[2,48]{1,0:T(2,128)S(1)} %bitcast.410, f32[2,48,48]{2,1,0:T(8,128)S(1)} %get-tuple-element.65, ...), kind=kLoop, calls=%fused_computation.14 | loop fusion | flops 3096576 | bytes 1014912 | tf_op jit(solution)/shard_map/vmap()/mul | solution.py:77
  40.3 2.3 %multiply_reduce_fusion.5 = (f32[2,2,48,48]{3,2,1,0:T(8,128)S(1)}, f32[2,2,48,48]{3,2,1,0:T(8,128)S(1)}, f32[2,2,48,48]{3,2,1,0:T(8,128)S(1)}) fusion(f32[2,48,48,48]{3,2,1,0:T(8,128)S(1)} %add_multiply_fusion.1, f32[2,2,48]{2,1,0:T(2,128)S(1)} %copy.328), kind=kLoop, calls=%fused_computation.5 | loop fusion | flops 2626560 | bytes 996096 | tf_op jit(solution)/shard_map/vmap()/reduce_sum | solution.py:51
  45.5 2.5 %all-to-all-start.1 = ((f32[32,1,14]{2,1,0:T(1,128)}), f32[32,1,14]{2,1,0:T(1,128)S(1)}, u32[]{:S(2)}, u32[]{:S(2)}) async-start(f32[32,1,14]{2,1,0:T(1,128)} %broadcast_in_dim.12), calls=%async_computation.1 | async-start | bytes 32768 | tf_op jit(solution)/shard_map/all_to_all | solution.py:130
  48.2 1.7 %collective-permute-start.7 = (f32[2,2304]{1,0:T(2,128)S(1)}, f32[2,2304]{1,0:T(2,128)S(1)}, u32[]{:S(2)}, u32[]{:S(2)}) collective-permute-start(f32[2,2304]{1,0:T(2,128)S(1)} %get-tuple-element.21), channel_id=1, source_target_pairs={{24,0},{0,8},{8,16},{16,24},{25,1},{1,9},{9,17},{17,25},{26,2},{2,... | collective-permute-start | bytes 55304 | tf_op jit(solution)/shard_map/ppermute | solution.py:13
  49.9 3.1 %collective-permute-start.4 = (f32[2,2304]{1,0:T(2,128)S(1)}, f32[2,2304]{1,0:T(2,128)S(1)}, u32[]{:S(2)}, u32[]{:S(2)}) collective-permute-start(f32[2,2304]{1,0:T(2,128)S(1)} %get-tuple-element.18), channel_id=1, source_target_pairs={{1,0},{2,1},{3,2},{4,3},{5,4},{6,5},{7,6},{0,7},{9,8},{10,9},{11,1... | collective-permute-start | bytes 55304 | tf_op jit(solution)/shard_map/ppermute | solution.py:13
  53.0 1.3 %collective-permute-start.5 = (f32[2,2304]{1,0:T(2,128)S(1)}, f32[2,2304]{1,0:T(2,128)S(1)}, u32[]{:S(2)}, u32[]{:S(2)}) collective-permute-start(f32[2,2304]{1,0:T(2,128)S(1)} %get-tuple-element.19), channel_id=1, source_target_pairs={{8,0},{16,8},{24,16},{0,24},{9,1},{17,9},{25,17},{1,25},{10,2},{18... | collective-permute-start | bytes 55304 | tf_op jit(solution)/shard_map/ppermute | solution.py:13
  54.3 0.8 all-to-all-done.1
  59.9 2.3 %add_multiply_fusion = f32[2,48,48,48]{3,2,1,0:T(8,128)S(1)} fusion(f32[2,48,48]{2,1,0:T(8,128)S(1)} %get-tuple-element.57, f32[2,48,48]{2,1,0:T(8,128)S(1)} %get-tuple-element.58, f32[2,48,48]{2,1,0:T(8,128)S(1)} %get-tuple-element.59, f32[2,48,48]{2,1,0:T(8,128)S(1)} %get-tuple-element.60, f32[2,48,48]{2,1,0:T(8,128)S(1)} %get-tuple-element.61, ...), kind=kLoop, calls=%fused_computation.13 | loop fusion | flops 3096576 | bytes 1014912 | tf_op jit(solution)/shard_map/vmap()/mul | solution.py:77
  62.2 2.3 %multiply_reduce_fusion.2 = (f32[2,2,48,48]{3,2,1,0:T(8,128)S(1)}, f32[2,2,48,48]{3,2,1,0:T(8,128)S(1)}, f32[2,2,48,48]{3,2,1,0:T(8,128)S(1)}) fusion(f32[2,48,48,48]{3,2,1,0:T(8,128)S(1)} %add_multiply_fusion, f32[2,2,48]{2,1,0:T(2,128)S(1)} %copy.328), kind=kLoop, calls=%fused_computation.2 | loop fusion | flops 2626560 | bytes 996096 | tf_op jit(solution)/shard_map/vmap()/reduce_sum | solution.py:51
  67.3 2.5 %all-to-all-start.2 = ((f32[32,1,4]{2,1,0:T(1,128)}), f32[32,1,4]{2,1,0:T(1,128)S(1)}, u32[]{:S(2)}, u32[]{:S(2)}) async-start(f32[32,1,4]{2,1,0:T(1,128)} %broadcast_in_dim.13), calls=%async_computation.2 | async-start | bytes 32768 | tf_op jit(solution)/shard_map/all_to_all | solution.py:130
  69.9 3.4 %collective-permute-start.8 = (f32[2,2304]{1,0:T(2,128)S(1)}, f32[2,2304]{1,0:T(2,128)S(1)}, u32[]{:S(2)}, u32[]{:S(2)}) collective-permute-start(f32[2,2304]{1,0:T(2,128)S(1)} %get-tuple-element.22), channel_id=1, source_target_pairs={{1,0},{2,1},{3,2},{4,3},{5,4},{6,5},{7,6},{0,7},{9,8},{10,9},{11,1... | collective-permute-start | bytes 55304 | tf_op jit(solution)/shard_map/ppermute | solution.py:13
  73.3 2.4 %collective-permute-start.9 = (f32[2,2304]{1,0:T(2,128)S(1)}, f32[2,2304]{1,0:T(2,128)S(1)}, u32[]{:S(2)}, u32[]{:S(2)}) collective-permute-start(f32[2,2304]{1,0:T(2,128)S(1)} %get-tuple-element.23), channel_id=1, source_target_pairs={{8,0},{16,8},{24,16},{0,24},{9,1},{17,9},{25,17},{1,25},{10,2},{18... | collective-permute-start | bytes 55304 | tf_op jit(solution)/shard_map/ppermute | solution.py:13
  75.8 1.2 %all-to-all-done.2 = f32[32,1,4]{2,1,0:T(1,128)S(1)} async-done(((f32[32,1,4]{2,1,0:T(1,128)}), f32[32,1,4]{2,1,0:T(1,128)S(1)}, u32[]{:S(2)}, u32[]{:S(2)}) %all-to-all-start.2) | async-done | bytes 544 | tf_op jit(solution)/shard_map/all_to_all | solution.py:130
  82.0 0.8 multiply_add_fusion
  (191 shorter events, 18.1 us)
Async XLA Ops:
  1.5 4.3 %copy-start = (f32[1,1,2,48,48]{4,3,2,1,0:T(8,128)S(1)}, f32[1,1,2,48,48]{4,3,2,1,0:T(8,128)}, u32[]{:S(2)}) copy-start(f32[1,1,2,48,48]{4,3,2,1,0:T(8,128)} %param.7) | copy-start | bytes 55300
  5.8 2.3 %copy-start.2 = (f32[1,1,2,48]{3,2,1,0:T(2,128)S(1)}, f32[1,1,2,48]{3,2,1,0:T(2,128)}, u32[]{:S(2)}) copy-start(f32[1,1,2,48]{3,2,1,0:T(2,128)} %param.8) | copy-start | bytes 1156
  10.7 18.0 %copy-start.1 = (s32[4,8]{1,0:T(4,128)S(1)}, s32[4,8]{1,0:T(4,128)}, u32[]{:S(2)}) copy-start(s32[4,8]{1,0:T(4,128)} %param.10) | copy-start | bytes 388
  10.7 18.1 %copy-start.4 = (f32[1,1,6,48]{3,1,2,0:T(1,128)S(1)}, f32[1,1,6,48]{3,1,2,0:T(1,128)}, u32[]{:S(2)}) copy-start(f32[1,1,6,48]{3,1,2,0:T(1,128)} %param.11) | copy-start | bytes 3460
  10.7 18.2 %copy-start.3 = (f32[1,1,2,3]{3,2,1,0:T(2,128)S(1)}, f32[1,1,2,3]{3,2,1,0:T(2,128)}, u32[]{:S(2)}) copy-start(f32[1,1,2,3]{3,2,1,0:T(2,128)} %param.9) | copy-start | bytes 76
  14.3 16.2 %all-to-all-start = ((f32[32,1,12]{2,1,0:T(1,128)}), f32[32,1,12]{2,1,0:T(1,128)S(1)}, u32[]{:S(2)}, u32[]{:S(2)}) async-start(f32[32,1,12]{2,1,0:T(1,128)} %broadcast_in_dim.11), calls=%async_computation | async-start | bytes 32768 | tf_op jit(solution)/shard_map/all_to_all | solution.py:130
  22.8 9.1 %collective-permute-start.2 = (f32[2,2304]{1,0:T(2,128)S(1)}, f32[2,2304]{1,0:T(2,128)S(1)}, u32[]{:S(2)}, u32[]{:S(2)}) collective-permute-start(f32[2,2304]{1,0:T(2,128)S(1)} %get-tuple-element.16), channel_id=1, source_target_pairs={{1,0},{2,1},{3,2},{4,3},{5,4},{6,5},{7,6},{0,7},{9,8},{10,9},{11,1... | collective-permute-start | bytes 55304 | tf_op jit(solution)/shard_map/ppermute | solution.py:13
  26.3 5.7 %collective-permute-start.3 = (f32[2,2304]{1,0:T(2,128)S(1)}, f32[2,2304]{1,0:T(2,128)S(1)}, u32[]{:S(2)}, u32[]{:S(2)}) collective-permute-start(f32[2,2304]{1,0:T(2,128)S(1)} %get-tuple-element.17), channel_id=1, source_target_pairs={{8,0},{16,8},{24,16},{0,24},{9,1},{17,9},{25,17},{1,25},{10,2},{18... | collective-permute-start | bytes 55304 | tf_op jit(solution)/shard_map/ppermute | solution.py:13
  31.3 5.0 %collective-permute-start = (f32[2,2353]{1,0:T(2,128)S(1)}, f32[2,2353]{1,0:T(2,128)S(1)}, u32[]{:S(2)}, u32[]{:S(2)}) collective-permute-start(f32[2,2353]{1,0:T(2,128)S(1)} %concatenate.231), channel_id=1, source_target_pairs={{7,0},{0,1},{1,2},{2,3},{3,4},{4,5},{5,6},{6,7},{15,8},{8,9},{9,10... | collective-permute-start | bytes 56480 | tf_op jit(solution)/shard_map/ppermute | solution.py:13
  31.4 5.1 %collective-permute-start.1 = (f32[2,2353]{1,0:T(2,128)S(1)}, f32[2,2353]{1,0:T(2,128)S(1)}, u32[]{:S(2)}, u32[]{:S(2)}) collective-permute-start(f32[2,2353]{1,0:T(2,128)S(1)} %concatenate.232), channel_id=1, source_target_pairs={{24,0},{0,8},{8,16},{16,24},{25,1},{1,9},{9,17},{17,25},{26,2},{2,... | collective-permute-start | bytes 56480 | tf_op jit(solution)/shard_map/ppermute | solution.py:13
  45.5 9.7 %all-to-all-start.1 = ((f32[32,1,14]{2,1,0:T(1,128)}), f32[32,1,14]{2,1,0:T(1,128)S(1)}, u32[]{:S(2)}, u32[]{:S(2)}) async-start(f32[32,1,14]{2,1,0:T(1,128)} %broadcast_in_dim.12), calls=%async_computation.1 | async-start | bytes 32768 | tf_op jit(solution)/shard_map/all_to_all | solution.py:130
  48.1 10.7 %collective-permute-start.6 = (f32[2,2304]{1,0:T(2,128)S(1)}, f32[2,2304]{1,0:T(2,128)S(1)}, u32[]{:S(2)}, u32[]{:S(2)}) collective-permute-start(f32[2,2304]{1,0:T(2,128)S(1)} %get-tuple-element.20), channel_id=1, source_target_pairs={{7,0},{0,1},{1,2},{2,3},{3,4},{4,5},{5,6},{6,7},{15,8},{8,9},{9,10... | collective-permute-start | bytes 55304 | tf_op jit(solution)/shard_map/ppermute | solution.py:13
  48.2 10.5 %collective-permute-start.7 = (f32[2,2304]{1,0:T(2,128)S(1)}, f32[2,2304]{1,0:T(2,128)S(1)}, u32[]{:S(2)}, u32[]{:S(2)}) collective-permute-start(f32[2,2304]{1,0:T(2,128)S(1)} %get-tuple-element.21), channel_id=1, source_target_pairs={{24,0},{0,8},{8,16},{16,24},{25,1},{1,9},{9,17},{17,25},{26,2},{2,... | collective-permute-start | bytes 55304 | tf_op jit(solution)/shard_map/ppermute | solution.py:13
  49.9 8.6 %collective-permute-start.4 = (f32[2,2304]{1,0:T(2,128)S(1)}, f32[2,2304]{1,0:T(2,128)S(1)}, u32[]{:S(2)}, u32[]{:S(2)}) collective-permute-start(f32[2,2304]{1,0:T(2,128)S(1)} %get-tuple-element.18), channel_id=1, source_target_pairs={{1,0},{2,1},{3,2},{4,3},{5,4},{6,5},{7,6},{0,7},{9,8},{10,9},{11,1... | collective-permute-start | bytes 55304 | tf_op jit(solution)/shard_map/ppermute | solution.py:13
  53.0 5.5 %collective-permute-start.5 = (f32[2,2304]{1,0:T(2,128)S(1)}, f32[2,2304]{1,0:T(2,128)S(1)}, u32[]{:S(2)}, u32[]{:S(2)}) collective-permute-start(f32[2,2304]{1,0:T(2,128)S(1)} %get-tuple-element.19), channel_id=1, source_target_pairs={{8,0},{16,8},{24,16},{0,24},{9,1},{17,9},{25,17},{1,25},{10,2},{18... | collective-permute-start | bytes 55304 | tf_op jit(solution)/shard_map/ppermute | solution.py:13
  67.3 9.6 %all-to-all-start.2 = ((f32[32,1,4]{2,1,0:T(1,128)}), f32[32,1,4]{2,1,0:T(1,128)S(1)}, u32[]{:S(2)}, u32[]{:S(2)}) async-start(f32[32,1,4]{2,1,0:T(1,128)} %broadcast_in_dim.13), calls=%async_computation.2 | async-start | bytes 32768 | tf_op jit(solution)/shard_map/all_to_all | solution.py:130
  69.9 12.9 %collective-permute-start.8 = (f32[2,2304]{1,0:T(2,128)S(1)}, f32[2,2304]{1,0:T(2,128)S(1)}, u32[]{:S(2)}, u32[]{:S(2)}) collective-permute-start(f32[2,2304]{1,0:T(2,128)S(1)} %get-tuple-element.22), channel_id=1, source_target_pairs={{1,0},{2,1},{3,2},{4,3},{5,4},{6,5},{7,6},{0,7},{9,8},{10,9},{11,1... | collective-permute-start | bytes 55304 | tf_op jit(solution)/shard_map/ppermute | solution.py:13
  73.3 9.5 %collective-permute-start.9 = (f32[2,2304]{1,0:T(2,128)S(1)}, f32[2,2304]{1,0:T(2,128)S(1)}, u32[]{:S(2)}, u32[]{:S(2)}) collective-permute-start(f32[2,2304]{1,0:T(2,128)S(1)} %get-tuple-element.23), channel_id=1, source_target_pairs={{8,0},{16,8},{24,16},{0,24},{9,1},{17,9},{25,17},{1,25},{10,2},{18... | collective-permute-start | bytes 55304 | tf_op jit(solution)/shard_map/ppermute | solution.py:13

commit v14 on v11

--- a/solution.py
+++ b/solution.py
@@ -150,9 +150,9 @@
     def coarse(means):
         here = means[group_index]
         before = means[prev_group]
-        own = jnp.dot(coarse_rows, here, precision=PRECISE).reshape(slot_count, 3)
-        first = jnp.dot(rows_in[:, 0], here, precision=PRECISE)
-        second = jnp.dot(rows_in[:, 1], before, precision=PRECISE)
+        own = jnp.dot(coarse_rows, here, precision=FAST).reshape(slot_count, 3)
+        first = jnp.dot(rows_in[:, 0], here, precision=FAST)
+        second = jnp.dot(rows_in[:, 1], before, precision=FAST)
         return own, jnp.stack([first, second], axis=1)
 
     def jumps(traces_now, both, extra=None, after=None):

time: 83.4 us -> 83.3 us (level)
  no operation moved by 1% of the time
where the time goes in v14:
time: 83.3 us; the launch traced here: 83 us
  starting transfers between devices  26.8 us (32%)
  other arithmetic  16.4 us (20%)
  local copies, waits for them, and re-layouts  12.3 us (15%)
  matrix products  11.1 us (13%)
  waiting for transfers between devices  9.2 us (11%)
  between operations  7.26 us (9%)
    ppermute x10, starting transfers between devices, shifted(): return lax.ppermute(block, axis, route)  14.4 us
    all_to_all x3, starting transfers between devices, gather_all(): got = lax.all_to_all(spread, ('grp', 'dev'), 0, 0, tiled=True)  12.4 us
    reduce_sum x3, other arithmetic, trace_solved(): along_a = jnp.sum(end_rows[:, :, None, None] * solved[None], axis=1)  6.94 us
    all_to_all x3, waiting for transfers between devices, gather_all(): got = lax.all_to_all(spread, ('grp', 'dev'), 0, 0, tiled=True)  5.97 us
    mul x2, other arithmetic, apply_one(): one_inverse * face_spectrum(one_transform, low_side, high_side)  4.61 us
    ppermute x10, waiting for transfers between devices, shifted(): return lax.ppermute(block, axis, route)  3.23 us
    dot_general x6, matrix products, trace_solved(): jnp.einsum('bj,edjk,ck->edbc', transform, planes, transform, precision=FAST)  2.75 us
    reshape x1, local copies, waits for them, and re-layouts, spectral(): spatial = patch_load.astype(jnp.float32).reshape(points, points, points)  2.66 us
  transfers between devices with their start and end apart: 13, of which 5 were waited for; matrix products, arithmetic and copies ran while one was open for 10% of the time, Pallas kernels for 0%

profile of v14, /device:TPU:0, one launch (start us, length us, event | category | flops | bytes accessed | tf_op | source)
XLA Modules:
  0.0 83.0 jit_solution(14478939299090428068)
XLA Ops:
  0.6 0.8 broadcast_add_fusion
  1.5 2.7 %reshape.1117 = bf16[2,48,48,48]{3,2,1,0:T(8,128)(2,1)S(1)} reshape(bf16[1,1,2,48,2304]{4,3,2,1,0:T(8,128)(2,1)} %param.6) | data formatting | bytes 884736 | tf_op jit(solution)/shard_map/vmap()/reshape | solution.py:22
  4.1 1.6 %fusion.7 = f32[2,48,48,48]{3,1,2,0:T(8,128)S(1)} fusion(bf16[2,48,48,48]{3,2,1,0:T(8,128)(2,1)S(1)} %reshape.1117, f32[1,1,2,48,48]{4,3,2,1,0:T(8,128)} %param.7), kind=kOutput, calls=%fused_computation.17 | convolution fusion | flops 63700992 | bytes 1345536 | tf_op jit(solution)/shard_map/vmap(ai,abc->ibc)/dot_general | solution.py:23
  5.8 2.2 %fusion.2 = f32[2,48,48,48]{3,2,1,0:T(8,128)S(1)} fusion(f32[2,48,48,48]{3,1,2,0:T(8,128)S(1)} %fusion.7, f32[1,1,2,48,48]{4,3,2,1,0:T(8,128)S(1)} %copy-done), kind=kOutput, calls=%fused_computation.11 | convolution fusion | flops 63700992 | bytes 1787904 | tf_op jit(solution)/shard_map/vmap(bj,ibc->ijc)/dot_general | solution.py:24
  8.1 2.6 %fusion.4 = f32[2,48,48,48]{3,2,1,0:T(8,128)S(1)} fusion(f32[2,48,48,48]{3,2,1,0:T(8,128)S(1)} %fusion.2, f32[2,48]{1,0:T(2,128)S(1)} %bitcast.419, f32[2,48,48]{2,1,0:T(8,128)S(1)} %broadcast_add_fusion, f32[1,1,2,48,48]{4,3,2,1,0:T(8,128)S(1)} %copy-done), kind=kOutput, calls=%fused_computation.16 | convolution fusion | flops 64364544 | bytes 1806720 | tf_op jit(solution)/shard_map/vmap(ck,ijc->ijk)/dot_general | solution.py:25
  10.7 2.3 %multiply_reduce_fusion.8 = (f32[2,2,48,48]{3,2,1,0:T(8,128)S(1)}, f32[2,2,48,48]{3,2,1,0:T(8,128)S(1)}, f32[2,2,48,48]{3,2,1,0:T(8,128)S(1)}) fusion(f32[2,48,48,48]{3,2,1,0:T(8,128)S(1)} %fusion.4, f32[2,2,48]{2,1,0:T(2,128)S(1)} %copy.336), kind=kLoop, calls=%fused_computation.8 | loop fusion | flops 2626560 | bytes 996096 | tf_op jit(solution)/shard_map/vmap()/reduce_sum | solution.py:51
  14.3 7.3 %all-to-all-start = ((f32[32,1,12]{2,1,0:T(1,128)}), f32[32,1,12]{2,1,0:T(1,128)S(1)}, u32[]{:S(2)}, u32[]{:S(2)}) async-start(f32[32,1,12]{2,1,0:T(1,128)} %broadcast_in_dim.11), calls=%async_computation | async-start | bytes 32768 | tf_op jit(solution)/shard_map/all_to_all | solution.py:130
  24.7 4.0 %all-to-all-done = f32[32,1,12]{2,1,0:T(1,128)S(1)} async-done(((f32[32,1,12]{2,1,0:T(1,128)}), f32[32,1,12]{2,1,0:T(1,128)S(1)}, u32[]{:S(2)}, u32[]{:S(2)}) %all-to-all-start) | async-done | bytes 1568 | tf_op jit(solution)/shard_map/all_to_all | solution.py:130
  28.8 1.8 %collective-permute-start.3 = (f32[2,2304]{1,0:T(2,128)S(1)}, f32[2,2304]{1,0:T(2,128)S(1)}, u32[]{:S(2)}, u32[]{:S(2)}) collective-permute-start(f32[2,2304]{1,0:T(2,128)S(1)} %get-tuple-element.17), channel_id=1, source_target_pairs={{8,0},{16,8},{24,16},{0,24},{9,1},{17,9},{25,17},{1,25},{10,2},{18... | collective-permute-start | bytes 55304 | tf_op jit(solution)/shard_map/ppermute | solution.py:13
  33.0 2.6 %collective-permute-done = f32[2,2353]{1,0:T(2,128)S(1)} collective-permute-done((f32[2,2353]{1,0:T(2,128)S(1)}, f32[2,2353]{1,0:T(2,128)S(1)}, u32[]{:S(2)}, u32[]{:S(2)}) %collective-permute-start) | collective-permute-done | bytes 18856 | tf_op jit(solution)/shard_map/ppermute | solution.py:13
  37.3 2.3 %add_multiply_fusion.1 = f32[2,48,48,48]{3,2,1,0:T(8,128)S(1)} fusion(f32[2,48,48]{2,1,0:T(8,128)S(1)} %get-tuple-element.65, f32[2,48]{1,0:T(2,128)S(1)} %bitcast.408, f32[2,48,48]{2,1,0:T(8,128)S(1)} %get-tuple-element.66, f32[2,48]{1,0:T(2,128)S(1)} %bitcast.405, f32[2,48,48]{2,1,0:T(8,128)S(1)} %get-tuple-element.67, ...), kind=kLoop, calls=%fused_computation.14 | loop fusion | flops 3096576 | bytes 1014912 | tf_op jit(solution)/shard_map/vmap()/mul | solution.py:77
  39.6 2.3 %multiply_reduce_fusion.5 = (f32[2,2,48,48]{3,2,1,0:T(8,128)S(1)}, f32[2,2,48,48]{3,2,1,0:T(8,128)S(1)}, f32[2,2,48,48]{3,2,1,0:T(8,128)S(1)}) fusion(f32[2,48,48,48]{3,2,1,0:T(8,128)S(1)} %add_multiply_fusion.1, f32[2,2,48]{2,1,0:T(2,128)S(1)} %copy.336), kind=kLoop, calls=%fused_computation.5 | loop fusion | flops 2626560 | bytes 996096 | tf_op jit(solution)/shard_map/vmap()/reduce_sum | solution.py:51
  44.8 2.5 %all-to-all-start.1 = ((f32[32,1,14]{2,1,0:T(1,128)}), f32[32,1,14]{2,1,0:T(1,128)S(1)}, u32[]{:S(2)}, u32[]{:S(2)}) async-start(f32[32,1,14]{2,1,0:T(1,128)} %broadcast_in_dim.12), calls=%async_computation.1 | async-start | bytes 32768 | tf_op jit(solution)/shard_map/all_to_all | solution.py:130
  47.5 1.7 %collective-permute-start.7 = (f32[2,2304]{1,0:T(2,128)S(1)}, f32[2,2304]{1,0:T(2,128)S(1)}, u32[]{:S(2)}, u32[]{:S(2)}) collective-permute-start(f32[2,2304]{1,0:T(2,128)S(1)} %get-tuple-element.21), channel_id=1, source_target_pairs={{24,0},{0,8},{8,16},{16,24},{25,1},{1,9},{9,17},{17,25},{26,2},{2,... | collective-permute-start | bytes 55304 | tf_op jit(solution)/shard_map/ppermute | solution.py:13
  49.2 3.1 %collective-permute-start.4 = (f32[2,2304]{1,0:T(2,128)S(1)}, f32[2,2304]{1,0:T(2,128)S(1)}, u32[]{:S(2)}, u32[]{:S(2)}) collective-permute-start(f32[2,2304]{1,0:T(2,128)S(1)} %get-tuple-element.18), channel_id=1, source_target_pairs={{1,0},{2,1},{3,2},{4,3},{5,4},{6,5},{7,6},{0,7},{9,8},{10,9},{11,1... | collective-permute-start | bytes 55304 | tf_op jit(solution)/shard_map/ppermute | solution.py:13
  52.3 1.3 %collective-permute-start.5 = (f32[2,2304]{1,0:T(2,128)S(1)}, f32[2,2304]{1,0:T(2,128)S(1)}, u32[]{:S(2)}, u32[]{:S(2)}) collective-permute-start(f32[2,2304]{1,0:T(2,128)S(1)} %get-tuple-element.19), channel_id=1, source_target_pairs={{8,0},{16,8},{24,16},{0,24},{9,1},{17,9},{25,17},{1,25},{10,2},{18... | collective-permute-start | bytes 55304 | tf_op jit(solution)/shard_map/ppermute | solution.py:13
  53.6 0.8 all-to-all-done.1
  59.1 2.3 %add_multiply_fusion = f32[2,48,48,48]{3,2,1,0:T(8,128)S(1)} fusion(f32[2,48,48]{2,1,0:T(8,128)S(1)} %get-tuple-element.59, f32[2,48,48]{2,1,0:T(8,128)S(1)} %get-tuple-element.60, f32[2,48,48]{2,1,0:T(8,128)S(1)} %get-tuple-element.61, f32[2,48,48]{2,1,0:T(8,128)S(1)} %get-tuple-element.62, f32[2,48,48]{2,1,0:T(8,128)S(1)} %get-tuple-element.63, ...), kind=kLoop, calls=%fused_computation.13 | loop fusion | flops 3096576 | bytes 1014912 | tf_op jit(solution)/shard_map/vmap()/mul | solution.py:77
  61.4 2.3 %multiply_reduce_fusion.2 = (f32[2,2,48,48]{3,2,1,0:T(8,128)S(1)}, f32[2,2,48,48]{3,2,1,0:T(8,128)S(1)}, f32[2,2,48,48]{3,2,1,0:T(8,128)S(1)}) fusion(f32[2,48,48,48]{3,2,1,0:T(8,128)S(1)} %add_multiply_fusion, f32[2,2,48]{2,1,0:T(2,128)S(1)} %copy.336), kind=kLoop, calls=%fused_computation.2 | loop fusion | flops 2626560 | bytes 996096 | tf_op jit(solution)/shard_map/vmap()/reduce_sum | solution.py:51
  66.5 2.5 %all-to-all-start.2 = ((f32[32,1,4]{2,1,0:T(1,128)}), f32[32,1,4]{2,1,0:T(1,128)S(1)}, u32[]{:S(2)}, u32[]{:S(2)}) async-start(f32[32,1,4]{2,1,0:T(1,128)} %broadcast_in_dim.13), calls=%async_computation.2 | async-start | bytes 32768 | tf_op jit(solution)/shard_map/all_to_all | solution.py:130
  69.1 3.4 %collective-permute-start.8 = (f32[2,2304]{1,0:T(2,128)S(1)}, f32[2,2304]{1,0:T(2,128)S(1)}, u32[]{:S(2)}, u32[]{:S(2)}) collective-permute-start(f32[2,2304]{1,0:T(2,128)S(1)} %get-tuple-element.22), channel_id=1, source_target_pairs={{1,0},{2,1},{3,2},{4,3},{5,4},{6,5},{7,6},{0,7},{9,8},{10,9},{11,1... | collective-permute-start | bytes 55304 | tf_op jit(solution)/shard_map/ppermute | solution.py:13
  72.5 2.4 %collective-permute-start.9 = (f32[2,2304]{1,0:T(2,128)S(1)}, f32[2,2304]{1,0:T(2,128)S(1)}, u32[]{:S(2)}, u32[]{:S(2)}) collective-permute-start(f32[2,2304]{1,0:T(2,128)S(1)} %get-tuple-element.23), channel_id=1, source_target_pairs={{8,0},{16,8},{24,16},{0,24},{9,1},{17,9},{25,17},{1,25},{10,2},{18... | collective-permute-start | bytes 55304 | tf_op jit(solution)/shard_map/ppermute | solution.py:13
  75.0 1.2 %all-to-all-done.2 = f32[32,1,4]{2,1,0:T(1,128)S(1)} async-done(((f32[32,1,4]{2,1,0:T(1,128)}), f32[32,1,4]{2,1,0:T(1,128)S(1)}, u32[]{:S(2)}, u32[]{:S(2)}) %all-to-all-start.2) | async-done | bytes 544 | tf_op jit(solution)/shard_map/all_to_all | solution.py:130
  81.2 0.8 multiply_add_fusion
  (191 shorter events, 18.8 us)
Async XLA Ops:
  1.5 4.3 %copy-start = (f32[1,1,2,48,48]{4,3,2,1,0:T(8,128)S(1)}, f32[1,1,2,48,48]{4,3,2,1,0:T(8,128)}, u32[]{:S(2)}) copy-start(f32[1,1,2,48,48]{4,3,2,1,0:T(8,128)} %param.7) | copy-start | bytes 55300
  5.8 2.3 %copy-start.2 = (f32[1,1,2,48]{3,2,1,0:T(2,128)S(1)}, f32[1,1,2,48]{3,2,1,0:T(2,128)}, u32[]{:S(2)}) copy-start(f32[1,1,2,48]{3,2,1,0:T(2,128)} %param.8) | copy-start | bytes 1156
  10.7 12.2 %copy-start.1 = (s32[4,8]{1,0:T(4,128)S(1)}, s32[4,8]{1,0:T(4,128)}, u32[]{:S(2)}) copy-start(s32[4,8]{1,0:T(4,128)} %param.10) | copy-start | bytes 388
  10.7 12.3 %copy-start.4 = (f32[1,1,6,48]{3,1,2,0:T(1,128)S(1)}, f32[1,1,6,48]{3,1,2,0:T(1,128)}, u32[]{:S(2)}) copy-start(f32[1,1,6,48]{3,1,2,0:T(1,128)} %param.11) | copy-start | bytes 3460
  10.7 12.4 %copy-start.3 = (f32[1,1,2,3]{3,2,1,0:T(2,128)S(1)}, f32[1,1,2,3]{3,2,1,0:T(2,128)}, u32[]{:S(2)}) copy-start(f32[1,1,2,3]{3,2,1,0:T(2,128)} %param.9) | copy-start | bytes 76
  14.3 14.4 %all-to-all-start = ((f32[32,1,12]{2,1,0:T(1,128)}), f32[32,1,12]{2,1,0:T(1,128)S(1)}, u32[]{:S(2)}, u32[]{:S(2)}) async-start(f32[32,1,12]{2,1,0:T(1,128)} %broadcast_in_dim.11), calls=%async_computation | async-start | bytes 32768 | tf_op jit(solution)/shard_map/all_to_all | solution.py:130
  28.8 3.3 %collective-permute-start.2 = (f32[2,2304]{1,0:T(2,128)S(1)}, f32[2,2304]{1,0:T(2,128)S(1)}, u32[]{:S(2)}, u32[]{:S(2)}) collective-permute-start(f32[2,2304]{1,0:T(2,128)S(1)} %get-tuple-element.16), channel_id=1, source_target_pairs={{1,0},{2,1},{3,2},{4,3},{5,4},{6,5},{7,6},{0,7},{9,8},{10,9},{11,1... | collective-permute-start | bytes 55304 | tf_op jit(solution)/shard_map/ppermute | solution.py:13
  28.8 3.8 %collective-permute-start.3 = (f32[2,2304]{1,0:T(2,128)S(1)}, f32[2,2304]{1,0:T(2,128)S(1)}, u32[]{:S(2)}, u32[]{:S(2)}) collective-permute-start(f32[2,2304]{1,0:T(2,128)S(1)} %get-tuple-element.17), channel_id=1, source_target_pairs={{8,0},{16,8},{24,16},{0,24},{9,1},{17,9},{25,17},{1,25},{10,2},{18... | collective-permute-start | bytes 55304 | tf_op jit(solution)/shard_map/ppermute | solution.py:13
  30.6 5.0 %collective-permute-start = (f32[2,2353]{1,0:T(2,128)S(1)}, f32[2,2353]{1,0:T(2,128)S(1)}, u32[]{:S(2)}, u32[]{:S(2)}) collective-permute-start(f32[2,2353]{1,0:T(2,128)S(1)} %concatenate.231), channel_id=1, source_target_pairs={{7,0},{0,1},{1,2},{2,3},{3,4},{4,5},{5,6},{6,7},{15,8},{8,9},{9,10... | collective-permute-start | bytes 56480 | tf_op jit(solution)/shard_map/ppermute | solution.py:13
  30.6 5.1 %collective-permute-start.1 = (f32[2,2353]{1,0:T(2,128)S(1)}, f32[2,2353]{1,0:T(2,128)S(1)}, u32[]{:S(2)}, u32[]{:S(2)}) collective-permute-start(f32[2,2353]{1,0:T(2,128)S(1)} %concatenate.232), channel_id=1, source_target_pairs={{24,0},{0,8},{8,16},{16,24},{25,1},{1,9},{9,17},{17,25},{26,2},{2,... | collective-permute-start | bytes 56480 | tf_op jit(solution)/shard_map/ppermute | solution.py:13
  44.8 9.7 %all-to-all-start.1 = ((f32[32,1,14]{2,1,0:T(1,128)}), f32[32,1,14]{2,1,0:T(1,128)S(1)}, u32[]{:S(2)}, u32[]{:S(2)}) async-start(f32[32,1,14]{2,1,0:T(1,128)} %broadcast_in_dim.12), calls=%async_computation.1 | async-start | bytes 32768 | tf_op jit(solution)/shard_map/all_to_all | solution.py:130
  47.3 10.6 %collective-permute-start.6 = (f32[2,2304]{1,0:T(2,128)S(1)}, f32[2,2304]{1,0:T(2,128)S(1)}, u32[]{:S(2)}, u32[]{:S(2)}) collective-permute-start(f32[2,2304]{1,0:T(2,128)S(1)} %get-tuple-element.20), channel_id=1, source_target_pairs={{7,0},{0,1},{1,2},{2,3},{3,4},{4,5},{5,6},{6,7},{15,8},{8,9},{9,10... | collective-permute-start | bytes 55304 | tf_op jit(solution)/shard_map/ppermute | solution.py:13
  47.5 10.4 %collective-permute-start.7 = (f32[2,2304]{1,0:T(2,128)S(1)}, f32[2,2304]{1,0:T(2,128)S(1)}, u32[]{:S(2)}, u32[]{:S(2)}) collective-permute-start(f32[2,2304]{1,0:T(2,128)S(1)} %get-tuple-element.21), channel_id=1, source_target_pairs={{24,0},{0,8},{8,16},{16,24},{25,1},{1,9},{9,17},{17,25},{26,2},{2,... | collective-permute-start | bytes 55304 | tf_op jit(solution)/shard_map/ppermute | solution.py:13
  49.2 8.6 %collective-permute-start.4 = (f32[2,2304]{1,0:T(2,128)S(1)}, f32[2,2304]{1,0:T(2,128)S(1)}, u32[]{:S(2)}, u32[]{:S(2)}) collective-permute-start(f32[2,2304]{1,0:T(2,128)S(1)} %get-tuple-element.18), channel_id=1, source_target_pairs={{1,0},{2,1},{3,2},{4,3},{5,4},{6,5},{7,6},{0,7},{9,8},{10,9},{11,1... | collective-permute-start | bytes 55304 | tf_op jit(solution)/shard_map/ppermute | solution.py:13
  52.3 5.5 %collective-permute-start.5 = (f32[2,2304]{1,0:T(2,128)S(1)}, f32[2,2304]{1,0:T(2,128)S(1)}, u32[]{:S(2)}, u32[]{:S(2)}) collective-permute-start(f32[2,2304]{1,0:T(2,128)S(1)} %get-tuple-element.19), channel_id=1, source_target_pairs={{8,0},{16,8},{24,16},{0,24},{9,1},{17,9},{25,17},{1,25},{10,2},{18... | collective-permute-start | bytes 55304 | tf_op jit(solution)/shard_map/ppermute | solution.py:13
  66.5 9.6 %all-to-all-start.2 = ((f32[32,1,4]{2,1,0:T(1,128)}), f32[32,1,4]{2,1,0:T(1,128)S(1)}, u32[]{:S(2)}, u32[]{:S(2)}) async-start(f32[32,1,4]{2,1,0:T(1,128)} %broadcast_in_dim.13), calls=%async_computation.2 | async-start | bytes 32768 | tf_op jit(solution)/shard_map/all_to_all | solution.py:130
  69.1 12.9 %collective-permute-start.8 = (f32[2,2304]{1,0:T(2,128)S(1)}, f32[2,2304]{1,0:T(2,128)S(1)}, u32[]{:S(2)}, u32[]{:S(2)}) collective-permute-start(f32[2,2304]{1,0:T(2,128)S(1)} %get-tuple-element.22), channel_id=1, source_target_pairs={{1,0},{2,1},{3,2},{4,3},{5,4},{6,5},{7,6},{0,7},{9,8},{10,9},{11,1... | collective-permute-start | bytes 55304 | tf_op jit(solution)/shard_map/ppermute | solution.py:13
  72.5 9.5 %collective-permute-start.9 = (f32[2,2304]{1,0:T(2,128)S(1)}, f32[2,2304]{1,0:T(2,128)S(1)}, u32[]{:S(2)}, u32[]{:S(2)}) collective-permute-start(f32[2,2304]{1,0:T(2,128)S(1)} %get-tuple-element.23), channel_id=1, source_target_pairs={{8,0},{16,8},{24,16},{0,24},{9,1},{17,9},{25,17},{1,25},{10,2},{18... | collective-permute-start | bytes 55304 | tf_op jit(solution)/shard_map/ppermute | solution.py:13
